TPU v7x, 512 devices: a whole 4x4x16 slice. The times are simulated.
512 devices in a mesh: section: 32 (over z_hi, y, core), tp: 16 (over z_lo, x).
Axes of the slice: x: 4, y: 4, z: 16 (z_hi: 4, z_lo: 4; z = z_hi * 4 + z_lo), core: 2. Of those that a mesh axis runs over, the one named last changes fastest.
Arguments:
- grad_in: bfloat16 [32, 160, 8192], P('section', None, 'tp'), may hold values from -6 to 6
- out_proj: bfloat16 [32, 4096, 8192], P('section', 'tp'), may hold values from -0.09375 to 0.09375
- value_proj: bfloat16 [32, 8192, 512], P('section', 'tp'), may hold values from -0.0625 to 0.0625
- head_delta: bfloat16 [32, 160, 4096], P('section', None, 'tp'), may hold values from -6 to 6
- pattern: bfloat16 [32, 32, 160, 160], P('section', 'tp'), may hold values from 0 to 0.25
- positions: int32 [160], replicated, may hold values from -1 to 31, as said below
- node_map: int32 [32, 32], P('section'), may hold values from 0 to 31, each once within a row
Outputs:
- residual_grad: bfloat16 [32, 160, 8192], P('section', None, 'tp')
- edge_scores: float32 [32, 32, 32], P('section')
Inputs may be any that keep to these rules, and one draw needn't show every extreme that they name: positions[t] = (t mod 32) - p, or -1 where that is negative, with one left padding p of 0 to 15 for each block of 32 tokens; the first block is unpadded. `node_map`: each row names every node once.
All inputs are finite; a program needn't handle non-finite values.
Results may differ from a plain program's by a relative error of at most 0.0095.
Values may be sent and summed in bfloat16 or wider, within the bound.
No kernel may reach another device: no remote copies, remote signals or barrier semaphores. Data moves between devices by JAX's collectives and lax.ppermute only.
A program may use at most 128 MiB of HBM per device.

v0:
```python
import jax
import jax.numpy as jnp
from jax import lax
from jax.sharding import PartitionSpec as P

HEADS = 32
HEAD_DIM = 128
KV = 4
PROMPT = 32
GROUP = 8


def laid_out(tiles, dim):
    dims = list(tiles.shape[1:])
    dims[dim] *= tiles.shape[0]
    return jnp.moveaxis(tiles, 0, dim).reshape(dims)


def from_everyone(array, axis):
    count = lax.axis_size(axis)
    return lax.all_to_all(
        jnp.broadcast_to(array[None], (count, *array.shape)), axis, 0, 0, tiled=True
    )


def gathered_copies(array, axis, dim):
    return laid_out(from_everyone(array, axis), dim)


def in_blocks(array, dim, count):
    dims = array.shape
    tiles = array.reshape(*dims[:dim], count, dims[dim] // count, *dims[dim + 1 :])
    return jnp.moveaxis(tiles, dim, 0)


def cut_rows(length, count):
    unit = 8 if length >= 8 * count else 1
    return [length // unit * k // count * unit for k in range(1, count)]


def several_exchanges(array, axis, pieces, split_dim, concat_dim):
    tiles = in_blocks(array, split_dim, lax.axis_size(axis))
    split_at = max(range(1, max(2, tiles.ndim - 1)), key=lambda d: tiles.shape[d])
    finished = []
    for slab in jnp.split(tiles, cut_rows(tiles.shape[split_at], pieces), axis=split_at):
        if slab.size:
            finished.append(lax.all_to_all(slab, axis, split_axis=0, concat_axis=0, tiled=True))
    return laid_out(jnp.concatenate(finished, axis=split_at), concat_dim)


def over_copies(array, axis):
    everything = from_everyone(array, axis)
    return jnp.sum(everything, axis=0)


def on_device(grad_in, out_proj, value_proj, head_delta, pattern, positions, node_map):
    tokens = grad_in.shape[1]
    local_width = grad_in.shape[2]
    own_rows = out_proj.shape[1]
    own_heads = own_rows // HEAD_DIM
    section_count = lax.axis_size("section")
    weights = out_proj[0]
    token_ids = jnp.arange(tokens)
    block_ids = token_ids // PROMPT
    allowed = (
        (block_ids[:, None] == block_ids[None, :])
        & (positions[None, :] >= 0)
        & (positions[None, :] <= positions[:, None])
    )
    visible = allowed.astype(jnp.bfloat16)
    head_grad = lax.dot_general(
        gathered_copies(grad_in, "tp", 2)[0],
        weights,
        (((1,), (1,)), ((), ())),
        preferred_element_type=jnp.float32,
    ).astype(jnp.bfloat16)
    masked = pattern[0] * visible[None]
    value_grad = jnp.einsum(
        "hts,thc->shc",
        masked,
        head_grad.reshape(tokens, own_heads, HEAD_DIM),
        preferred_element_type=jnp.float32,
    ).astype(jnp.bfloat16)
    every_head = gathered_copies(value_grad.reshape(tokens, own_rows), "tp", 1)
    summed = every_head.astype(jnp.float32).reshape(tokens, KV, GROUP, HEAD_DIM).sum(axis=2)
    group_grad = summed.reshape(tokens, KV * HEAD_DIM).astype(jnp.bfloat16)
    increment = lax.dot_general(
        group_grad, value_proj[0], (((1,), (1,)), ((), ())), preferred_element_type=jnp.float32
    )
    residual_grad = (grad_in[0].astype(jnp.float32) + increment).astype(jnp.bfloat16)
    target_row = increment.astype(jnp.bfloat16)
    target_rows = lax.all_gather(target_row[None], "section", axis=0, tiled=True)
    own_delta = jnp.einsum(
        "thc,hcd->htd",
        head_delta[0].reshape(tokens, own_heads, HEAD_DIM),
        weights.reshape(own_heads, HEAD_DIM, weights.shape[1]),
        preferred_element_type=jnp.float32,
    ).astype(jnp.bfloat16)
    delta = several_exchanges(own_delta, "tp", 2, 2, 0)
    partial_scores = lax.dot_general(
        delta.reshape(HEADS, tokens * local_width),
        target_rows.reshape(section_count, tokens * local_width),
        (((1,), (1,)), ((), ())),
        preferred_element_type=jnp.float32,
    )
    totals = over_copies(partial_scores, "tp")
    later = jnp.arange(section_count) > lax.axis_index("section")
    raw_scores = jnp.where(later[None, :], totals / tokens, jnp.zeros_like(totals))
    onehot = (node_map[0][:, None] == jnp.arange(HEADS)[None, :]).astype(jnp.float32)
    edge_scores = jnp.dot(onehot.T, raw_scores, precision=lax.Precision.HIGHEST)
    return (residual_grad[None], edge_scores[None])


def solution(mesh):
    placed = (
        P("section", None, "tp"),
        P("section", "tp", None),
        P("section", "tp", None),
        P("section", None, "tp"),
        P("section", "tp", None, None),
        P(),
        P("section", None),
    )
    return jax.shard_map(
        on_device,
        mesh=mesh,
        in_specs=placed,
        out_specs=(P("section", None, "tp"), P("section", None, None)),
        check_vma=False,
    )
```

profile of v0, /device:TPU:1, one launch (start us, length us, event | category | flops | bytes accessed | tf_op | source)
XLA Modules:
  0.0 340.4 jit_solution(7306948362007261664)
XLA Ops:
  7.2 0.0 copy-start
  7.2 0.0 copy-start.5
  7.2 2.7 broadcast_in_dim.21
  9.9 9.0 %all-to-all-start = ((bf16[16,1,160,512]{3,2,1,0:T(8,128)(2,1)}), bf16[16,1,160,512]{3,2,1,0:T(8,128)(2,1)S(1)}, u32[]{:S(2)}, u32[]{:S(2)}) async-start(bf16[16,1,160,512]{3,2,1,0:T(8,128)(2,1)} %broadcast_in_dim.21), calls=%async_computation | async-start | bytes 5242880 | tf_op jit(solution)/shard_map/all_to_all | solution.py:21
  19.0 0.0 copy-done.5
  19.0 0.1 and_convert_fusion
  19.1 50.4 %all-to-all-done = bf16[16,1,160,512]{3,2,1,0:T(8,128)(2,1)S(1)} async-done(((bf16[16,1,160,512]{3,2,1,0:T(8,128)(2,1)}), bf16[16,1,160,512]{3,2,1,0:T(8,128)(2,1)S(1)}, u32[]{:S(2)}, u32[]{:S(2)}) %all-to-all-start) | async-done | bytes 2621472 | tf_op jit(solution)/shard_map/all_to_all | solution.py:21
  69.5 0.0 copy-start.1
  69.5 0.3 copy.35
  69.9 1.9 copy-done.1
  71.7 0.0 copy-start.3
  71.7 1.5 fusion.6
  73.3 0.0 copy-done.3
  73.3 0.0 copy-start.4
  73.3 0.2 fusion.5
  73.6 1.2 broadcast_in_dim.26
  74.8 13.3 %all-to-all-start.1 = ((bf16[16,160,256]{2,1,0:T(8,128)(2,1)}), bf16[16,160,256]{2,1,0:T(8,128)(2,1)}, u32[]{:S(2)}, u32[]{:S(2)}) async-start(bf16[16,160,256]{2,1,0:T(8,128)(2,1)} %broadcast_in_dim.26), calls=%async_computation.1 | async-start | bytes 2621440 | tf_op jit(solution)/shard_map/all_to_all | solution.py:21
  88.1 0.0 copy-done.4
  88.1 3.7 %convolution_convert_fusion = bf16[2,160,8192]{2,1,0:T(8,128)(2,1)S(1)} fusion(bf16[2,128,8192]{2,1,0:T(8,128)(2,1)} %bitcast.66, bf16[160,2,128]{2,1,0:T(2,128)(2,1)S(1)} %reshape_squeeze.6), kind=kOutput, calls=%fused_computation | convolution fusion | flops 673710080 | bytes 9519104 | tf_op jit(solution)/shard_map/thc,hcd->htd/dot_general | solution.py:93
  91.8 0.7 copy.53
  92.5 1.8 fusion.26
  94.4 20.2 %all-to-all-done.1 = bf16[16,160,256]{2,1,0:T(8,128)(2,1)} async-done(((bf16[16,160,256]{2,1,0:T(8,128)(2,1)}), bf16[16,160,256]{2,1,0:T(8,128)(2,1)}, u32[]{:S(2)}, u32[]{:S(2)}) %all-to-all-start.1) | async-done | bytes 1310752 | tf_op jit(solution)/shard_map/all_to_all | solution.py:21
  114.6 9.0 %all-to-all-start.3 = ((bf16[16,2,80,512]{3,2,1,0:T(8,128)(2,1)}), bf16[16,2,80,512]{3,2,1,0:T(8,128)(2,1)}, u32[]{:S(2)}, u32[]{:S(2)}) async-start(bf16[16,2,80,512]{3,2,1,0:T(8,128)(2,1)} %get-tuple-element.3), calls=%async_computation.3 | async-start | bytes 5242880 | tf_op jit(solution)/shard_map/all_to_all | solution.py:47
  123.6 0.0 copy-start.2
  123.7 0.0 all-gather.3.cloned.1.call-start
  123.7 3.1 copy.28
  126.8 3.2 reshape.130
  130.0 2.3 reduce_sum.21
  132.3 0.0 copy-done
  132.3 0.0 copy-done.2
  132.3 1.0 fusion.27
  133.4 0.0 all-gather.3.cloned.1.call-update
  133.4 50.6 %all-to-all-done.3 = bf16[16,2,80,512]{3,2,1,0:T(8,128)(2,1)} async-done(((bf16[16,2,80,512]{3,2,1,0:T(8,128)(2,1)}), bf16[16,2,80,512]{3,2,1,0:T(8,128)(2,1)}, u32[]{:S(2)}, u32[]{:S(2)}) %all-to-all-start.3) | async-done | bytes 2621472 | tf_op jit(solution)/shard_map/all_to_all | solution.py:47
  184.0 114.6 %all_to_all.25 = bf16[16,2,80,512]{3,2,1,0:T(8,128)(2,1)S(1)} all-to-all(bf16[16,2,80,512]{3,2,1,0:T(8,128)(2,1)S(1)} %get-tuple-element.2), channel_id=1, replica_groups=mesh['section'=32,'tp'=16] {'tp'}, dimensions={0} | all-to-all | bytes 5242880 | tf_op jit(solution)/shard_map/all_to_all | solution.py:47
  298.5 2.2 pad_maximum_fusion
  300.8 5.4 %copy.37 = bf16[4,8,160,512]{3,1,2,0:T(8,128)(2,1)} copy(bf16[4,8,160,512]{3,2,1,0:T(8,128)(2,1)S(1)} %bitcast.63) | data formatting | bytes 10485760
  306.1 0.0 all-gather.3.cloned.1.call-done
  306.1 6.4 %reshape.132 = bf16[32,81920]{1,0:T(8,128)(2,1)} reshape(bf16[5120,512]{1,0:T(8,128)(2,1)} %all-gather.3.cloned.1.call-done) | data formatting | bytes 10485760 | tf_op jit(solution)/shard_map/reshape | solution.py:102
  312.6 0.0 copy-start.6
  312.6 5.5 %fusion.32 = f32[32,32]{1,0:T(8,128)S(1)} fusion(bf16[32,81920]{1,0:T(8,128)(2,1)} %bitcast.61, bf16[32,81920]{1,0:T(8,128)(2,1)} %reshape.132), kind=kOutput, calls=%fused_computation.40 | convolution fusion | flops 167772160 | bytes 10489856 | tf_op jit(solution)/shard_map/dot_general | solution.py:100
  318.2 0.8 reshape.135
  319.0 5.0 %all-to-all-start.4 = ((f32[16,1,1024]{2,1,0:T(1,128)}), f32[16,1,1024]{2,1,0:T(1,128)S(1)}, u32[]{:S(2)}, u32[]{:S(2)}) async-start(f32[16,1,1024]{2,1,0:T(1,128)} %reshape.135), calls=%async_computation.4 | async-start | bytes 131072 | tf_op jit(solution)/shard_map/all_to_all | solution.py:21
  324.0 7.2 %all-to-all-done.4 = f32[16,1,1024]{2,1,0:T(1,128)S(1)} async-done(((f32[16,1,1024]{2,1,0:T(1,128)}), f32[16,1,1024]{2,1,0:T(1,128)S(1)}, u32[]{:S(2)}, u32[]{:S(2)}) %all-to-all-start.4) | async-done | bytes 65568 | tf_op jit(solution)/shard_map/all_to_all | solution.py:21
  331.2 0.5 broadcast.110
  331.7 0.8 reduce.1
  332.5 0.1 reshape.136
  332.7 0.0 copy-done.6
  332.7 0.9 convolution_bitcast_fusion
  (7 shorter events, 0.1 us)
Async XLA Ops:
  7.2 125.1 %copy-start = (bf16[1,512,512]{2,1,0:T(8,128)(2,1)S(1)}, bf16[1,512,512]{2,1,0:T(8,128)(2,1)}, u32[]{:S(2)}) copy-start(bf16[1,512,512]{2,1,0:T(8,128)(2,1)} %param.9) | copy-start | bytes 1572868
  7.2 11.8 %copy-start.5 = (s32[160]{0:T(256)S(1)}, s32[160]{0:T(256)}, u32[]{:S(2)}) copy-start(s32[160]{0:T(256)} %param.12) | copy-start | bytes 1924
  9.9 59.6 %all-to-all-start = ((bf16[16,1,160,512]{3,2,1,0:T(8,128)(2,1)}), bf16[16,1,160,512]{3,2,1,0:T(8,128)(2,1)S(1)}, u32[]{:S(2)}, u32[]{:S(2)}) async-start(bf16[16,1,160,512]{3,2,1,0:T(8,128)(2,1)} %broadcast_in_dim.21), calls=%async_computation | async-start | bytes 5242880 | tf_op jit(solution)/shard_map/all_to_all | solution.py:21
  69.5 2.2 copy-start.1
  71.7 1.6 copy-start.3
  73.3 14.8 %copy-start.4 = (bf16[1,160,256]{2,1,0:T(8,128)(2,1)S(1)}, bf16[1,160,256]{2,1,0:T(8,128)(2,1)}, u32[]{:S(2)}) copy-start(bf16[1,160,256]{2,1,0:T(8,128)(2,1)} %param.10) | copy-start | bytes 245764
  74.8 39.8 %all-to-all-start.1 = ((bf16[16,160,256]{2,1,0:T(8,128)(2,1)}), bf16[16,160,256]{2,1,0:T(8,128)(2,1)}, u32[]{:S(2)}, u32[]{:S(2)}) async-start(bf16[16,160,256]{2,1,0:T(8,128)(2,1)} %broadcast_in_dim.26), calls=%async_computation.1 | async-start | bytes 2621440 | tf_op jit(solution)/shard_map/all_to_all | solution.py:21
  114.6 69.4 %all-to-all-start.3 = ((bf16[16,2,80,512]{3,2,1,0:T(8,128)(2,1)}), bf16[16,2,80,512]{3,2,1,0:T(8,128)(2,1)}, u32[]{:S(2)}, u32[]{:S(2)}) async-start(bf16[16,2,80,512]{3,2,1,0:T(8,128)(2,1)} %get-tuple-element.3), calls=%async_computation.3 | async-start | bytes 5242880 | tf_op jit(solution)/shard_map/all_to_all | solution.py:47
  123.6 8.7 %copy-start.2 = (bf16[1,160,512]{2,1,0:T(8,128)(2,1)S(1)}, bf16[1,160,512]{2,1,0:T(8,128)(2,1)}, u32[]{:S(2)}) copy-start(bf16[1,160,512]{2,1,0:T(8,128)(2,1)} %param.7) | copy-start | bytes 491524
  123.7 182.5 %all-gather.3.cloned.1.call-start = ((), (), s32[]{:S(2)}) async-start(), calls=%async_computation.5 | async-start | bytes 5406720 | tf_op jit(solution)/shard_map/all_gather | solution.py:92
  312.6 20.1 %copy-start.6 = (s32[1,32]{1,0:T(1,128)S(1)}, s32[1,32]{1,0:T(1,128)}, u32[]{:S(2)}) copy-start(s32[1,32]{1,0:T(1,128)} %param.13) | copy-start | bytes 388
  319.0 12.3 %all-to-all-start.4 = ((f32[16,1,1024]{2,1,0:T(1,128)}), f32[16,1,1024]{2,1,0:T(1,128)S(1)}, u32[]{:S(2)}, u32[]{:S(2)}) async-start(f32[16,1,1024]{2,1,0:T(1,128)} %reshape.135), calls=%async_computation.4 | async-start | bytes 131072 | tf_op jit(solution)/shard_map/all_to_all | solution.py:21
Sparse Core Ops, SparseCore 0:
  133.5 122.2 all-gather.2
where the time goes:
time: 343 us; the launch traced here: 340 us
  waiting for transfers between devices  128 us (37%)
  blocking collectives  115 us (34%)
  starting transfers between devices  36.4 us (11%)
  local copies, waits for them, and re-layouts  28.3 us (8%)
  between operations  14.3 us (4%)
  matrix products  13 us (4%)
  other arithmetic  5.45 us (2%)
    all_to_all x1, blocking collectives, several_exchanges(): lax.all_to_all(slab, axis, split_axis=0, concat_axis=0, tiled=True)  115 us
    all_to_all x3, waiting for transfers between devices, from_everyone(): lax.all_to_all(jnp.broadcast_to(array[None], (count, *array.shape)), axis...  77.9 us
    all_to_all x1, waiting for transfers between devices, several_exchanges(): lax.all_to_all(slab, axis, split_axis=0, concat_axis=0, tiled=True)  50.6 us
    all_to_all x3, starting transfers between devices, from_everyone(): lax.all_to_all(jnp.broadcast_to(array[None], (count, *array.shape)), axis...  27.3 us
    all_to_all x1, starting transfers between devices, several_exchanges(): lax.all_to_all(slab, axis, split_axis=0, concat_axis=0, tiled=True)  9.05 us
    unnamed x18, local copies, waits for them, and re-layouts  8.5 us
  transfers between devices with their start and end apart: 5, of which 4 were waited for; matrix products, arithmetic and copies ran while one was open for 7% of the time, Pallas kernels for 0%

commit v1 on v0

v1 whole, which is shorter than its diff:
```python
import jax
import jax.numpy as jnp
from jax import lax
from jax.sharding import PartitionSpec as P

HEADS = 32
HEAD_DIM = 128
KV = 4
PROMPT = 32
GROUP = 8


def on_device(grad_in, out_proj, value_proj, head_delta, pattern, positions, node_map):
    tokens = grad_in.shape[1]
    local_width = grad_in.shape[2]
    own_rows = out_proj.shape[1]
    own_heads = own_rows // HEAD_DIM
    width = out_proj.shape[2]
    tp_count = lax.axis_size("tp")
    section_count = lax.axis_size("section")
    weights = out_proj[0]

    blocks = weights.reshape(own_rows, tp_count, width // tp_count).transpose(1, 0, 2)
    column_blocks = lax.all_to_all(blocks, "tp", 0, 0, tiled=True)
    all_delta_cols = lax.all_gather(head_delta[0], "tp", axis=1, tiled=True)

    token_ids = jnp.arange(tokens)
    block_ids = token_ids // PROMPT
    allowed = (
        (block_ids[:, None] == block_ids[None, :])
        & (positions[None, :] >= 0)
        & (positions[None, :] <= positions[:, None])
    )
    visible = allowed.astype(jnp.bfloat16)
    grad_rows = lax.all_gather(grad_in[0], "tp", axis=1, tiled=True)
    head_grad = lax.dot_general(
        grad_rows,
        weights,
        (((1,), (1,)), ((), ())),
        preferred_element_type=jnp.float32,
    ).astype(jnp.bfloat16)
    masked = pattern[0] * visible[None]
    value_grad = jnp.einsum(
        "hts,thc->shc",
        masked,
        head_grad.reshape(tokens, own_heads, HEAD_DIM),
        preferred_element_type=jnp.float32,
    ).astype(jnp.bfloat16)
    pair_sum = value_grad.astype(jnp.float32).sum(axis=1)
    group_of = (lax.axis_index("tp") * own_heads) // GROUP
    slots = jnp.zeros((tokens, KV, HEAD_DIM), jnp.float32)
    slots = lax.dynamic_update_slice(slots, pair_sum[:, None, :], (0, group_of, 0))
    summed = lax.psum(slots, "tp")
    group_grad = summed.reshape(tokens, KV * HEAD_DIM).astype(jnp.bfloat16)
    increment = lax.dot_general(
        group_grad, value_proj[0], (((1,), (1,)), ((), ())), preferred_element_type=jnp.float32
    )
    residual_grad = (grad_in[0].astype(jnp.float32) + increment).astype(jnp.bfloat16)
    target_row = increment.astype(jnp.bfloat16)
    target_rows = lax.all_gather(target_row[None], "section", axis=0, tiled=True)

    delta = jnp.einsum(
        "thc,hcd->htd",
        all_delta_cols.reshape(tokens, HEADS, HEAD_DIM),
        column_blocks.reshape(HEADS, HEAD_DIM, local_width),
        preferred_element_type=jnp.float32,
    ).astype(jnp.bfloat16)
    partial_scores = lax.dot_general(
        delta.reshape(HEADS, tokens * local_width),
        target_rows.reshape(section_count, tokens * local_width),
        (((1,), (1,)), ((), ())),
        preferred_element_type=jnp.float32,
    )
    totals = lax.psum(partial_scores, "tp")
    later = jnp.arange(section_count) > lax.axis_index("section")
    raw_scores = jnp.where(later[None, :], totals / tokens, jnp.zeros_like(totals))
    onehot = (node_map[0][:, None] == jnp.arange(HEADS)[None, :]).astype(jnp.float32)
    edge_scores = jnp.dot(onehot.T, raw_scores, precision=lax.Precision.HIGHEST)
    return (residual_grad[None], edge_scores[None])


def solution(mesh):
    placed = (
        P("section", None, "tp"),
        P("section", "tp", None),
        P("section", "tp", None),
        P("section", None, "tp"),
        P("section", "tp", None, None),
        P(),
        P("section", None),
    )
    return jax.shard_map(
        on_device,
        mesh=mesh,
        in_specs=placed,
        out_specs=(P("section", None, "tp"), P("section", None, None)),
        check_vma=False,
    )
```

time: 343 us -> 442 us (1.29)
  the two profiles are of different devices: /device:TPU:1 before, /device:TPU:8 now
where the time goes in v1:
time: 442 us; the launch traced here: 441 us
  waiting for transfers between devices  219 us (50%)
  blocking collectives  154 us (35%)
  matrix products  27.7 us (6%)
  local copies, waits for them, and re-layouts  17.2 us (4%)
  between operations  13.9 us (3%)
  starting transfers between devices  8.77 us (2%)
    all_gather x1, waiting for transfers between devices, on_device(): grad_rows = lax.all_gather(grad_in[0], 'tp', axis=1, tiled=True)  125 us
    all_gather x1, waiting for transfers between devices, on_device(): lax.all_gather(target_row[None], 'section', axis=0, tiled=True)  92.8 us
    psum x1, blocking collectives, on_device(): summed = lax.psum(slots, 'tp')  78.9 us
    psum x1, blocking collectives, on_device(): totals = lax.psum(partial_scores, 'tp')  75.6 us
    dot_general x1, matrix products, on_device(): lax.dot_general(delta.reshape(HEADS, tokens * local_width), target_rows.r...  15 us
  transfers between devices with their start and end apart: 4, of which 2 were waited for; matrix products, arithmetic and copies ran while one was open for 7% of the time, Pallas kernels for 0%

profile of v1, /device:TPU:8, one launch (start us, length us, event | category | flops | bytes accessed | tf_op | source)
XLA Modules:
  0.0 441.4 jit_solution(2010720892174601740)
XLA Ops:
  7.2 0.0 copy-start
  7.2 0.0 all-gather.7.cloned.1.call-start
  7.2 0.7 all-gather.7.cloned.1.call-update
  7.9 6.4 %copy.21 = bf16[1,256,8192]{1,2,0:T(8,128)(2,1)} copy(bf16[1,256,8192]{2,1,0:T(8,128)(2,1)} %param.8) | data formatting | bytes 8388608 | tf_op args[1]
  14.3 0.0 copy-start.3
  14.3 8.6 %all-to-all-start = ((bf16[16,256,512]{1,2,0:T(8,128)(2,1)}), bf16[16,256,512]{1,2,0:T(8,128)(2,1)}, u32[]{:S(2)}, u32[]{:S(2)}) async-start(bf16[16,256,512]{1,2,0:T(8,128)(2,1)} %bitcast.55), calls=%async_computation | async-start | bytes 8388608 | tf_op jit(solution)/shard_map/all_to_all | solution.py:24
  23.0 0.0 all-gather.9.cloned.1.call-start
  23.0 0.7 all-gather.9.cloned.1.call-update
  23.7 0.0 all-gather.11.cloned.1.call-start
  23.8 0.0 copy-done.3
  23.8 0.1 and_convert_fusion
  24.0 0.0 copy-start.2
  24.0 0.0 copy-start.1
  24.0 125.0 %all-gather.7.cloned.1.call-done = bf16[1,160,8192]{2,1,0:T(8,128)(2,1)} async-done(((bf16[1,160,512]{2,1,0:T(8,128)(2,1)}), bf16[1,160,8192]{2,1,0:T(8,128)(2,1)}) %all-gather.7.cloned.1.call-update) | async-done | bytes 2621456 | tf_op jit(solution)/shard_map/all_gather | solution.py:35
  149.0 4.5 %fusion.14 = bf16[20,2,8,128]{3,2,1,0:T(8,128)(2,1)S(1)} fusion(bf16[1,256,8192]{2,1,0:T(8,128)(2,1)} %param.8, bf16[1,160,8192]{2,1,0:T(8,128)(2,1)} %all-gather.7.cloned.1.call-done), kind=kOutput, calls=%fused_computation.12 | convolution fusion | flops 671129600 | bytes 6897664 | tf_op jit(solution)/shard_map/dot_general | solution.py:36
  153.5 0.0 copy-done.2
  153.5 0.2 fusion.13
  153.8 2.7 dynamic_update_slice.3
  156.6 78.9 %all-reduce.1 = bf16[160,4,128]{2,1,0:T(4,128)(2,1)S(1)} all-reduce(f32[160,4,128]{2,1,0:T(4,128)S(1)} %dynamic_update_slice.3), channel_id=1, replica_groups=mesh['section'=32,'tp'=16] {'tp'}, use_global_device_ids=true, to_apply=%region_1.2 | all-reduce | flops 81920 | bytes 491520 | tf_op jit(solution)/shard_map/psum | solution.py:53
  235.5 0.0 copy-done
  235.5 0.0 copy-done.1
  235.5 1.0 fusion.41
  236.6 0.0 all-gather.11.cloned.1.call-update
  236.6 0.0 all-gather.9.cloned.1.call-done
  236.6 1.6 copy.29
  238.2 0.0 all-to-all-done
  238.2 6.4 %copy.22 = bf16[16,256,512]{2,1,0:T(8,128)(2,1)} copy(bf16[16,256,512]{1,2,0:T(8,128)(2,1)} %all-to-all-done) | data formatting | bytes 8388608 | tf_op jit(solution)/shard_map/all_to_all | solution.py:24
  244.6 6.0 %convolution_convert_fusion = bf16[32,160,512]{2,1,0:T(8,128)(2,1)} fusion(bf16[32,128,512]{2,1,0:T(8,128)(2,1)} %bitcast.56, bf16[160,32,128]{2,1,0:T(8,128)(2,1)S(1)} %bitcast.57), kind=kOutput, calls=%fused_computation.5 | convolution fusion | flops 673710080 | bytes 10747904 | tf_op jit(solution)/shard_map/thc,hcd->htd/dot_general | solution.py:62
  250.7 92.8 %all-gather.11.cloned.1.call-done = bf16[5120,512]{1,0:T(8,128)(2,1)} async-done(((bf16[160,512]{1,0:T(8,128)(2,1)}), bf16[5120,512]{1,0:T(8,128)(2,1)}) %all-gather.11.cloned.1.call-update) | async-done | bytes 5242896 | tf_op jit(solution)/shard_map/all_gather | solution.py:60
  343.5 0.0 copy-start.4
  343.5 15.0 %fusion.19 = f32[32,32]{1,0:T(8,128)S(1)} fusion(bf16[32,160,512]{2,1,0:T(8,128)(2,1)} %bitcast.61, bf16[32,160,512]{2,1,0:T(8,128)(2,1)} %convolution_convert_fusion), kind=kOutput, calls=%fused_computation.13 | convolution fusion | flops 167772160 | bytes 10489856 | tf_op jit(solution)/shard_map/dot_general | solution.py:68
  358.5 75.6 %psum.15 = f32[32,32]{1,0:T(8,128)S(1)} all-reduce(f32[32,32]{1,0:T(8,128)S(1)} %fusion.19), channel_id=1, replica_groups=mesh['section'=32,'tp'=16] {'tp'}, use_global_device_ids=true, to_apply=%region_2.3 | all-reduce | flops 1024 | bytes 8192 | tf_op jit(solution)/shard_map/psum | solution.py:74
  434.0 0.0 copy-done.4
  434.0 0.9 convolution_bitcast_fusion
  (4 shorter events, 0.1 us)
Async XLA Ops:
  7.2 228.3 %copy-start = (bf16[1,512,512]{2,1,0:T(8,128)(2,1)S(1)}, bf16[1,512,512]{2,1,0:T(8,128)(2,1)}, u32[]{:S(2)}) copy-start(bf16[1,512,512]{2,1,0:T(8,128)(2,1)} %param.9) | copy-start | bytes 1572868
  7.2 141.8 %all-gather.7.cloned.1.call-start = ((), (), s32[]{:S(2)}) async-start(), calls=%async_computation.1 | async-start | bytes 2785280 | tf_op jit(solution)/shard_map/all_gather | solution.py:35
  14.3 9.5 %copy-start.3 = (s32[160]{0:T(256)S(1)}, s32[160]{0:T(256)}, u32[]{:S(2)}) copy-start(s32[160]{0:T(256)} %param.12) | copy-start | bytes 1924
  14.3 223.9 %all-to-all-start = ((bf16[16,256,512]{1,2,0:T(8,128)(2,1)}), bf16[16,256,512]{1,2,0:T(8,128)(2,1)}, u32[]{:S(2)}, u32[]{:S(2)}) async-start(bf16[16,256,512]{1,2,0:T(8,128)(2,1)} %bitcast.55), calls=%async_computation | async-start | bytes 8388608 | tf_op jit(solution)/shard_map/all_to_all | solution.py:24
  23.0 213.6 %all-gather.9.cloned.1.call-start = ((), (), s32[]{:S(2)}) async-start(), calls=%async_computation.2 | async-start | bytes 1392640 | tf_op jit(solution)/shard_map/all_gather | solution.py:25
  23.7 319.7 %all-gather.11.cloned.1.call-start = ((), (), s32[]{:S(2)}) async-start(), calls=%async_computation.3 | async-start | bytes 5406720 | tf_op jit(solution)/shard_map/all_gather | solution.py:60
  24.0 129.5 %copy-start.2 = (bf16[1,2,160,160]{3,2,1,0:T(8,128)(2,1)S(1)}, bf16[1,2,160,160]{3,2,1,0:T(8,128)(2,1)}, u32[]{:S(2)}) copy-start(bf16[1,2,160,160]{3,2,1,0:T(8,128)(2,1)} %param.11) | copy-start | bytes 307204
  24.0 211.5 %copy-start.1 = (bf16[1,160,512]{2,1,0:T(8,128)(2,1)S(1)}, bf16[1,160,512]{2,1,0:T(8,128)(2,1)}, u32[]{:S(2)}) copy-start(bf16[1,160,512]{2,1,0:T(8,128)(2,1)} %param.7) | copy-start | bytes 491524
  343.5 90.5 %copy-start.4 = (s32[1,32]{1,0:T(1,128)S(1)}, s32[1,32]{1,0:T(1,128)}, u32[]{:S(2)}) copy-start(s32[1,32]{1,0:T(1,128)} %param.13) | copy-start | bytes 388
Sparse Core Ops, SparseCore 0:
  10.1 138.8 all-gather.6
  151.0 73.8 all-gather.8
  236.7 106.7 all-gather.10

commit v2 on v1

v2 whole, which is shorter than its diff:
```python
import jax
import jax.numpy as jnp
import numpy as np
from jax import lax
from jax.sharding import Mesh
from jax.sharding import PartitionSpec as P

HEADS = 32
HEAD_DIM = 128
KV = 4
PROMPT = 32
GROUP = 8
TP = ("zl", "x")


def from_everyone(array, axis):
    count = lax.axis_size(axis)
    return lax.all_to_all(
        jnp.broadcast_to(array[None], (count, *array.shape)), axis, 0, 0, tiled=True
    )


def on_device(grad_in, out_proj, value_proj, head_delta, pattern, positions, node_map):
    tokens = grad_in.shape[1]
    local_width = grad_in.shape[2]
    own_rows = out_proj.shape[1]
    own_heads = own_rows // HEAD_DIM
    width = out_proj.shape[2]
    tp_count = lax.axis_size(TP)
    section_count = lax.axis_size("section")
    weights = out_proj[0]

    own_delta = jnp.einsum(
        "thc,hcd->htd",
        head_delta[0].reshape(tokens, own_heads, HEAD_DIM),
        weights.reshape(own_heads, HEAD_DIM, width),
        preferred_element_type=jnp.float32,
    ).astype(jnp.bfloat16)
    pieces = own_delta.reshape(own_heads, tokens, tp_count, local_width).transpose(2, 0, 1, 3)
    delta = lax.all_to_all(pieces, TP, 0, 0, tiled=True)

    token_ids = jnp.arange(tokens)
    block_ids = token_ids // PROMPT
    allowed = (
        (block_ids[:, None] == block_ids[None, :])
        & (positions[None, :] >= 0)
        & (positions[None, :] <= positions[:, None])
    )
    visible = allowed.astype(jnp.bfloat16)
    everyone = from_everyone(grad_in[0], TP)
    grad_rows = jnp.moveaxis(everyone, 0, 1).reshape(tokens, width)
    head_grad = lax.dot_general(
        grad_rows,
        weights,
        (((1,), (1,)), ((), ())),
        preferred_element_type=jnp.float32,
    ).astype(jnp.bfloat16)
    masked = pattern[0] * visible[None]
    value_grad = jnp.einsum(
        "hts,thc->shc",
        masked,
        head_grad.reshape(tokens, own_heads, HEAD_DIM),
        preferred_element_type=jnp.float32,
    ).astype(jnp.bfloat16)
    pair_sum = value_grad.astype(jnp.float32).sum(axis=1)
    group_sum = from_everyone(pair_sum, "x").sum(axis=0).astype(jnp.bfloat16)
    groups = from_everyone(group_sum, "zl")
    group_grad = jnp.moveaxis(groups, 0, 1).reshape(tokens, KV * HEAD_DIM)
    increment = lax.dot_general(
        group_grad, value_proj[0], (((1,), (1,)), ((), ())), preferred_element_type=jnp.float32
    )
    residual_grad = (grad_in[0].astype(jnp.float32) + increment).astype(jnp.bfloat16)
    target_row = increment.astype(jnp.bfloat16)
    target_rows = lax.all_gather(target_row[None], "section", axis=0, tiled=True)

    partial_scores = lax.dot_general(
        delta.reshape(HEADS, tokens * local_width),
        target_rows.reshape(section_count, tokens * local_width),
        (((1,), (1,)), ((), ())),
        preferred_element_type=jnp.float32,
    )
    row_sum = from_everyone(partial_scores, "x").sum(axis=0)
    totals = from_everyone(row_sum, "zl").sum(axis=0)
    later = jnp.arange(section_count) > lax.axis_index("section")
    raw_scores = jnp.where(later[None, :], totals / tokens, jnp.zeros_like(totals))
    onehot = (node_map[0][:, None] == jnp.arange(HEADS)[None, :]).astype(jnp.float32)
    edge_scores = jnp.dot(onehot.T, raw_scores, precision=lax.Precision.HIGHEST)
    return (residual_grad[None], edge_scores[None])


def solution(mesh):
    sections, tps = mesh.devices.shape
    side = int(round(np.sqrt(tps)))
    fine = Mesh(mesh.devices.reshape(sections, tps // side, side), ("section",) + TP)
    placed = (
        P("section", None, TP),
        P("section", TP, None),
        P("section", TP, None),
        P("section", None, TP),
        P("section", TP, None, None),
        P(),
        P("section", None),
    )
    return jax.shard_map(
        on_device,
        mesh=fine,
        in_specs=placed,
        out_specs=(P("section", None, TP), P("section", None, None)),
        check_vma=False,
    )
```

time: 442 us -> 325 us (0.74)
  the two profiles are of different devices: /device:TPU:8 before, /device:TPU:1 now
where the time goes in v2:
time: 325 us; the launch traced here: 321 us
  waiting for transfers between devices  189 us (58%)
  starting transfers between devices  66.5 us (20%)
  local copies, waits for them, and re-layouts  25.1 us (8%)
  between operations  14.2 us (4%)
  matrix products  13 us (4%)
  blocking collectives  11.8 us (4%)
    all_to_all x1, waiting for transfers between devices, on_device(): delta = lax.all_to_all(pieces, TP, 0, 0, tiled=True)  130 us
    all_to_all x4, starting transfers between devices, from_everyone(): lax.all_to_all(jnp.broadcast_to(array[None], (count, *array.shape)), axis...  61 us
    all_to_all x4, waiting for transfers between devices, from_everyone(): lax.all_to_all(jnp.broadcast_to(array[None], (count, *array.shape)), axis...  59.1 us
    all_to_all x1, blocking collectives, from_everyone(): lax.all_to_all(jnp.broadcast_to(array[None], (count, *array.shape)), axis...  11.8 us
    unnamed x19, local copies, waits for them, and re-layouts  11.3 us
  transfers between devices with their start and end apart: 6, of which 4 were waited for; matrix products, arithmetic and copies ran while one was open for 5% of the time, Pallas kernels for 0%

profile of v2, /device:TPU:1, one launch (start us, length us, event | category | flops | bytes accessed | tf_op | source)
XLA Modules:
  0.0 321.0 jit_solution(4250585393566935211)
XLA Ops:
  7.2 0.0 copy-start
  7.2 0.0 copy-start.5
  7.2 2.7 broadcast_in_dim.23
  9.9 9.0 %all-to-all-start = ((bf16[16,160,512]{2,1,0:T(8,128)(2,1)}), bf16[16,160,512]{2,1,0:T(8,128)(2,1)S(1)}, u32[]{:S(2)}, u32[]{:S(2)}) async-start(bf16[16,160,512]{2,1,0:T(8,128)(2,1)} %broadcast_in_dim.23), calls=%async_computation | async-start | bytes 5242880 | tf_op jit(solution)/shard_map/all_to_all | solution.py:18
  19.0 0.0 copy-done.5
  19.0 0.1 and_convert_fusion
  19.1 50.4 %all-to-all-done = bf16[16,160,512]{2,1,0:T(8,128)(2,1)S(1)} async-done(((bf16[16,160,512]{2,1,0:T(8,128)(2,1)}), bf16[16,160,512]{2,1,0:T(8,128)(2,1)S(1)}, u32[]{:S(2)}, u32[]{:S(2)}) %all-to-all-start) | async-done | bytes 2621472 | tf_op jit(solution)/shard_map/all_to_all | solution.py:18
  69.5 0.0 copy-start.1
  69.5 0.3 copy.33
  69.8 0.0 copy-start.3
  69.8 1.9 copy-done.1
  71.7 0.0 copy-start.4
  71.7 1.5 fusion.7
  73.3 0.0 copy-done.3
  73.3 0.2 fusion.6
  73.6 11.8 %all_to_all.30 = f32[4,160,128]{2,1,0:T(8,128)S(1)} all-to-all(f32[4,160,128]{2,1,0:T(8,128)S(1)} %broadcast_in_dim.24), channel_id=1, replica_groups=mesh['section'=32,'zl'=4,'x'=4] {'x'}, dimensions={0} | all-to-all | bytes 655360 | tf_op jit(solution)/shard_map/all_to_all | solution.py:18
  85.4 0.7 broadcast_in_dim.25
  86.1 8.6 %all-to-all-start.2 = ((bf16[4,160,128]{2,1,0:T(8,128)(2,1)}), bf16[4,160,128]{2,1,0:T(8,128)(2,1)S(1)}, u32[]{:S(2)}, u32[]{:S(2)}) async-start(bf16[4,160,128]{2,1,0:T(8,128)(2,1)} %broadcast_in_dim.25), calls=%async_computation.2 | async-start | bytes 327680 | tf_op jit(solution)/shard_map/all_to_all | solution.py:18
  94.7 0.0 copy-done.4
  94.7 3.7 %convolution_convert_fusion = bf16[2,160,8192]{2,1,0:T(8,128)(2,1)S(1)} fusion(bf16[2,128,8192]{2,1,0:T(8,128)(2,1)} %bitcast.60, bf16[160,2,128]{2,1,0:T(2,128)(2,1)S(1)} %reshape_squeeze.6), kind=kOutput, calls=%fused_computation | convolution fusion | flops 673710080 | bytes 9519104 | tf_op jit(solution)/shard_map/thc,hcd->htd/dot_general | solution.py:33
  98.4 3.1 copy.49
  101.5 0.0 all-to-all-done.2
  101.5 0.0 copy-start.2
  101.5 5.5 %all-to-all-start.3 = ((bf16[16,2,160,512]{3,2,1,0:T(8,128)(2,1)}), bf16[16,2,160,512]{3,2,1,0:T(8,128)(2,1)}, u32[]{:S(2)}, u32[]{:S(2)}) async-start(bf16[16,2,160,512]{3,2,1,0:T(8,128)(2,1)} %bitcast.56), calls=%async_computation.3 | async-start | bytes 10485760 | tf_op jit(solution)/shard_map/all_to_all | solution.py:40
  107.0 0.0 all-gather.3.cloned.1.call-start
  107.1 0.0 copy-done
  107.1 0.0 copy-done.2
  107.1 1.0 fusion.27
  108.1 0.0 all-gather.3.cloned.1.call-update
  108.2 129.8 %all-to-all-done.3 = bf16[16,2,160,512]{3,2,1,0:T(8,128)(2,1)} async-done(((bf16[16,2,160,512]{3,2,1,0:T(8,128)(2,1)}), bf16[16,2,160,512]{3,2,1,0:T(8,128)(2,1)}, u32[]{:S(2)}, u32[]{:S(2)}) %all-to-all-start.3) | async-done | bytes 5242912 | tf_op jit(solution)/shard_map/all_to_all | solution.py:40
  237.9 7.8 %copy.35 = bf16[4,8,160,512]{3,1,2,0:T(8,128)(2,1)} copy(bf16[4,8,160,512]{3,2,1,0:T(8,128)(2,1)} %bitcast.21) | data formatting | bytes 10485760
  245.8 0.0 all-gather.3.cloned.1.call-done
  245.8 6.4 %reshape.137 = bf16[32,81920]{1,0:T(8,128)(2,1)} reshape(bf16[5120,512]{1,0:T(8,128)(2,1)} %all-gather.3.cloned.1.call-done) | data formatting | bytes 10485760 | tf_op jit(solution)/shard_map/reshape | solution.py:78
  252.2 0.0 copy-start.6
  252.2 5.5 %fusion.32 = f32[32,32]{1,0:T(8,128)S(1)} fusion(bf16[32,81920]{1,0:T(8,128)(2,1)} %bitcast.57, bf16[32,81920]{1,0:T(8,128)(2,1)} %reshape.137), kind=kOutput, calls=%fused_computation.38 | convolution fusion | flops 167772160 | bytes 10489856 | tf_op jit(solution)/shard_map/dot_general | solution.py:76
  257.8 0.7 reshape.140
  258.5 17.3 %all-to-all-start.4 = ((f32[4,1,1024]{2,1,0:T(1,128)}), f32[4,1,1024]{2,1,0:T(1,128)S(1)}, u32[]{:S(2)}, u32[]{:S(2)}) async-start(f32[4,1,1024]{2,1,0:T(1,128)} %reshape.140), calls=%async_computation.4 | async-start | bytes 32768 | tf_op jit(solution)/shard_map/all_to_all | solution.py:18
  275.8 4.2 %all-to-all-done.4 = f32[4,1,1024]{2,1,0:T(1,128)S(1)} async-done(((f32[4,1,1024]{2,1,0:T(1,128)}), f32[4,1,1024]{2,1,0:T(1,128)S(1)}, u32[]{:S(2)}, u32[]{:S(2)}) %all-to-all-start.4) | async-done | bytes 16416 | tf_op jit(solution)/shard_map/all_to_all | solution.py:18
  280.0 0.5 broadcast.112
  280.5 0.7 reduce.1
  281.2 0.1 reshape.141
  281.3 0.7 reshape.142
  282.0 26.1 %all-to-all-start.5 = ((f32[4,1,1024]{2,1,0:T(1,128)}), f32[4,1,1024]{2,1,0:T(1,128)S(1)}, u32[]{:S(2)}, u32[]{:S(2)}) async-start(f32[4,1,1024]{2,1,0:T(1,128)} %reshape.142), calls=%async_computation.5 | async-start | bytes 32768 | tf_op jit(solution)/shard_map/all_to_all | solution.py:18
  308.1 4.5 %all-to-all-done.5 = f32[4,1,1024]{2,1,0:T(1,128)S(1)} async-done(((f32[4,1,1024]{2,1,0:T(1,128)}), f32[4,1,1024]{2,1,0:T(1,128)S(1)}, u32[]{:S(2)}, u32[]{:S(2)}) %all-to-all-start.5) | async-done | bytes 16416 | tf_op jit(solution)/shard_map/all_to_all | solution.py:18
  312.5 0.7 reduce.2
  313.2 0.1 reshape.143
  313.3 0.0 copy-done.6
  313.3 0.9 convolution_bitcast_fusion
  (10 shorter events, 0.1 us)
Async XLA Ops:
  7.2 99.9 %copy-start = (bf16[1,512,512]{2,1,0:T(8,128)(2,1)S(1)}, bf16[1,512,512]{2,1,0:T(8,128)(2,1)}, u32[]{:S(2)}) copy-start(bf16[1,512,512]{2,1,0:T(8,128)(2,1)} %param.9) | copy-start | bytes 1572868
  7.2 11.8 %copy-start.5 = (s32[160]{0:T(256)S(1)}, s32[160]{0:T(256)}, u32[]{:S(2)}) copy-start(s32[160]{0:T(256)} %param.12) | copy-start | bytes 1924
  9.9 59.6 %all-to-all-start = ((bf16[16,160,512]{2,1,0:T(8,128)(2,1)}), bf16[16,160,512]{2,1,0:T(8,128)(2,1)S(1)}, u32[]{:S(2)}, u32[]{:S(2)}) async-start(bf16[16,160,512]{2,1,0:T(8,128)(2,1)} %broadcast_in_dim.23), calls=%async_computation | async-start | bytes 5242880 | tf_op jit(solution)/shard_map/all_to_all | solution.py:18
  69.5 2.2 copy-start.1
  69.8 3.4 %copy-start.3 = (bf16[1,2,160,160]{3,2,1,0:T(8,128)(2,1)S(1)}, bf16[1,2,160,160]{3,2,1,0:T(8,128)(2,1)}, u32[]{:S(2)}) copy-start(bf16[1,2,160,160]{3,2,1,0:T(8,128)(2,1)} %param.11) | copy-start | bytes 307204
  71.7 22.9 %copy-start.4 = (bf16[1,160,256]{2,1,0:T(8,128)(2,1)S(1)}, bf16[1,160,256]{2,1,0:T(8,128)(2,1)}, u32[]{:S(2)}) copy-start(bf16[1,160,256]{2,1,0:T(8,128)(2,1)} %param.10) | copy-start | bytes 245764
  86.1 15.4 %all-to-all-start.2 = ((bf16[4,160,128]{2,1,0:T(8,128)(2,1)}), bf16[4,160,128]{2,1,0:T(8,128)(2,1)S(1)}, u32[]{:S(2)}, u32[]{:S(2)}) async-start(bf16[4,160,128]{2,1,0:T(8,128)(2,1)} %broadcast_in_dim.25), calls=%async_computation.2 | async-start | bytes 327680 | tf_op jit(solution)/shard_map/all_to_all | solution.py:18
  101.5 5.6 %copy-start.2 = (bf16[1,160,512]{2,1,0:T(8,128)(2,1)S(1)}, bf16[1,160,512]{2,1,0:T(8,128)(2,1)}, u32[]{:S(2)}) copy-start(bf16[1,160,512]{2,1,0:T(8,128)(2,1)} %param.7) | copy-start | bytes 491524
  101.5 136.5 %all-to-all-start.3 = ((bf16[16,2,160,512]{3,2,1,0:T(8,128)(2,1)}), bf16[16,2,160,512]{3,2,1,0:T(8,128)(2,1)}, u32[]{:S(2)}, u32[]{:S(2)}) async-start(bf16[16,2,160,512]{3,2,1,0:T(8,128)(2,1)} %bitcast.56), calls=%async_computation.3 | async-start | bytes 10485760 | tf_op jit(solution)/shard_map/all_to_all | solution.py:40
  107.0 138.7 %all-gather.3.cloned.1.call-start = ((), (), s32[]{:S(2)}) async-start(), calls=%async_computation.6 | async-start | bytes 5406720 | tf_op jit(solution)/shard_map/all_gather | solution.py:74
  252.2 61.1 %copy-start.6 = (s32[1,32]{1,0:T(1,128)S(1)}, s32[1,32]{1,0:T(1,128)}, u32[]{:S(2)}) copy-start(s32[1,32]{1,0:T(1,128)} %param.13) | copy-start | bytes 388
  258.5 21.5 %all-to-all-start.4 = ((f32[4,1,1024]{2,1,0:T(1,128)}), f32[4,1,1024]{2,1,0:T(1,128)S(1)}, u32[]{:S(2)}, u32[]{:S(2)}) async-start(f32[4,1,1024]{2,1,0:T(1,128)} %reshape.140), calls=%async_computation.4 | async-start | bytes 32768 | tf_op jit(solution)/shard_map/all_to_all | solution.py:18
  282.0 30.5 %all-to-all-start.5 = ((f32[4,1,1024]{2,1,0:T(1,128)}), f32[4,1,1024]{2,1,0:T(1,128)S(1)}, u32[]{:S(2)}, u32[]{:S(2)}) async-start(f32[4,1,1024]{2,1,0:T(1,128)} %reshape.142), calls=%async_computation.5 | async-start | bytes 32768 | tf_op jit(solution)/shard_map/all_to_all | solution.py:18
Sparse Core Ops, SparseCore 0:
  111.0 134.4 all-gather.2

commit v3 on v2

--- a/solution.py
+++ b/solution.py
@@ -11,6 +11,8 @@
 PROMPT = 32
 GROUP = 8
 TP = ("zl", "x")
+SECTION = ("zh", "y", "core")
+PLANE = ("zh", "y")
 
 
 def from_everyone(array, axis):
@@ -27,7 +29,7 @@
     own_heads = own_rows // HEAD_DIM
     width = out_proj.shape[2]
     tp_count = lax.axis_size(TP)
-    section_count = lax.axis_size("section")
+    section_count = lax.axis_size(SECTION)
     weights = out_proj[0]
 
     own_delta = jnp.einsum(
@@ -71,17 +73,18 @@
     )
     residual_grad = (grad_in[0].astype(jnp.float32) + increment).astype(jnp.bfloat16)
     target_row = increment.astype(jnp.bfloat16)
-    target_rows = lax.all_gather(target_row[None], "section", axis=0, tiled=True)
-
-    partial_scores = lax.dot_general(
-        delta.reshape(HEADS, tokens * local_width),
-        target_rows.reshape(section_count, tokens * local_width),
-        (((1,), (1,)), ((), ())),
-        preferred_element_type=jnp.float32,
-    )
-    row_sum = from_everyone(partial_scores, "x").sum(axis=0)
-    totals = from_everyone(row_sum, "zl").sum(axis=0)
-    later = jnp.arange(section_count) > lax.axis_index("section")
+    mine = lax.all_gather(target_row, PLANE, axis=0, tiled=False)
+    core = lax.axis_index("core")
+    theirs = lax.ppermute(mine, "core", [(0, 1), (1, 0)])
+    all_heads = delta.reshape(HEADS, tokens, local_width)
+    contract = (((1, 2), (1, 2)), ((), ()))
+    with_mine = lax.dot_general(all_heads, mine, contract, preferred_element_type=jnp.float32)
+    with_theirs = lax.dot_general(all_heads, theirs, contract, preferred_element_type=jnp.float32)
+    first = jnp.where(core == 0, with_mine, with_theirs)
+    second = jnp.where(core == 0, with_theirs, with_mine)
+    partial_scores = jnp.stack([first, second], axis=-1).reshape(HEADS, section_count)
+    totals = from_everyone(partial_scores, TP).sum(axis=0)
+    later = jnp.arange(section_count) > lax.axis_index(SECTION)
     raw_scores = jnp.where(later[None, :], totals / tokens, jnp.zeros_like(totals))
     onehot = (node_map[0][:, None] == jnp.arange(HEADS)[None, :]).astype(jnp.float32)
     edge_scores = jnp.dot(onehot.T, raw_scores, precision=lax.Precision.HIGHEST)
@@ -91,20 +94,25 @@
 def solution(mesh):
     sections, tps = mesh.devices.shape
     side = int(round(np.sqrt(tps)))
-    fine = Mesh(mesh.devices.reshape(sections, tps // side, side), ("section",) + TP)
+    cores = 2
+    rows = int(round(np.sqrt(sections // cores)))
+    fine = Mesh(
+        mesh.devices.reshape(sections // cores // rows, rows, cores, tps // side, side),
+        SECTION + TP,
+    )
     placed = (
-        P("section", None, TP),
-        P("section", TP, None),
-        P("section", TP, None),
-        P("section", None, TP),
-        P("section", TP, None, None),
+        P(SECTION, None, TP),
+        P(SECTION, TP, None),
+        P(SECTION, TP, None),
+        P(SECTION, None, TP),
+        P(SECTION, TP, None, None),
         P(),
-        P("section", None),
+        P(SECTION, None),
     )
     return jax.shard_map(
         on_device,
         mesh=fine,
         in_specs=placed,
-        out_specs=(P("section", None, TP), P("section", None, None)),
+        out_specs=(P(SECTION, None, TP), P(SECTION, None, None)),
         check_vma=False,
     )

time: 325 us -> 321 us (0.988); the launches traced: 321 us -> 321 us
  matrix products: 13 us -> 27.3 us
  local copies, waits for them, and re-layouts: 25.1 us -> 15.1 us
    all_to_all x1, waiting for transfers between devices: 130 us -> 0.01 us  [on_device(): delta = lax.all_to_all(pieces, TP, 0, 0, tiled=True)]
    all_gather x1, waiting for transfers between devices: 0.01 us -> 130 us  [on_device(): mine = lax.all_gather(target_row, PLANE, axis=0, tiled=False)]
    dot_general x1 -> x2, matrix products: 5.54 us -> 19.9 us  [the longest x1 10.7 us: on_device(): lax.dot_general(all_heads, mine, contract, preferred_element_type=jnp.flo...]
    unnamed x19 -> x18, local copies, waits for them, and re-layouts: 11.3 us -> 2.82 us
    reshape x1 -> x0, local copies, waits for them, and re-layouts: 6.42 us -> none  [on_device(): target_rows.reshape(section_count, tokens * local_width)]
    all_to_all x4 -> x3, starting transfers between devices: 61 us -> 55.5 us  [from_everyone(): lax.all_to_all(jnp.broadcast_to(array[None], (count, *array.shape)), axis...]
    all_gather x0 -> x1, local copies, waits for them, and re-layouts: none -> 4.82 us  [on_device(): mine = lax.all_gather(target_row, PLANE, axis=0, tiled=False)]
    all_to_all x4 -> x3, waiting for transfers between devices: 59.1 us -> 57.7 us  [from_everyone(): lax.all_to_all(jnp.broadcast_to(array[None], (count, *array.shape)), axis...]
  transfers between devices with their start and end apart: 6 -> 6, of which waited for: 4 -> 3; matrix products, arithmetic and copies ran while one was open for 5% -> 7% of each run, Pallas kernels for 0% -> 0%
where the time goes in v3:
time: 321 us
  waiting for transfers between devices  187 us (58%)
  starting transfers between devices  64 us (20%)
  matrix products  27.3 us (9%)
  local copies, waits for them, and re-layouts  15.1 us (5%)
  between operations  14.3 us (4%)
  blocking collectives  11.8 us (4%)
    all_gather x1, waiting for transfers between devices, on_device(): mine = lax.all_gather(target_row, PLANE, axis=0, tiled=False)  130 us
    all_to_all x3, waiting for transfers between devices, from_everyone(): lax.all_to_all(jnp.broadcast_to(array[None], (count, *array.shape)), axis...  57.7 us
    all_to_all x3, starting transfers between devices, from_everyone(): lax.all_to_all(jnp.broadcast_to(array[None], (count, *array.shape)), axis...  55.5 us
    all_to_all x1, blocking collectives, from_everyone(): lax.all_to_all(jnp.broadcast_to(array[None], (count, *array.shape)), axis...  11.8 us
    dot_general x1, matrix products, on_device(): lax.dot_general(all_heads, mine, contract, preferred_element_type=jnp.flo...  10.7 us
    dot_general x1, matrix products, on_device(): lax.dot_general(all_heads, theirs, contract, preferred_element_type=jnp.f...  9.21 us
  transfers between devices with their start and end apart: 6, of which 3 were waited for; matrix products, arithmetic and copies ran while one was open for 7% of the time, Pallas kernels for 0%

profile of v3, /device:TPU:1, one launch (start us, length us, event | category | flops | bytes accessed | tf_op | source)
XLA Modules:
  0.0 320.7 jit_solution(16083106923483691243)
XLA Ops:
  7.2 0.0 copy-start
  7.2 0.0 copy-start.6
  7.2 2.8 broadcast_in_dim.21
  9.9 9.0 %all-to-all-start = ((bf16[16,160,512]{2,1,0:T(8,128)(2,1)}), bf16[16,160,512]{2,1,0:T(8,128)(2,1)S(1)}, u32[]{:S(2)}, u32[]{:S(2)}) async-start(bf16[16,160,512]{2,1,0:T(8,128)(2,1)} %broadcast_in_dim.21), calls=%async_computation | async-start | bytes 5242880 | tf_op jit(solution)/shard_map/all_to_all | solution.py:20
  19.0 0.0 copy-done.6
  19.0 0.1 and_convert_fusion
  19.1 50.4 %all-to-all-done = bf16[16,160,512]{2,1,0:T(8,128)(2,1)S(1)} async-done(((bf16[16,160,512]{2,1,0:T(8,128)(2,1)}), bf16[16,160,512]{2,1,0:T(8,128)(2,1)S(1)}, u32[]{:S(2)}, u32[]{:S(2)}) %all-to-all-start) | async-done | bytes 2621472 | tf_op jit(solution)/shard_map/all_to_all | solution.py:20
  69.6 0.0 copy-start.1
  69.6 0.3 copy.51
  69.9 1.9 copy-done.1
  71.7 0.0 copy-start.4
  71.7 0.0 copy-start.5
  71.7 1.5 fusion.11
  73.3 0.0 copy-done.4
  73.3 0.2 fusion.10
  73.6 11.8 %all_to_all.25 = f32[4,160,128]{2,1,0:T(8,128)S(1)} all-to-all(f32[4,160,128]{2,1,0:T(8,128)S(1)} %broadcast_in_dim.22), channel_id=1, replica_groups=mesh['zh'=4,'y'=4,'core'=2,'zl'=4,'x'=4] {'x'}, dimensions={0} | all-to-all | bytes 655360 | tf_op jit(solution)/shard_map/all_to_all | solution.py:20
  85.4 0.7 broadcast_in_dim.23
  86.1 8.6 %all-to-all-start.2 = ((bf16[4,160,128]{2,1,0:T(8,128)(2,1)}), bf16[4,160,128]{2,1,0:T(8,128)(2,1)S(1)}, u32[]{:S(2)}, u32[]{:S(2)}) async-start(bf16[4,160,128]{2,1,0:T(8,128)(2,1)} %broadcast_in_dim.23), calls=%async_computation.2 | async-start | bytes 327680 | tf_op jit(solution)/shard_map/all_to_all | solution.py:20
  94.7 0.0 copy-done.5
  94.7 3.7 %convolution_convert_fusion = bf16[2,160,8192]{2,1,0:T(8,128)(2,1)S(1)} fusion(bf16[2,128,8192]{2,1,0:T(8,128)(2,1)} %bitcast.68, bf16[160,2,128]{2,1,0:T(2,128)(2,1)S(1)} %reshape_squeeze.6), kind=kOutput, calls=%fused_computation | convolution fusion | flops 673710080 | bytes 9519104 | tf_op jit(solution)/shard_map/thc,hcd->htd/dot_general | solution.py:35
  98.4 3.0 copy.78
  101.5 0.0 all-to-all-done.2
  101.5 0.0 copy-start.3
  101.5 5.5 %all-to-all-start.3 = ((bf16[16,2,160,512]{3,2,1,0:T(8,128)(2,1)}), bf16[16,2,160,512]{3,2,1,0:T(8,128)(2,1)}, u32[]{:S(2)}, u32[]{:S(2)}) async-start(bf16[16,2,160,512]{3,2,1,0:T(8,128)(2,1)} %bitcast.65), calls=%async_computation.3 | async-start | bytes 10485760 | tf_op jit(solution)/shard_map/all_to_all | solution.py:42
  107.0 0.0 all-gather.3.cloned.1.call-start
  107.1 0.0 copy-done
  107.1 0.0 copy-done.3
  107.1 1.0 fusion.38
  108.1 0.0 all-gather.3.cloned.1.call-update
  108.1 129.6 %all-gather.3.cloned.1.call-done = bf16[2560,512]{1,0:T(8,128)(2,1)} async-done(((bf16[160,512]{1,0:T(8,128)(2,1)}), bf16[2560,512]{1,0:T(8,128)(2,1)}) %all-gather.3.cloned.1.call-update) | async-done | bytes 2621456 | tf_op jit(solution)/shard_map/all_gather | solution.py:76
  237.7 0.0 copy-start.2
  237.7 4.8 %copy.43 = bf16[16,160,512]{2,0,1:T(8,128)(2,1)} copy(bf16[16,160,512]{2,1,0:T(8,128)(2,1)} %bitcast.69) | data formatting | bytes 5242880 | tf_op jit(solution)/shard_map/all_gather | solution.py:76
  242.5 3.0 collective-permute-start
  245.5 0.0 all-to-all-done.3
  245.6 0.0 copy-done.2
  245.6 10.7 %fusion.14 = f32[32,16]{0,1:T(8,128)S(1)} fusion(bf16[32,160,512]{2,1,0:T(8,128)(2,1)} %bitcast.11, bf16[16,160,512]{2,1,0:T(8,128)(2,1)S(1)} %bitcast.70), kind=kOutput, calls=%fused_computation.14 | convolution fusion | flops 83886080 | bytes 7866368 | tf_op jit(solution)/shard_map/dot_general | solution.py:81
  256.2 0.0 copy-start.7
  256.3 0.0 collective-permute-done
  256.3 9.2 %select_bitcast_fusion.1 = (f32[32,16,1]{0,1,2:T(8,128)S(1)}, f32[32,16,1]{0,1,2:T(8,128)S(1)}) fusion(f32[32,16]{0,1:T(8,128)S(1)} %fusion.14, pred[]{:T(512)S(6)} %eq.43, bf16[16,160,512]{2,0,1:T(8,128)(2,1)} %collective-permute-done, bf16[32,160,512]{2,1,0:T(8,128)(2,1)} %bitcast.11), kind=kOutput, calls=%fused_computation.35 | convolution fusion | flops 83887104 | bytes 7870465 | tf_op jit(solution)/shard_map/dot_general | solution.py:82
  265.5 0.1 copy.46
  265.6 0.8 reshape.136
  266.4 37.9 %all-to-all-start.4 = ((f32[16,1,1024]{2,1,0:T(1,128)}), f32[16,1,1024]{2,1,0:T(1,128)S(1)}, u32[]{:S(2)}, u32[]{:S(2)}) async-start(f32[16,1,1024]{2,1,0:T(1,128)} %reshape.136), calls=%async_computation.4 | async-start | bytes 131072 | tf_op jit(solution)/shard_map/all_to_all | solution.py:20
  304.3 7.2 %all-to-all-done.4 = f32[16,1,1024]{2,1,0:T(1,128)S(1)} async-done(((f32[16,1,1024]{2,1,0:T(1,128)}), f32[16,1,1024]{2,1,0:T(1,128)S(1)}, u32[]{:S(2)}, u32[]{:S(2)}) %all-to-all-start.4) | async-done | bytes 65568 | tf_op jit(solution)/shard_map/all_to_all | solution.py:20
  311.5 0.5 broadcast.110
  312.1 0.8 reduce.1
  312.9 0.1 reshape.137
  313.0 0.0 copy-done.7
  313.0 0.9 convolution_bitcast_fusion
  (10 shorter events, 0.2 us)
Async XLA Ops:
  7.2 99.9 %copy-start = (bf16[1,512,512]{2,1,0:T(8,128)(2,1)S(1)}, bf16[1,512,512]{2,1,0:T(8,128)(2,1)}, u32[]{:S(2)}) copy-start(bf16[1,512,512]{2,1,0:T(8,128)(2,1)} %param.9) | copy-start | bytes 1572868
  7.2 11.8 %copy-start.6 = (s32[160]{0:T(256)S(1)}, s32[160]{0:T(256)}, u32[]{:S(2)}) copy-start(s32[160]{0:T(256)} %param.12) | copy-start | bytes 1924
  9.9 59.6 %all-to-all-start = ((bf16[16,160,512]{2,1,0:T(8,128)(2,1)}), bf16[16,160,512]{2,1,0:T(8,128)(2,1)S(1)}, u32[]{:S(2)}, u32[]{:S(2)}) async-start(bf16[16,160,512]{2,1,0:T(8,128)(2,1)} %broadcast_in_dim.21), calls=%async_computation | async-start | bytes 5242880 | tf_op jit(solution)/shard_map/all_to_all | solution.py:20
  69.6 2.2 copy-start.1
  71.7 1.6 copy-start.4
  71.7 22.9 %copy-start.5 = (bf16[1,160,256]{2,1,0:T(8,128)(2,1)S(1)}, bf16[1,160,256]{2,1,0:T(8,128)(2,1)}, u32[]{:S(2)}) copy-start(bf16[1,160,256]{2,1,0:T(8,128)(2,1)} %param.10) | copy-start | bytes 245764
  86.1 15.3 %all-to-all-start.2 = ((bf16[4,160,128]{2,1,0:T(8,128)(2,1)}), bf16[4,160,128]{2,1,0:T(8,128)(2,1)S(1)}, u32[]{:S(2)}, u32[]{:S(2)}) async-start(bf16[4,160,128]{2,1,0:T(8,128)(2,1)} %broadcast_in_dim.23), calls=%async_computation.2 | async-start | bytes 327680 | tf_op jit(solution)/shard_map/all_to_all | solution.py:20
  101.5 5.6 %copy-start.3 = (bf16[1,160,512]{2,1,0:T(8,128)(2,1)S(1)}, bf16[1,160,512]{2,1,0:T(8,128)(2,1)}, u32[]{:S(2)}) copy-start(bf16[1,160,512]{2,1,0:T(8,128)(2,1)} %param.7) | copy-start | bytes 491524
  101.5 144.1 %all-to-all-start.3 = ((bf16[16,2,160,512]{3,2,1,0:T(8,128)(2,1)}), bf16[16,2,160,512]{3,2,1,0:T(8,128)(2,1)}, u32[]{:S(2)}, u32[]{:S(2)}) async-start(bf16[16,2,160,512]{3,2,1,0:T(8,128)(2,1)} %bitcast.65), calls=%async_computation.3 | async-start | bytes 10485760 | tf_op jit(solution)/shard_map/all_to_all | solution.py:42
  107.0 130.7 %all-gather.3.cloned.1.call-start = ((), (), s32[]{:S(2)}) async-start(), calls=%async_computation.5 | async-start | bytes 2785280 | tf_op jit(solution)/shard_map/all_gather | solution.py:76
  237.7 7.8 %copy-start.2 = (bf16[2560,512]{1,0:T(8,128)(2,1)S(1)}, bf16[2560,512]{1,0:T(8,128)(2,1)}, u32[]{:S(2)}) copy-start(bf16[2560,512]{1,0:T(8,128)(2,1)} %all-gather.3.cloned.1.call-done) | copy-start | bytes 7864324
  242.5 13.7 %collective-permute-start = (bf16[16,160,512]{2,0,1:T(8,128)(2,1)}, bf16[16,160,512]{2,0,1:T(8,128)(2,1)}, u32[]{:S(2)}, u32[]{:S(2)}) collective-permute-start(bf16[16,160,512]{2,0,1:T(8,128)(2,1)} %copy.43), channel_id=1, source_target_pairs={{0,16},{16,0},{1,17},{17,1},{2,18},{18,2},{3,19},{19,3},{4,20},{20... | collective-permute-start | bytes 7864328 | tf_op jit(solution)/shard_map/ppermute | solution.py:78
  256.2 56.8 %copy-start.7 = (s32[1,32]{1,0:T(1,128)S(1)}, s32[1,32]{1,0:T(1,128)}, u32[]{:S(2)}) copy-start(s32[1,32]{1,0:T(1,128)} %param.13) | copy-start | bytes 388
  266.4 45.1 %all-to-all-start.4 = ((f32[16,1,1024]{2,1,0:T(1,128)}), f32[16,1,1024]{2,1,0:T(1,128)S(1)}, u32[]{:S(2)}, u32[]{:S(2)}) async-start(f32[16,1,1024]{2,1,0:T(1,128)} %reshape.136), calls=%async_computation.4 | async-start | bytes 131072 | tf_op jit(solution)/shard_map/all_to_all | solution.py:20
Sparse Core Ops, SparseCore 0:
  110.9 126.8 all-gather.2

commit v4 on v3

--- a/solution.py
+++ b/solution.py
@@ -22,6 +22,13 @@
     )
 
 
+def gathered(piece):
+    column = from_everyone(piece, "zl")
+    row = from_everyone(column, "x")
+    tokens = piece.shape[0]
+    return jnp.transpose(row, (2, 1, 0, 3)).reshape(tokens, -1)
+
+
 def on_device(grad_in, out_proj, value_proj, head_delta, pattern, positions, node_map):
     tokens = grad_in.shape[1]
     local_width = grad_in.shape[2]
@@ -32,14 +39,9 @@
     section_count = lax.axis_size(SECTION)
     weights = out_proj[0]
 
-    own_delta = jnp.einsum(
-        "thc,hcd->htd",
-        head_delta[0].reshape(tokens, own_heads, HEAD_DIM),
-        weights.reshape(own_heads, HEAD_DIM, width),
-        preferred_element_type=jnp.float32,
-    ).astype(jnp.bfloat16)
-    pieces = own_delta.reshape(own_heads, tokens, tp_count, local_width).transpose(2, 0, 1, 3)
-    delta = lax.all_to_all(pieces, TP, 0, 0, tiled=True)
+    blocks = weights.reshape(own_rows, tp_count, local_width).transpose(1, 0, 2)
+    column_blocks = lax.all_to_all(blocks, TP, 0, 0, tiled=True)
+    delta_cols = gathered(head_delta[0])
 
     token_ids = jnp.arange(tokens)
     block_ids = token_ids // PROMPT
@@ -49,8 +51,7 @@
         & (positions[None, :] <= positions[:, None])
     )
     visible = allowed.astype(jnp.bfloat16)
-    everyone = from_everyone(grad_in[0], TP)
-    grad_rows = jnp.moveaxis(everyone, 0, 1).reshape(tokens, width)
+    grad_rows = gathered(grad_in[0])
     head_grad = lax.dot_general(
         grad_rows,
         weights,
@@ -76,7 +77,12 @@
     mine = lax.all_gather(target_row, PLANE, axis=0, tiled=False)
     core = lax.axis_index("core")
     theirs = lax.ppermute(mine, "core", [(0, 1), (1, 0)])
-    all_heads = delta.reshape(HEADS, tokens, local_width)
+    all_heads = jnp.einsum(
+        "thc,hcd->htd",
+        delta_cols.reshape(tokens, HEADS, HEAD_DIM),
+        column_blocks.reshape(HEADS, HEAD_DIM, local_width),
+        preferred_element_type=jnp.float32,
+    ).astype(jnp.bfloat16)
     contract = (((1, 2), (1, 2)), ((), ()))
     with_mine = lax.dot_general(all_heads, mine, contract, preferred_element_type=jnp.float32)
     with_theirs = lax.dot_general(all_heads, theirs, contract, preferred_element_type=jnp.float32)

time: 321 us -> 331 us (1.031)
  local copies, waits for them, and re-layouts: 15.1 us -> 33.9 us
  waiting for transfers between devices: 187 us -> 175 us
  blocking collectives: 11.8 us -> 22 us
  starting transfers between devices: 64 us -> 56.8 us
    all_gather x1, waiting for transfers between devices: 130 us -> 119 us  [on_device(): mine = lax.all_gather(target_row, PLANE, axis=0, tiled=False)]
    all_to_all x1, blocking collectives: 11.8 us -> 22 us  [from_everyone(): lax.all_to_all(jnp.broadcast_to(array[None], (count, *array.shape)), axis...]
    all_to_all x3 -> x6, starting transfers between devices: 55.5 us -> 47.9 us  [from_everyone(): lax.all_to_all(jnp.broadcast_to(array[None], (count, *array.shape)), axis...]
    transpose x0 -> x2, local copies, waits for them, and re-layouts: none -> 6.56 us  [gathered(): return jnp.transpose(row, (2, 1, 0, 3)).reshape(tokens, -1)]
    another operation x1 -> x2, local copies, waits for them, and re-layouts: 0.02 us -> 5.12 us  [the longest x1 4.36 us: on_device(): blocks = weights.reshape(own_rows, tp_count, local_width).transpose(1, 0, 2)]
    broadcast_in_dim x5 -> x8, local copies, waits for them, and re-layouts: 3.56 us -> 6.91 us  [from_everyone(): jnp.broadcast_to(array[None], (count, *array.shape))]
    all_to_all x3 -> x6, waiting for transfers between devices: 57.7 us -> 55.9 us  [from_everyone(): lax.all_to_all(jnp.broadcast_to(array[None], (count, *array.shape)), axis...]
  transfers between devices with their start and end apart: 6 -> 9, of which waited for: 3 -> 5; matrix products, arithmetic and copies ran while one was open for 7% -> 13% of each run, Pallas kernels for 0% -> 0%
where the time goes in v4:
time: 331 us; the launch traced here: 330 us
  waiting for transfers between devices  175 us (53%)
  starting transfers between devices  56.8 us (17%)
  local copies, waits for them, and re-layouts  33.9 us (10%)
  matrix products  25.7 us (8%)
  blocking collectives  22 us (7%)
  between operations  14.3 us (4%)
    all_gather x1, waiting for transfers between devices, on_device(): mine = lax.all_gather(target_row, PLANE, axis=0, tiled=False)  119 us
    all_to_all x6, waiting for transfers between devices, from_everyone(): lax.all_to_all(jnp.broadcast_to(array[None], (count, *array.shape)), axis...  55.9 us
    all_to_all x6, starting transfers between devices, from_everyone(): lax.all_to_all(jnp.broadcast_to(array[None], (count, *array.shape)), axis...  47.9 us
    all_to_all x1, blocking collectives, from_everyone(): lax.all_to_all(jnp.broadcast_to(array[None], (count, *array.shape)), axis...  22 us
    dot_general x1, matrix products, on_device(): lax.dot_general(all_heads, mine, contract, preferred_element_type=jnp.flo...  8.2 us
    dot_general x1, matrix products, on_device(): lax.dot_general(all_heads, theirs, contract, preferred_element_type=jnp.f...  7.69 us
    broadcast_in_dim x8, local copies, waits for them, and re-layouts, from_everyone(): jnp.broadcast_to(array[None], (count, *array.shape))  6.91 us
  transfers between devices with their start and end apart: 9, of which 5 were waited for; matrix products, arithmetic and copies ran while one was open for 13% of the time, Pallas kernels for 0%

profile of v4, /device:TPU:1, one launch (start us, length us, event | category | flops | bytes accessed | tf_op | source)
XLA Modules:
  0.0 330.0 jit_solution(16346740244264969313)
XLA Ops:
  7.2 0.0 copy-start
  7.2 1.0 broadcast_in_dim.29
  8.2 22.0 %all_to_all.40 = bf16[4,160,512]{2,1,0:T(8,128)(2,1)S(1)} all-to-all(bf16[4,160,512]{2,1,0:T(8,128)(2,1)S(1)} %broadcast_in_dim.29), channel_id=1, replica_groups=mesh['zh'=4,'y'=4,'core'=2,'zl'=4,'x'=4] {'zl'}, dimensions={0} | all-to-all | bytes 1310720 | tf_op jit(solution)/shard_map/all_to_all | solution.py:20
  30.2 0.5 copy.43
  30.7 2.2 broadcast_in_dim.30
  32.9 4.8 %all-to-all-start.1 = ((bf16[4,4,160,512]{3,1,2,0:T(4,128)(2,1)}), bf16[4,4,160,512]{3,1,2,0:T(4,128)(2,1)S(1)}, u32[]{:S(2)}, u32[]{:S(2)}) async-start(bf16[4,4,160,512]{3,1,2,0:T(4,128)(2,1)} %broadcast_in_dim.30), calls=%async_computation.1 | async-start | bytes 5242880 | tf_op jit(solution)/shard_map/all_to_all | solution.py:20
  37.7 0.6 and_select_fusion
  38.3 29.3 %all-to-all-done.1 = bf16[4,4,160,512]{3,1,2,0:T(4,128)(2,1)S(1)} async-done(((bf16[4,4,160,512]{3,1,2,0:T(4,128)(2,1)}), bf16[4,4,160,512]{3,1,2,0:T(4,128)(2,1)S(1)}, u32[]{:S(2)}, u32[]{:S(2)}) %all-to-all-start.1) | async-done | bytes 2621472 | tf_op jit(solution)/shard_map/all_to_all | solution.py:20
  67.6 0.8 broadcast_in_dim.39
  68.4 3.8 %all-to-all-start.4 = ((bf16[4,160,256]{2,1,0:T(8,128)(2,1)}), bf16[4,160,256]{2,1,0:T(8,128)(2,1)S(1)}, u32[]{:S(2)}, u32[]{:S(2)}) async-start(bf16[4,160,256]{2,1,0:T(8,128)(2,1)} %broadcast_in_dim.39), calls=%async_computation.4 | async-start | bytes 655360 | tf_op jit(solution)/shard_map/all_to_all | solution.py:20
  72.2 0.9 and_convert_fusion
  73.1 4.9 %copy.44 = bf16[160,4,4,512]{3,2,1,0:T(4,128)(2,1)} copy(bf16[160,4,4,512]{3,1,0,2:T(4,128)(2,1)S(1)} %bitcast.65) | data formatting | bytes 5242880 | tf_op jit(solution)/shard_map/transpose | solution.py:29
  77.9 4.3 %reshape.127 = bf16[160,8192]{1,0:T(8,128)(2,1)S(1)} reshape(bf16[160,4,4,512]{3,2,1,0:T(4,128)(2,1)} %copy.44) | data formatting | bytes 5242880 | tf_op jit(solution)/shard_map/reshape | solution.py:29
  82.2 0.0 copy-start.3
  82.2 3.8 %fusion.12 = bf16[20,2,8,128]{3,2,1,0:T(8,128)(2,1)S(1)} fusion(bf16[160,8192]{1,0:T(8,128)(2,1)S(1)} %reshape.127, bf16[1,256,8192]{2,1,0:T(8,128)(2,1)} %param.8), kind=kOutput, calls=%fused_computation.13 | convolution fusion | flops 671129600 | bytes 6897664 | tf_op jit(solution)/shard_map/dot_general | solution.py:55
  86.0 0.2 fusion.11
  86.3 0.0 all-to-all-done.4
  86.3 0.7 broadcast_in_dim.31
  87.0 3.5 %all-to-all-start.2 = ((f32[4,160,128]{2,1,0:T(8,128)}), f32[4,160,128]{2,1,0:T(8,128)S(1)}, u32[]{:S(2)}, u32[]{:S(2)}) async-start(f32[4,160,128]{2,1,0:T(8,128)} %broadcast_in_dim.31), calls=%async_computation.2 | async-start | bytes 655360 | tf_op jit(solution)/shard_map/all_to_all | solution.py:20
  90.5 0.3 copy.48
  90.7 5.6 %all-to-all-done.2 = f32[4,160,128]{2,1,0:T(8,128)S(1)} async-done(((f32[4,160,128]{2,1,0:T(8,128)}), f32[4,160,128]{2,1,0:T(8,128)S(1)}, u32[]{:S(2)}, u32[]{:S(2)}) %all-to-all-start.2) | async-done | bytes 327712 | tf_op jit(solution)/shard_map/all_to_all | solution.py:20
  96.3 1.4 broadcast_in_dim.40
  97.7 3.5 %all-to-all-start.5 = ((bf16[4,4,160,256]{3,1,2,0:T(4,128)(2,1)}), bf16[4,4,160,256]{3,1,2,0:T(4,128)(2,1)S(1)}, u32[]{:S(2)}, u32[]{:S(2)}) async-start(bf16[4,4,160,256]{3,1,2,0:T(4,128)(2,1)} %broadcast_in_dim.40), calls=%async_computation.5 | async-start | bytes 2621440 | tf_op jit(solution)/shard_map/all_to_all | solution.py:20
  101.3 13.7 %all-to-all-done.5 = bf16[4,4,160,256]{3,1,2,0:T(4,128)(2,1)S(1)} async-done(((bf16[4,4,160,256]{3,1,2,0:T(4,128)(2,1)}), bf16[4,4,160,256]{3,1,2,0:T(4,128)(2,1)S(1)}, u32[]{:S(2)}, u32[]{:S(2)}) %all-to-all-start.5) | async-done | bytes 1310752 | tf_op jit(solution)/shard_map/all_to_all | solution.py:20
  115.0 0.7 broadcast_in_dim.32
  115.7 4.3 %all-to-all-start.3 = ((bf16[4,160,128]{2,1,0:T(8,128)(2,1)}), bf16[4,160,128]{2,1,0:T(8,128)(2,1)S(1)}, u32[]{:S(2)}, u32[]{:S(2)}) async-start(bf16[4,160,128]{2,1,0:T(8,128)(2,1)} %broadcast_in_dim.32), calls=%async_computation.3 | async-start | bytes 327680 | tf_op jit(solution)/shard_map/all_to_all | solution.py:20
  120.0 4.0 %copy.61 = bf16[32,8,16,512]{3,2,1,0:T(8,128)(2,1)S(1)} copy(bf16[32,8,16,512]{3,1,2,0:T(8,128)(2,1)} %bitcast.67) | data formatting | bytes 8388608
  124.0 4.4 %copy.87 = bf16[256,16,512]{2,0,1:T(8,128)(2,1)} copy(bf16[256,16,512]{2,1,0:T(8,128)(2,1)S(1)} %bitcast.64) | data formatting | bytes 8388608 | tf_op jit(solution)/shard_map/reshape;squeeze | solution.py:42
  128.4 5.5 %all-to-all-start.6 = ((bf16[16,256,512]{2,1,0:T(8,128)(2,1)}), bf16[16,256,512]{2,1,0:T(8,128)(2,1)}, u32[]{:S(2)}, u32[]{:S(2)}) async-start(bf16[16,256,512]{2,1,0:T(8,128)(2,1)} %bitcast.63), calls=%async_computation.6 | async-start | bytes 8388608 | tf_op jit(solution)/shard_map/all_to_all | solution.py:43
  133.9 0.0 all-gather.3.cloned.1.call-start
  134.0 1.0 fusion.38
  135.1 0.0 all-gather.3.cloned.1.call-update
  135.1 119.1 %all-gather.3.cloned.1.call-done = bf16[2560,512]{1,0:T(8,128)(2,1)} async-done(((bf16[160,512]{1,0:T(8,128)(2,1)}), bf16[2560,512]{1,0:T(8,128)(2,1)}) %all-gather.3.cloned.1.call-update) | async-done | bytes 2621456 | tf_op jit(solution)/shard_map/all_gather | solution.py:77
  254.2 4.8 %copy.53 = bf16[16,160,512]{2,0,1:T(8,128)(2,1)} copy(bf16[16,160,512]{2,1,0:T(8,128)(2,1)} %bitcast.68) | data formatting | bytes 5242880 | tf_op jit(solution)/shard_map/all_gather | solution.py:77
  259.0 3.4 %collective-permute-start = (bf16[16,160,512]{2,0,1:T(8,128)(2,1)}, bf16[16,160,512]{2,0,1:T(8,128)(2,1)}, u32[]{:S(2)}, u32[]{:S(2)}) collective-permute-start(bf16[16,160,512]{2,0,1:T(8,128)(2,1)} %copy.53), channel_id=1, source_target_pairs={{0,16},{16,0},{1,17},{17,1},{2,18},{18,2},{3,19},{19,3},{4,20},{20... | collective-permute-start | bytes 7864328 | tf_op jit(solution)/shard_map/ppermute | solution.py:79
  262.4 1.7 copy.49
  264.1 0.8 reshape_reshape.3
  264.9 3.9 %convolution_convert_fusion = bf16[32,160,512]{2,1,0:T(8,128)(2,1)S(1)} fusion(bf16[32,128,512]{2,1,0:T(8,128)(2,1)} %bitcast.12, bf16[160,32,128]{2,1,0:T(8,128)(2,1)S(1)} %reshape_reshape.3), kind=kOutput, calls=%fused_computation.7 | convolution fusion | flops 673710080 | bytes 10747904 | tf_op jit(solution)/shard_map/thc,hcd->htd/dot_general | solution.py:80
  268.7 8.2 %fusion.15 = f32[32,16]{0,1:T(8,128)S(1)} fusion(bf16[32,160,512]{2,1,0:T(8,128)(2,1)S(1)} %convolution_convert_fusion, bf16[16,160,512]{2,1,0:T(8,128)(2,1)S(1)} %bitcast.69), kind=kOutput, calls=%fused_computation.15 | convolution fusion | flops 83886080 | bytes 7866368 | tf_op jit(solution)/shard_map/dot_general | solution.py:87
  277.0 7.7 %select_bitcast_fusion.1 = (f32[32,16,1]{0,1,2:T(8,128)S(1)}, f32[32,16,1]{0,1,2:T(8,128)S(1)}) fusion(f32[32,16]{0,1:T(8,128)S(1)} %fusion.15, pred[]{:T(512)S(6)} %eq.43, bf16[16,160,512]{2,0,1:T(8,128)(2,1)} %collective-permute-done, bf16[32,160,512]{2,1,0:T(8,128)(2,1)S(1)} %convolution_convert_fusion), kind=kOutput, calls=%fused_computation.35 | convolution fusion | flops 83887104 | bytes 7870465 | tf_op jit(solution)/shard_map/dot_general | solution.py:88
  284.7 0.1 copy.57
  284.8 0.8 reshape.134
  285.6 27.9 %all-to-all-start.7 = ((f32[16,1,1024]{2,1,0:T(1,128)}), f32[16,1,1024]{2,1,0:T(1,128)S(1)}, u32[]{:S(2)}, u32[]{:S(2)}) async-start(f32[16,1,1024]{2,1,0:T(1,128)} %reshape.134), calls=%async_computation.7 | async-start | bytes 131072 | tf_op jit(solution)/shard_map/all_to_all | solution.py:20
  313.5 7.2 %all-to-all-done.7 = f32[16,1,1024]{2,1,0:T(1,128)S(1)} async-done(((f32[16,1,1024]{2,1,0:T(1,128)}), f32[16,1,1024]{2,1,0:T(1,128)S(1)}, u32[]{:S(2)}, u32[]{:S(2)}) %all-to-all-start.7) | async-done | bytes 65568 | tf_op jit(solution)/shard_map/all_to_all | solution.py:20
  320.8 0.5 broadcast.112
  321.3 0.8 reduce.1
  322.1 0.1 reshape.135
  322.2 0.9 convolution_bitcast_fusion
  (22 shorter events, 0.1 us)
Async XLA Ops:
  7.2 126.8 %copy-start = (bf16[1,512,512]{2,1,0:T(8,128)(2,1)S(1)}, bf16[1,512,512]{2,1,0:T(8,128)(2,1)}, u32[]{:S(2)}) copy-start(bf16[1,512,512]{2,1,0:T(8,128)(2,1)} %param.9) | copy-start | bytes 1572868
  32.9 34.7 %copy-start.4 = (bf16[1,160,256]{2,1,0:T(8,128)(2,1)S(1)}, bf16[1,160,256]{2,1,0:T(8,128)(2,1)}, u32[]{:S(2)}) copy-start(bf16[1,160,256]{2,1,0:T(8,128)(2,1)} %param.10) | copy-start | bytes 245764
  32.9 39.3 %copy-start.5 = (s32[160]{0:T(256)S(1)}, s32[160]{0:T(256)}, u32[]{:S(2)}) copy-start(s32[160]{0:T(256)} %param.12) | copy-start | bytes 1924
  32.9 34.7 %all-to-all-start.1 = ((bf16[4,4,160,512]{3,1,2,0:T(4,128)(2,1)}), bf16[4,4,160,512]{3,1,2,0:T(4,128)(2,1)S(1)}, u32[]{:S(2)}, u32[]{:S(2)}) async-start(bf16[4,4,160,512]{3,1,2,0:T(4,128)(2,1)} %broadcast_in_dim.30), calls=%async_computation.1 | async-start | bytes 5242880 | tf_op jit(solution)/shard_map/all_to_all | solution.py:20
  68.4 17.9 %all-to-all-start.4 = ((bf16[4,160,256]{2,1,0:T(8,128)(2,1)}), bf16[4,160,256]{2,1,0:T(8,128)(2,1)S(1)}, u32[]{:S(2)}, u32[]{:S(2)}) async-start(bf16[4,160,256]{2,1,0:T(8,128)(2,1)} %broadcast_in_dim.39), calls=%async_computation.4 | async-start | bytes 655360 | tf_op jit(solution)/shard_map/all_to_all | solution.py:20
  82.2 3.8 %copy-start.3 = (bf16[1,2,160,160]{3,2,1,0:T(8,128)(2,1)S(1)}, bf16[1,2,160,160]{3,2,1,0:T(8,128)(2,1)}, u32[]{:S(2)}) copy-start(bf16[1,2,160,160]{3,2,1,0:T(8,128)(2,1)} %param.11) | copy-start | bytes 307204
  87.0 9.3 %all-to-all-start.2 = ((f32[4,160,128]{2,1,0:T(8,128)}), f32[4,160,128]{2,1,0:T(8,128)S(1)}, u32[]{:S(2)}, u32[]{:S(2)}) async-start(f32[4,160,128]{2,1,0:T(8,128)} %broadcast_in_dim.31), calls=%async_computation.2 | async-start | bytes 655360 | tf_op jit(solution)/shard_map/all_to_all | solution.py:20
  97.7 17.3 %all-to-all-start.5 = ((bf16[4,4,160,256]{3,1,2,0:T(4,128)(2,1)}), bf16[4,4,160,256]{3,1,2,0:T(4,128)(2,1)S(1)}, u32[]{:S(2)}, u32[]{:S(2)}) async-start(bf16[4,4,160,256]{3,1,2,0:T(4,128)(2,1)} %broadcast_in_dim.40), calls=%async_computation.5 | async-start | bytes 2621440 | tf_op jit(solution)/shard_map/all_to_all | solution.py:20
  115.7 12.7 %all-to-all-start.3 = ((bf16[4,160,128]{2,1,0:T(8,128)(2,1)}), bf16[4,160,128]{2,1,0:T(8,128)(2,1)S(1)}, u32[]{:S(2)}, u32[]{:S(2)}) async-start(bf16[4,160,128]{2,1,0:T(8,128)(2,1)} %broadcast_in_dim.32), calls=%async_computation.3 | async-start | bytes 327680 | tf_op jit(solution)/shard_map/all_to_all | solution.py:20
  128.4 5.6 %copy-start.2 = (bf16[1,160,512]{2,1,0:T(8,128)(2,1)S(1)}, bf16[1,160,512]{2,1,0:T(8,128)(2,1)}, u32[]{:S(2)}) copy-start(bf16[1,160,512]{2,1,0:T(8,128)(2,1)} %param.7) | copy-start | bytes 491524
  128.4 136.4 %all-to-all-start.6 = ((bf16[16,256,512]{2,1,0:T(8,128)(2,1)}), bf16[16,256,512]{2,1,0:T(8,128)(2,1)}, u32[]{:S(2)}, u32[]{:S(2)}) async-start(bf16[16,256,512]{2,1,0:T(8,128)(2,1)} %bitcast.63), calls=%async_computation.6 | async-start | bytes 8388608 | tf_op jit(solution)/shard_map/all_to_all | solution.py:43
  133.9 120.2 %all-gather.3.cloned.1.call-start = ((), (), s32[]{:S(2)}) async-start(), calls=%async_computation.8 | async-start | bytes 2785280 | tf_op jit(solution)/shard_map/all_gather | solution.py:77
  259.0 18.0 %collective-permute-start = (bf16[16,160,512]{2,0,1:T(8,128)(2,1)}, bf16[16,160,512]{2,0,1:T(8,128)(2,1)}, u32[]{:S(2)}, u32[]{:S(2)}) collective-permute-start(bf16[16,160,512]{2,0,1:T(8,128)(2,1)} %copy.53), channel_id=1, source_target_pairs={{0,16},{16,0},{1,17},{17,1},{2,18},{18,2},{3,19},{19,3},{4,20},{20... | collective-permute-start | bytes 7864328 | tf_op jit(solution)/shard_map/ppermute | solution.py:79
  264.9 3.9 %copy-start.1 = (bf16[2560,512]{1,0:T(8,128)(2,1)S(1)}, bf16[2560,512]{1,0:T(8,128)(2,1)}, u32[]{:S(2)}) copy-start(bf16[2560,512]{1,0:T(8,128)(2,1)} %all-gather.3.cloned.1.call-done) | copy-start | bytes 7864324
  276.9 45.3 %copy-start.6 = (s32[1,32]{1,0:T(1,128)S(1)}, s32[1,32]{1,0:T(1,128)}, u32[]{:S(2)}) copy-start(s32[1,32]{1,0:T(1,128)} %param.13) | copy-start | bytes 388
  285.6 35.2 %all-to-all-start.7 = ((f32[16,1,1024]{2,1,0:T(1,128)}), f32[16,1,1024]{2,1,0:T(1,128)S(1)}, u32[]{:S(2)}, u32[]{:S(2)}) async-start(f32[16,1,1024]{2,1,0:T(1,128)} %reshape.134), calls=%async_computation.7 | async-start | bytes 131072 | tf_op jit(solution)/shard_map/all_to_all | solution.py:20
Sparse Core Ops, SparseCore 0:
  137.8 116.3 all-gather.2

commit v5 on v3

--- a/solution.py
+++ b/solution.py
@@ -20,6 +20,24 @@
     return lax.all_to_all(
         jnp.broadcast_to(array[None], (count, *array.shape)), axis, 0, 0, tiled=True
     )
+
+
+def by_permutes(array, axis):
+    count = lax.axis_size(axis)
+    me = lax.axis_index(axis)
+    shifted = [array] + [
+        lax.ppermute(array, axis, [(i, (i + k) % count) for i in range(count)])
+        for k in range(1, count)
+    ]
+    stacked = jnp.stack(shifted)
+    return jnp.take(stacked, (me - jnp.arange(count)) % count, axis=0)
+
+
+def gathered(piece):
+    column = by_permutes(piece, "zl")
+    row = by_permutes(column, "x")
+    tokens = piece.shape[0]
+    return jnp.transpose(row, (2, 1, 0, 3)).reshape(tokens, -1)
 
 
 def on_device(grad_in, out_proj, value_proj, head_delta, pattern, positions, node_map):
@@ -49,8 +67,7 @@
         & (positions[None, :] <= positions[:, None])
     )
     visible = allowed.astype(jnp.bfloat16)
-    everyone = from_everyone(grad_in[0], TP)
-    grad_rows = jnp.moveaxis(everyone, 0, 1).reshape(tokens, width)
+    grad_rows = gathered(grad_in[0])
     head_grad = lax.dot_general(
         grad_rows,
         weights,
@@ -65,8 +82,8 @@
         preferred_element_type=jnp.float32,
     ).astype(jnp.bfloat16)
     pair_sum = value_grad.astype(jnp.float32).sum(axis=1)
-    group_sum = from_everyone(pair_sum, "x").sum(axis=0).astype(jnp.bfloat16)
-    groups = from_everyone(group_sum, "zl")
+    group_sum = by_permutes(pair_sum, "x").sum(axis=0).astype(jnp.bfloat16)
+    groups = by_permutes(group_sum, "zl")
     group_grad = jnp.moveaxis(groups, 0, 1).reshape(tokens, KV * HEAD_DIM)
     increment = lax.dot_general(
         group_grad, value_proj[0], (((1,), (1,)), ((), ())), preferred_element_type=jnp.float32

time: 321 us -> 392 us (1.22)
  waiting for transfers between devices: 187 us -> 272 us
  starting transfers between devices: 64 us -> 50.3 us
  blocking collectives: 11.8 us -> 0 us
  local copies, waits for them, and re-layouts: 15.1 us -> 20.1 us
    ppermute x0 -> x12, waiting for transfers between devices: none -> 156 us  [by_permutes(): lax.ppermute(array, axis, [(i, (i + k) % count) for i in range(count)])]
    all_to_all x3 -> x1, starting transfers between devices: 55.5 us -> 4.69 us  [from_everyone(): lax.all_to_all(jnp.broadcast_to(array[None], (count, *array.shape)), axis...]
    all_to_all x3 -> x1, waiting for transfers between devices: 57.7 us -> 7.23 us  [from_everyone(): lax.all_to_all(jnp.broadcast_to(array[None], (count, *array.shape)), axis...]
    ppermute x0 -> x12, starting transfers between devices: none -> 33.2 us  [by_permutes(): lax.ppermute(array, axis, [(i, (i + k) % count) for i in range(count)])]
    all_gather x1, waiting for transfers between devices: 130 us -> 109 us  [on_device(): mine = lax.all_gather(target_row, PLANE, axis=0, tiled=False)]
    all_to_all x1 -> x0, blocking collectives: 11.8 us -> none  [from_everyone(): lax.all_to_all(jnp.broadcast_to(array[None], (count, *array.shape)), axis...]
    gather x0 -> x4, local copies, waits for them, and re-layouts: none -> 4.03 us  [by_permutes(): return jnp.take(stacked, (me - jnp.arange(count)) % count, axis=0)]
  transfers between devices with their start and end apart: 6 -> 16, of which waited for: 3 -> 11; matrix products, arithmetic and copies ran while one was open for 7% -> 9% of each run, Pallas kernels for 0% -> 0%
where the time goes in v5:
time: 392 us; the launch traced here: 391 us
  waiting for transfers between devices  272 us (69%)
  starting transfers between devices  50.3 us (13%)
  matrix products  30.3 us (8%)
  local copies, waits for them, and re-layouts  20.1 us (5%)
  between operations  14.4 us (4%)
    ppermute x12, waiting for transfers between devices, by_permutes(): lax.ppermute(array, axis, [(i, (i + k) % count) for i in range(count)])  156 us
    all_gather x1, waiting for transfers between devices, on_device(): mine = lax.all_gather(target_row, PLANE, axis=0, tiled=False)  109 us
    ppermute x12, starting transfers between devices, by_permutes(): lax.ppermute(array, axis, [(i, (i + k) % count) for i in range(count)])  33.2 us
    dot_general x1, matrix products, on_device(): lax.dot_general(all_heads, mine, contract, preferred_element_type=jnp.flo...  10.7 us
    dot_general x1, matrix products, on_device(): lax.dot_general(all_heads, theirs, contract, preferred_element_type=jnp.f...  9.21 us
    all_to_all x1, starting transfers between devices, on_device(): delta = lax.all_to_all(pieces, TP, 0, 0, tiled=True)  9.19 us
  transfers between devices with their start and end apart: 16, of which 11 were waited for; matrix products, arithmetic and copies ran while one was open for 9% of the time, Pallas kernels for 0%

profile of v5, /device:TPU:1, one launch (start us, length us, event | category | flops | bytes accessed | tf_op | source)
XLA Modules:
  0.0 391.5 jit_solution(1789832643927695582)
XLA Ops:
  7.2 1.0 reshape_squeeze.6
  8.1 3.7 convolution_convert_fusion
  11.9 3.0 copy.86
  14.9 9.2 %all-to-all-start = ((bf16[16,2,160,512]{3,2,1,0:T(8,128)(2,1)}), bf16[16,2,160,512]{3,2,1,0:T(8,128)(2,1)}, u32[]{:S(2)}, u32[]{:S(2)}) async-start(bf16[16,2,160,512]{3,2,1,0:T(8,128)(2,1)} %bitcast.85), calls=%async_computation | async-start | bytes 10485760 | tf_op jit(solution)/shard_map/all_to_all | solution.py:60
  24.2 5.0 %collective-permute-start.2 = (bf16[160,512]{1,0:T(8,128)(2,1)S(1)}, bf16[160,512]{1,0:T(8,128)(2,1)S(1)}, u32[]{:S(2)}, u32[]{:S(2)}) collective-permute-start(bf16[160,512]{1,0:T(8,128)(2,1)S(1)} %bitcast.93), channel_id=1, source_target_pairs={{0,12},{4,0},{8,4},{12,8},{1,13},{5,1},{9,5},{13,9},{2,14},{6,2},{... | collective-permute-start | bytes 491528 | tf_op jit(solution)/shard_map/ppermute | solution.py:29
  29.2 1.9 collective-permute-start.1
  31.1 2.5 collective-permute-start
  33.7 76.3 %collective-permute-done.2 = bf16[160,512]{1,0:T(8,128)(2,1)S(1)} collective-permute-done((bf16[160,512]{1,0:T(8,128)(2,1)S(1)}, bf16[160,512]{1,0:T(8,128)(2,1)S(1)}, u32[]{:S(2)}, u32[]{:S(2)}) %collective-permute-start.2) | collective-permute-done | bytes 163872 | tf_op jit(solution)/shard_map/ppermute | solution.py:29
  110.0 43.2 %collective-permute-done.1 = bf16[160,512]{1,0:T(8,128)(2,1)S(1)} collective-permute-done((bf16[160,512]{1,0:T(8,128)(2,1)S(1)}, bf16[160,512]{1,0:T(8,128)(2,1)S(1)}, u32[]{:S(2)}, u32[]{:S(2)}) %collective-permute-start.1) | collective-permute-done | bytes 163872 | tf_op jit(solution)/shard_map/ppermute | solution.py:29
  153.3 0.6 gather_fusion
  153.9 0.1 broadcast_select_fusion
  154.0 4.4 %collective-permute-start.5 = (bf16[4,160,512]{2,1,0:T(8,128)(2,1)S(1)}, bf16[4,160,512]{2,1,0:T(8,128)(2,1)S(1)}, u32[]{:S(2)}, u32[]{:S(2)}) collective-permute-start(bf16[4,160,512]{2,1,0:T(8,128)(2,1)S(1)} %broadcast_select_fusion), channel_id=1, source_target_pairs={{0,3},{1,0},{2,1},{3,2},{4,7},{5,4},{6,5},{7,6},{8,11},{9,8},{10,9... | collective-permute-start | bytes 1966088 | tf_op jit(solution)/shard_map/ppermute | solution.py:29
  158.4 2.4 collective-permute-start.4
  160.8 2.6 collective-permute-start.3
  163.7 8.1 %collective-permute-done.5 = bf16[4,160,512]{2,1,0:T(8,128)(2,1)S(1)} collective-permute-done((bf16[4,160,512]{2,1,0:T(8,128)(2,1)S(1)}, bf16[4,160,512]{2,1,0:T(8,128)(2,1)S(1)}, u32[]{:S(2)}, u32[]{:S(2)}) %collective-permute-start.5) | collective-permute-done | bytes 655392 | tf_op jit(solution)/shard_map/ppermute | solution.py:29
  171.8 4.6 %collective-permute-done.4 = bf16[4,160,512]{2,1,0:T(8,128)(2,1)S(1)} collective-permute-done((bf16[4,160,512]{2,1,0:T(8,128)(2,1)S(1)}, bf16[4,160,512]{2,1,0:T(8,128)(2,1)S(1)}, u32[]{:S(2)}, u32[]{:S(2)}) %collective-permute-start.4) | collective-permute-done | bytes 655392 | tf_op jit(solution)/shard_map/ppermute | solution.py:29
  176.3 16.2 %collective-permute-done.3 = bf16[4,160,512]{2,1,0:T(8,128)(2,1)S(1)} collective-permute-done((bf16[4,160,512]{2,1,0:T(8,128)(2,1)S(1)}, bf16[4,160,512]{2,1,0:T(8,128)(2,1)S(1)}, u32[]{:S(2)}, u32[]{:S(2)}) %collective-permute-start.3) | collective-permute-done | bytes 655392 | tf_op jit(solution)/shard_map/ppermute | solution.py:29
  192.5 0.3 pad_maximum_fusion
  192.8 2.3 gather_fusion.1
  195.1 2.1 select_bitcast_fusion
  197.2 2.0 copy.45
  199.2 3.6 reshape.247
  202.8 4.6 %fusion.11 = bf16[20,2,8,128]{3,2,1,0:T(8,128)(2,1)S(1)} fusion(bf16[160,8192]{1,0:T(8,128)(2,1)} %reshape.247, bf16[1,256,8192]{2,1,0:T(8,128)(2,1)} %param.8), kind=kOutput, calls=%fused_computation.18 | convolution fusion | flops 671129600 | bytes 6897664 | tf_op jit(solution)/shard_map/dot_general | solution.py:71
  207.4 0.2 fusion.10
  207.7 1.9 collective-permute-start.8
  209.6 2.4 collective-permute-start.7
  212.0 2.9 collective-permute-start.6
  214.9 1.4 collective-permute-done.7
  216.3 2.8 collective-permute-done.6
  219.1 0.6 gather_fusion.2
  219.8 1.9 collective-permute-start.11
  221.7 1.9 collective-permute-start.10
  223.6 3.4 collective-permute-start.9
  227.0 0.3 collective-permute-done.10
  227.4 3.1 collective-permute-done.9
  230.5 0.6 gather_fusion.3
  231.1 1.0 fusion.44
  232.2 109.3 %all-gather.3.cloned.1.call-done = bf16[2560,512]{1,0:T(8,128)(2,1)} async-done(((bf16[160,512]{1,0:T(8,128)(2,1)}), bf16[2560,512]{1,0:T(8,128)(2,1)}) %all-gather.3.cloned.1.call-update) | async-done | bytes 2621456 | tf_op jit(solution)/shard_map/all_gather | solution.py:93
  341.4 4.9 %copy.52 = bf16[16,160,512]{2,0,1:T(8,128)(2,1)} copy(bf16[16,160,512]{2,1,0:T(8,128)(2,1)} %bitcast.88) | data formatting | bytes 5242880 | tf_op jit(solution)/shard_map/all_gather | solution.py:93
  346.3 3.2 collective-permute-start.12
  349.5 10.7 %fusion.14 = f32[32,16]{0,1:T(8,128)S(1)} fusion(bf16[32,160,512]{2,1,0:T(8,128)(2,1)} %bitcast.28, bf16[16,160,512]{2,1,0:T(8,128)(2,1)S(1)} %bitcast.89), kind=kOutput, calls=%fused_computation.20 | convolution fusion | flops 83886080 | bytes 7866368 | tf_op jit(solution)/shard_map/dot_general | solution.py:98
  360.2 9.2 %select_bitcast_fusion.3 = (f32[32,16,1]{0,1,2:T(8,128)S(1)}, f32[32,16,1]{0,1,2:T(8,128)S(1)}) fusion(f32[32,16]{0,1:T(8,128)S(1)} %fusion.14, pred[]{:T(512)S(6)} %eq.48, bf16[16,160,512]{2,0,1:T(8,128)(2,1)} %collective-permute-done.12, bf16[32,160,512]{2,1,0:T(8,128)(2,1)} %bitcast.28), kind=kOutput, calls=%fused_computation.48 | convolution fusion | flops 83887104 | bytes 7870465 | tf_op jit(solution)/shard_map/dot_general | solution.py:99
  369.6 0.8 reshape.287
  370.3 4.7 %all-to-all-start.1 = ((f32[16,1,1024]{2,1,0:T(1,128)}), f32[16,1,1024]{2,1,0:T(1,128)S(1)}, u32[]{:S(2)}, u32[]{:S(2)}) async-start(f32[16,1,1024]{2,1,0:T(1,128)} %reshape.287), calls=%async_computation.1 | async-start | bytes 131072 | tf_op jit(solution)/shard_map/all_to_all | solution.py:20
  375.1 7.2 %all-to-all-done.1 = f32[16,1,1024]{2,1,0:T(1,128)S(1)} async-done(((f32[16,1,1024]{2,1,0:T(1,128)}), f32[16,1,1024]{2,1,0:T(1,128)S(1)}, u32[]{:S(2)}, u32[]{:S(2)}) %all-to-all-start.1) | async-done | bytes 65568 | tf_op jit(solution)/shard_map/all_to_all | solution.py:20
  382.3 0.5 broadcast.349
  382.8 0.8 reduce.1
  383.8 0.9 convolution_bitcast_fusion
  (40 shorter events, 0.9 us)
Async XLA Ops:
  7.2 223.9 %copy-start = (bf16[1,512,512]{2,1,0:T(8,128)(2,1)S(1)}, bf16[1,512,512]{2,1,0:T(8,128)(2,1)}, u32[]{:S(2)}) copy-start(bf16[1,512,512]{2,1,0:T(8,128)(2,1)} %param.9) | copy-start | bytes 1572868
  14.9 9.3 %copy-start.2 = (bf16[1,160,512]{2,1,0:T(8,128)(2,1)S(1)}, bf16[1,160,512]{2,1,0:T(8,128)(2,1)}, u32[]{:S(2)}) copy-start(bf16[1,160,512]{2,1,0:T(8,128)(2,1)} %param.7) | copy-start | bytes 491524
  14.9 334.6 %all-to-all-start = ((bf16[16,2,160,512]{3,2,1,0:T(8,128)(2,1)}), bf16[16,2,160,512]{3,2,1,0:T(8,128)(2,1)}, u32[]{:S(2)}, u32[]{:S(2)}) async-start(bf16[16,2,160,512]{3,2,1,0:T(8,128)(2,1)} %bitcast.85), calls=%async_computation | async-start | bytes 10485760 | tf_op jit(solution)/shard_map/all_to_all | solution.py:60
  24.1 139.3 %copy-start.4 = (s32[160]{0:T(256)S(1)}, s32[160]{0:T(256)}, u32[]{:S(2)}) copy-start(s32[160]{0:T(256)} %param.12) | copy-start | bytes 1924
  24.1 317.3 %all-gather.3.cloned.1.call-start = ((), (), s32[]{:S(2)}) async-start(), calls=%async_computation.2 | async-start | bytes 2785280 | tf_op jit(solution)/shard_map/all_gather | solution.py:93
  24.2 85.8 %collective-permute-start.2 = (bf16[160,512]{1,0:T(8,128)(2,1)S(1)}, bf16[160,512]{1,0:T(8,128)(2,1)S(1)}, u32[]{:S(2)}, u32[]{:S(2)}) collective-permute-start(bf16[160,512]{1,0:T(8,128)(2,1)S(1)} %bitcast.93), channel_id=1, source_target_pairs={{0,12},{4,0},{8,4},{12,8},{1,13},{5,1},{9,5},{13,9},{2,14},{6,2},{... | collective-permute-start | bytes 491528 | tf_op jit(solution)/shard_map/ppermute | solution.py:29
  29.2 124.0 %collective-permute-start.1 = (bf16[160,512]{1,0:T(8,128)(2,1)S(1)}, bf16[160,512]{1,0:T(8,128)(2,1)S(1)}, u32[]{:S(2)}, u32[]{:S(2)}) collective-permute-start(bf16[160,512]{1,0:T(8,128)(2,1)S(1)} %bitcast.94), channel_id=1, source_target_pairs={{0,8},{4,12},{8,0},{12,4},{1,9},{5,13},{9,1},{13,5},{2,10},{6,14},... | collective-permute-start | bytes 491528 | tf_op jit(solution)/shard_map/ppermute | solution.py:29
  31.1 122.1 %collective-permute-start = (bf16[160,512]{1,0:T(8,128)(2,1)S(1)}, bf16[160,512]{1,0:T(8,128)(2,1)S(1)}, u32[]{:S(2)}, u32[]{:S(2)}) collective-permute-start(bf16[160,512]{1,0:T(8,128)(2,1)S(1)} %bitcast.95), channel_id=1, source_target_pairs={{0,4},{4,8},{8,12},{12,0},{1,5},{5,9},{9,13},{13,1},{2,6},{6,10},{... | collective-permute-start | bytes 491528 | tf_op jit(solution)/shard_map/ppermute | solution.py:29
  154.0 17.7 %collective-permute-start.5 = (bf16[4,160,512]{2,1,0:T(8,128)(2,1)S(1)}, bf16[4,160,512]{2,1,0:T(8,128)(2,1)S(1)}, u32[]{:S(2)}, u32[]{:S(2)}) collective-permute-start(bf16[4,160,512]{2,1,0:T(8,128)(2,1)S(1)} %broadcast_select_fusion), channel_id=1, source_target_pairs={{0,3},{1,0},{2,1},{3,2},{4,7},{5,4},{6,5},{7,6},{8,11},{9,8},{10,9... | collective-permute-start | bytes 1966088 | tf_op jit(solution)/shard_map/ppermute | solution.py:29
  158.4 17.9 %collective-permute-start.4 = (bf16[4,160,512]{2,1,0:T(8,128)(2,1)S(1)}, bf16[4,160,512]{2,1,0:T(8,128)(2,1)S(1)}, u32[]{:S(2)}, u32[]{:S(2)}) collective-permute-start(bf16[4,160,512]{2,1,0:T(8,128)(2,1)S(1)} %broadcast_select_fusion), channel_id=1, source_target_pairs={{0,2},{1,3},{2,0},{3,1},{4,6},{5,7},{6,4},{7,5},{8,10},{9,11},{10,... | collective-permute-start | bytes 1966088 | tf_op jit(solution)/shard_map/ppermute | solution.py:29
  160.8 31.7 %collective-permute-start.3 = (bf16[4,160,512]{2,1,0:T(8,128)(2,1)S(1)}, bf16[4,160,512]{2,1,0:T(8,128)(2,1)S(1)}, u32[]{:S(2)}, u32[]{:S(2)}) collective-permute-start(bf16[4,160,512]{2,1,0:T(8,128)(2,1)S(1)} %broadcast_select_fusion), channel_id=1, source_target_pairs={{0,1},{1,2},{2,3},{3,0},{4,5},{5,6},{6,7},{7,4},{8,9},{9,10},{10,1... | collective-permute-start | bytes 1966088 | tf_op jit(solution)/shard_map/ppermute | solution.py:29
  202.8 4.6 %copy-start.3 = (bf16[1,2,160,160]{3,2,1,0:T(8,128)(2,1)S(1)}, bf16[1,2,160,160]{3,2,1,0:T(8,128)(2,1)}, u32[]{:S(2)}) copy-start(bf16[1,2,160,160]{3,2,1,0:T(8,128)(2,1)} %param.11) | copy-start | bytes 307204
  207.7 7.2 %collective-permute-start.8 = (f32[160,128]{1,0:T(8,128)S(1)}, f32[160,128]{1,0:T(8,128)S(1)}, u32[]{:S(2)}, u32[]{:S(2)}) collective-permute-start(f32[160,128]{1,0:T(8,128)S(1)} %bitcast.96), channel_id=1, source_target_pairs={{0,3},{1,0},{2,1},{3,2},{4,7},{5,4},{6,5},{7,6},{8,11},{9,8},{10,9... | collective-permute-start | bytes 245768 | tf_op jit(solution)/shard_map/ppermute | solution.py:29
  209.6 6.7 %collective-permute-start.7 = (f32[160,128]{1,0:T(8,128)S(1)}, f32[160,128]{1,0:T(8,128)S(1)}, u32[]{:S(2)}, u32[]{:S(2)}) collective-permute-start(f32[160,128]{1,0:T(8,128)S(1)} %bitcast.97), channel_id=1, source_target_pairs={{0,2},{1,3},{2,0},{3,1},{4,6},{5,7},{6,4},{7,5},{8,10},{9,11},{10,... | collective-permute-start | bytes 245768 | tf_op jit(solution)/shard_map/ppermute | solution.py:29
  212.0 7.1 %collective-permute-start.6 = (f32[160,128]{1,0:T(8,128)S(1)}, f32[160,128]{1,0:T(8,128)S(1)}, u32[]{:S(2)}, u32[]{:S(2)}) collective-permute-start(f32[160,128]{1,0:T(8,128)S(1)} %bitcast.98), channel_id=1, source_target_pairs={{0,1},{1,2},{2,3},{3,0},{4,5},{5,6},{6,7},{7,4},{8,9},{9,10},{10,1... | collective-permute-start | bytes 245768 | tf_op jit(solution)/shard_map/ppermute | solution.py:29
  219.8 7.2 %collective-permute-start.11 = (bf16[160,128]{1,0:T(8,128)(2,1)S(1)}, bf16[160,128]{1,0:T(8,128)(2,1)S(1)}, u32[]{:S(2)}, u32[]{:S(2)}) collective-permute-start(bf16[160,128]{1,0:T(8,128)(2,1)S(1)} %select_reduce_fusion), channel_id=1, source_target_pairs={{0,12},{4,0},{8,4},{12,8},{1,13},{5,1},{9,5},{13,9},{2,14},{6,2},{... | collective-permute-start | bytes 122888 | tf_op jit(solution)/shard_map/ppermute | solution.py:29
  221.7 5.6 %collective-permute-start.10 = (bf16[160,128]{1,0:T(8,128)(2,1)S(1)}, bf16[160,128]{1,0:T(8,128)(2,1)S(1)}, u32[]{:S(2)}, u32[]{:S(2)}) collective-permute-start(bf16[160,128]{1,0:T(8,128)(2,1)S(1)} %select_reduce_fusion), channel_id=1, source_target_pairs={{0,8},{4,12},{8,0},{12,4},{1,9},{5,13},{9,1},{13,5},{2,10},{6,14},... | collective-permute-start | bytes 122888 | tf_op jit(solution)/shard_map/ppermute | solution.py:29
  223.6 6.8 %collective-permute-start.9 = (bf16[160,128]{1,0:T(8,128)(2,1)S(1)}, bf16[160,128]{1,0:T(8,128)(2,1)S(1)}, u32[]{:S(2)}, u32[]{:S(2)}) collective-permute-start(bf16[160,128]{1,0:T(8,128)(2,1)S(1)} %select_reduce_fusion), channel_id=1, source_target_pairs={{0,4},{4,8},{8,12},{12,0},{1,5},{5,9},{9,13},{13,1},{2,6},{6,10},{... | collective-permute-start | bytes 122888 | tf_op jit(solution)/shard_map/ppermute | solution.py:29
  341.4 8.1 %copy-start.1 = (bf16[2560,512]{1,0:T(8,128)(2,1)S(1)}, bf16[2560,512]{1,0:T(8,128)(2,1)}, u32[]{:S(2)}) copy-start(bf16[2560,512]{1,0:T(8,128)(2,1)} %all-gather.3.cloned.1.call-done) | copy-start | bytes 7864324
  346.3 13.9 %collective-permute-start.12 = (bf16[16,160,512]{2,0,1:T(8,128)(2,1)}, bf16[16,160,512]{2,0,1:T(8,128)(2,1)}, u32[]{:S(2)}, u32[]{:S(2)}) collective-permute-start(bf16[16,160,512]{2,0,1:T(8,128)(2,1)} %copy.52), channel_id=1, source_target_pairs={{0,16},{16,0},{1,17},{17,1},{2,18},{18,2},{3,19},{19,3},{4,20},{20... | collective-permute-start | bytes 7864328 | tf_op jit(solution)/shard_map/ppermute | solution.py:95
  360.2 23.6 %copy-start.5 = (s32[1,32]{1,0:T(1,128)S(1)}, s32[1,32]{1,0:T(1,128)}, u32[]{:S(2)}) copy-start(s32[1,32]{1,0:T(1,128)} %param.13) | copy-start | bytes 388
  370.3 12.0 %all-to-all-start.1 = ((f32[16,1,1024]{2,1,0:T(1,128)}), f32[16,1,1024]{2,1,0:T(1,128)S(1)}, u32[]{:S(2)}, u32[]{:S(2)}) async-start(f32[16,1,1024]{2,1,0:T(1,128)} %reshape.287), calls=%async_computation.1 | async-start | bytes 131072 | tf_op jit(solution)/shard_map/all_to_all | solution.py:20
Sparse Core Ops, SparseCore 0:
  232.3 109.1 all-gather.2

commit v6 on v3

--- a/solution.py
+++ b/solution.py
@@ -78,10 +78,11 @@
     theirs = lax.ppermute(mine, "core", [(0, 1), (1, 0)])
     all_heads = delta.reshape(HEADS, tokens, local_width)
     contract = (((1, 2), (1, 2)), ((), ()))
-    with_mine = lax.dot_general(all_heads, mine, contract, preferred_element_type=jnp.float32)
-    with_theirs = lax.dot_general(all_heads, theirs, contract, preferred_element_type=jnp.float32)
-    first = jnp.where(core == 0, with_mine, with_theirs)
-    second = jnp.where(core == 0, with_theirs, with_mine)
+    both = jnp.concatenate([mine, theirs], axis=0)
+    scores = lax.dot_general(all_heads, both, contract, preferred_element_type=jnp.float32)
+    half = scores.shape[1] // 2
+    first = jnp.where(core == 0, scores[:, :half], scores[:, half:])
+    second = jnp.where(core == 0, scores[:, half:], scores[:, :half])
     partial_scores = jnp.stack([first, second], axis=-1).reshape(HEADS, section_count)
     totals = from_everyone(partial_scores, TP).sum(axis=0)
     later = jnp.arange(section_count) > lax.axis_index(SECTION)

time: 321 us -> 314 us (0.978)
  matrix products: 27.3 us -> 16.8 us
  waiting for transfers between devices: 187 us -> 192 us
    dot_general x2 -> x1, matrix products: 19.9 us -> 9.4 us  [on_device(): lax.dot_general(all_heads, both, contract, preferred_element_type=jnp.flo...]
    ppermute x1, waiting for transfers between devices: 0.01 us -> 4.46 us  [on_device(): theirs = lax.ppermute(mine, 'core', [(0, 1), (1, 0)])]
  transfers between devices with their start and end apart: 6 -> 6, of which waited for: 3 -> 4; matrix products, arithmetic and copies ran while one was open for 7% -> 4% of each run, Pallas kernels for 0% -> 0%
where the time goes in v6:
time: 314 us; the launch traced here: 313 us
  waiting for transfers between devices  192 us (61%)
  starting transfers between devices  63.7 us (20%)
  matrix products  16.8 us (5%)
  between operations  14.2 us (5%)
  local copies, waits for them, and re-layouts  13.4 us (4%)
  blocking collectives  11.8 us (4%)
    all_gather x1, waiting for transfers between devices, on_device(): mine = lax.all_gather(target_row, PLANE, axis=0, tiled=False)  130 us
    all_to_all x3, waiting for transfers between devices, from_everyone(): lax.all_to_all(jnp.broadcast_to(array[None], (count, *array.shape)), axis...  57.7 us
    all_to_all x3, starting transfers between devices, from_everyone(): lax.all_to_all(jnp.broadcast_to(array[None], (count, *array.shape)), axis...  54.8 us
    all_to_all x1, blocking collectives, from_everyone(): lax.all_to_all(jnp.broadcast_to(array[None], (count, *array.shape)), axis...  11.8 us
    dot_general x1, matrix products, on_device(): lax.dot_general(all_heads, both, contract, preferred_element_type=jnp.flo...  9.4 us
  transfers between devices with their start and end apart: 6, of which 4 were waited for; matrix products, arithmetic and copies ran while one was open for 4% of the time, Pallas kernels for 0%

profile of v6, /device:TPU:1, one launch (start us, length us, event | category | flops | bytes accessed | tf_op | source)
XLA Modules:
  0.0 313.4 jit_solution(15868643809766731)
XLA Ops:
  7.2 0.0 copy-start
  7.2 0.0 copy-start.5
  7.2 2.7 broadcast_in_dim.21
  9.9 9.0 %all-to-all-start = ((bf16[16,160,512]{2,1,0:T(8,128)(2,1)}), bf16[16,160,512]{2,1,0:T(8,128)(2,1)S(1)}, u32[]{:S(2)}, u32[]{:S(2)}) async-start(bf16[16,160,512]{2,1,0:T(8,128)(2,1)} %broadcast_in_dim.21), calls=%async_computation | async-start | bytes 5242880 | tf_op jit(solution)/shard_map/all_to_all | solution.py:20
  19.0 0.0 copy-done.5
  19.0 0.1 and_convert_fusion
  19.1 50.4 %all-to-all-done = bf16[16,160,512]{2,1,0:T(8,128)(2,1)S(1)} async-done(((bf16[16,160,512]{2,1,0:T(8,128)(2,1)}), bf16[16,160,512]{2,1,0:T(8,128)(2,1)S(1)}, u32[]{:S(2)}, u32[]{:S(2)}) %all-to-all-start) | async-done | bytes 2621472 | tf_op jit(solution)/shard_map/all_to_all | solution.py:20
  69.5 0.0 copy-start.1
  69.5 0.3 copy.51
  69.8 1.9 copy-done.1
  71.7 0.0 copy-start.3
  71.7 0.0 copy-start.4
  71.7 1.5 fusion.12
  73.3 0.0 copy-done.3
  73.3 0.2 fusion.11
  73.6 11.8 %all_to_all.25 = f32[4,160,128]{2,1,0:T(8,128)S(1)} all-to-all(f32[4,160,128]{2,1,0:T(8,128)S(1)} %broadcast_in_dim.22), channel_id=1, replica_groups=mesh['zh'=4,'y'=4,'core'=2,'zl'=4,'x'=4] {'x'}, dimensions={0} | all-to-all | bytes 655360 | tf_op jit(solution)/shard_map/all_to_all | solution.py:20
  85.4 0.7 broadcast_in_dim.23
  86.1 8.6 %all-to-all-start.2 = ((bf16[4,160,128]{2,1,0:T(8,128)(2,1)}), bf16[4,160,128]{2,1,0:T(8,128)(2,1)S(1)}, u32[]{:S(2)}, u32[]{:S(2)}) async-start(bf16[4,160,128]{2,1,0:T(8,128)(2,1)} %broadcast_in_dim.23), calls=%async_computation.2 | async-start | bytes 327680 | tf_op jit(solution)/shard_map/all_to_all | solution.py:20
  94.7 0.0 copy-done.4
  94.7 3.7 %convolution_convert_fusion = bf16[2,160,8192]{2,1,0:T(8,128)(2,1)S(1)} fusion(bf16[2,128,8192]{2,1,0:T(8,128)(2,1)} %bitcast.63, bf16[160,2,128]{2,1,0:T(2,128)(2,1)S(1)} %reshape_squeeze.6), kind=kOutput, calls=%fused_computation | convolution fusion | flops 673710080 | bytes 9519104 | tf_op jit(solution)/shard_map/thc,hcd->htd/dot_general | solution.py:35
  98.4 3.0 copy.70
  101.4 0.0 all-to-all-done.2
  101.5 0.0 copy-start.2
  101.5 5.5 %all-to-all-start.3 = ((bf16[16,2,160,512]{3,2,1,0:T(8,128)(2,1)}), bf16[16,2,160,512]{3,2,1,0:T(8,128)(2,1)}, u32[]{:S(2)}, u32[]{:S(2)}) async-start(bf16[16,2,160,512]{3,2,1,0:T(8,128)(2,1)} %bitcast.60), calls=%async_computation.3 | async-start | bytes 10485760 | tf_op jit(solution)/shard_map/all_to_all | solution.py:42
  107.0 0.0 all-gather.3.cloned.1.call-start
  107.1 0.0 copy-done
  107.1 0.0 copy-done.2
  107.1 1.0 fusion.38
  108.1 0.0 all-gather.3.cloned.1.call-update
  108.1 130.3 %all-gather.3.cloned.1.call-done = bf16[2560,512]{1,0:T(8,128)(2,1)} async-done(((bf16[160,512]{1,0:T(8,128)(2,1)}), bf16[2560,512]{1,0:T(8,128)(2,1)}) %all-gather.3.cloned.1.call-update) | async-done | bytes 2621456 | tf_op jit(solution)/shard_map/all_gather | solution.py:76
  238.4 3.2 %copy.44 = bf16[16,160,512]{2,0,1:T(8,128)(2,1)S(1)} copy(bf16[16,160,512]{2,1,0:T(8,128)(2,1)} %bitcast.64) | data formatting | bytes 5242880 | tf_op jit(solution)/shard_map/all_gather | solution.py:76
  241.6 3.3 %collective-permute-start = (bf16[16,160,512]{2,0,1:T(8,128)(2,1)S(1)}, bf16[16,160,512]{2,0,1:T(8,128)(2,1)}, u32[]{:S(2)}, u32[]{:S(2)}) collective-permute-start(bf16[16,160,512]{2,0,1:T(8,128)(2,1)S(1)} %copy.44), channel_id=1, source_target_pairs={{0,16},{16,0},{1,17},{17,1},{2,18},{18,2},{3,19},{19,3},{4,20},{20... | collective-permute-start | bytes 7864328 | tf_op jit(solution)/shard_map/ppermute | solution.py:78
  244.9 4.5 %collective-permute-done = bf16[16,160,512]{2,0,1:T(8,128)(2,1)} collective-permute-done((bf16[16,160,512]{2,0,1:T(8,128)(2,1)S(1)}, bf16[16,160,512]{2,0,1:T(8,128)(2,1)}, u32[]{:S(2)}, u32[]{:S(2)}) %collective-permute-start) | collective-permute-done | bytes 2621472 | tf_op jit(solution)/shard_map/ppermute | solution.py:78
  249.4 0.0 all-to-all-done.3
  249.4 0.0 copy-start.6
  249.4 9.4 %fusion.15 = f32[32,32]{0,1:T(8,128)S(1)} fusion(bf16[16,160,512]{2,0,1:T(8,128)(2,1)} %collective-permute-done, bf16[16,160,512]{2,0,1:T(8,128)(2,1)S(1)} %copy.44, bf16[32,160,512]{2,1,0:T(8,128)(2,1)} %bitcast.11), kind=kOutput, calls=%fused_computation.15 | convolution fusion | flops 178257920 | bytes 10489856 | tf_op jit(solution)/shard_map/dot_general | solution.py:82
  258.8 0.1 copy.46
  258.9 0.8 reshape.135
  259.7 37.2 %all-to-all-start.4 = ((f32[16,1,1024]{2,1,0:T(1,128)}), f32[16,1,1024]{2,1,0:T(1,128)S(1)}, u32[]{:S(2)}, u32[]{:S(2)}) async-start(f32[16,1,1024]{2,1,0:T(1,128)} %reshape.135), calls=%async_computation.4 | async-start | bytes 131072 | tf_op jit(solution)/shard_map/all_to_all | solution.py:20
  297.0 7.2 %all-to-all-done.4 = f32[16,1,1024]{2,1,0:T(1,128)S(1)} async-done(((f32[16,1,1024]{2,1,0:T(1,128)}), f32[16,1,1024]{2,1,0:T(1,128)S(1)}, u32[]{:S(2)}, u32[]{:S(2)}) %all-to-all-start.4) | async-done | bytes 65568 | tf_op jit(solution)/shard_map/all_to_all | solution.py:20
  304.2 0.5 broadcast.110
  304.7 0.8 reduce.1
  305.5 0.1 reshape.136
  305.7 0.0 copy-done.6
  305.7 0.9 convolution_bitcast_fusion
  (11 shorter events, 0.2 us)
Async XLA Ops:
  7.2 99.9 %copy-start = (bf16[1,512,512]{2,1,0:T(8,128)(2,1)S(1)}, bf16[1,512,512]{2,1,0:T(8,128)(2,1)}, u32[]{:S(2)}) copy-start(bf16[1,512,512]{2,1,0:T(8,128)(2,1)} %param.9) | copy-start | bytes 1572868
  7.2 11.8 %copy-start.5 = (s32[160]{0:T(256)S(1)}, s32[160]{0:T(256)}, u32[]{:S(2)}) copy-start(s32[160]{0:T(256)} %param.12) | copy-start | bytes 1924
  9.9 59.6 %all-to-all-start = ((bf16[16,160,512]{2,1,0:T(8,128)(2,1)}), bf16[16,160,512]{2,1,0:T(8,128)(2,1)S(1)}, u32[]{:S(2)}, u32[]{:S(2)}) async-start(bf16[16,160,512]{2,1,0:T(8,128)(2,1)} %broadcast_in_dim.21), calls=%async_computation | async-start | bytes 5242880 | tf_op jit(solution)/shard_map/all_to_all | solution.py:20
  69.5 2.2 copy-start.1
  71.7 1.6 copy-start.3
  71.7 22.9 %copy-start.4 = (bf16[1,160,256]{2,1,0:T(8,128)(2,1)S(1)}, bf16[1,160,256]{2,1,0:T(8,128)(2,1)}, u32[]{:S(2)}) copy-start(bf16[1,160,256]{2,1,0:T(8,128)(2,1)} %param.10) | copy-start | bytes 245764
  86.1 15.4 %all-to-all-start.2 = ((bf16[4,160,128]{2,1,0:T(8,128)(2,1)}), bf16[4,160,128]{2,1,0:T(8,128)(2,1)S(1)}, u32[]{:S(2)}, u32[]{:S(2)}) async-start(bf16[4,160,128]{2,1,0:T(8,128)(2,1)} %broadcast_in_dim.23), calls=%async_computation.2 | async-start | bytes 327680 | tf_op jit(solution)/shard_map/all_to_all | solution.py:20
  101.5 5.6 %copy-start.2 = (bf16[1,160,512]{2,1,0:T(8,128)(2,1)S(1)}, bf16[1,160,512]{2,1,0:T(8,128)(2,1)}, u32[]{:S(2)}) copy-start(bf16[1,160,512]{2,1,0:T(8,128)(2,1)} %param.7) | copy-start | bytes 491524
  101.5 147.9 %all-to-all-start.3 = ((bf16[16,2,160,512]{3,2,1,0:T(8,128)(2,1)}), bf16[16,2,160,512]{3,2,1,0:T(8,128)(2,1)}, u32[]{:S(2)}, u32[]{:S(2)}) async-start(bf16[16,2,160,512]{3,2,1,0:T(8,128)(2,1)} %bitcast.60), calls=%async_computation.3 | async-start | bytes 10485760 | tf_op jit(solution)/shard_map/all_to_all | solution.py:42
  107.0 131.4 %all-gather.3.cloned.1.call-start = ((), (), s32[]{:S(2)}) async-start(), calls=%async_computation.5 | async-start | bytes 2785280 | tf_op jit(solution)/shard_map/all_gather | solution.py:76
  241.6 7.7 %collective-permute-start = (bf16[16,160,512]{2,0,1:T(8,128)(2,1)S(1)}, bf16[16,160,512]{2,0,1:T(8,128)(2,1)}, u32[]{:S(2)}, u32[]{:S(2)}) collective-permute-start(bf16[16,160,512]{2,0,1:T(8,128)(2,1)S(1)} %copy.44), channel_id=1, source_target_pairs={{0,16},{16,0},{1,17},{17,1},{2,18},{18,2},{3,19},{19,3},{4,20},{20... | collective-permute-start | bytes 7864328 | tf_op jit(solution)/shard_map/ppermute | solution.py:78
  249.4 56.3 %copy-start.6 = (s32[1,32]{1,0:T(1,128)S(1)}, s32[1,32]{1,0:T(1,128)}, u32[]{:S(2)}) copy-start(s32[1,32]{1,0:T(1,128)} %param.13) | copy-start | bytes 388
  259.7 44.5 %all-to-all-start.4 = ((f32[16,1,1024]{2,1,0:T(1,128)}), f32[16,1,1024]{2,1,0:T(1,128)S(1)}, u32[]{:S(2)}, u32[]{:S(2)}) async-start(f32[16,1,1024]{2,1,0:T(1,128)} %reshape.135), calls=%async_computation.4 | async-start | bytes 131072 | tf_op jit(solution)/shard_map/all_to_all | solution.py:20
Sparse Core Ops, SparseCore 0:
  110.9 127.5 all-gather.2

commit v7 on v4

--- a/solution.py
+++ b/solution.py
@@ -41,7 +41,6 @@
 
     blocks = weights.reshape(own_rows, tp_count, local_width).transpose(1, 0, 2)
     column_blocks = lax.all_to_all(blocks, TP, 0, 0, tiled=True)
-    delta_cols = gathered(head_delta[0])
 
     token_ids = jnp.arange(tokens)
     block_ids = token_ids // PROMPT
@@ -51,7 +50,8 @@
         & (positions[None, :] <= positions[:, None])
     )
     visible = allowed.astype(jnp.bfloat16)
-    grad_rows = gathered(grad_in[0])
+    everyone = from_everyone(grad_in[0], TP)
+    grad_rows = jnp.moveaxis(everyone, 0, 1).reshape(tokens, width)
     head_grad = lax.dot_general(
         grad_rows,
         weights,
@@ -75,6 +75,8 @@
     residual_grad = (grad_in[0].astype(jnp.float32) + increment).astype(jnp.bfloat16)
     target_row = increment.astype(jnp.bfloat16)
     mine = lax.all_gather(target_row, PLANE, axis=0, tiled=False)
+    delta_piece, target_row = lax.optimization_barrier((head_delta[0], target_row))
+    delta_cols = gathered(delta_piece)
     core = lax.axis_index("core")
     theirs = lax.ppermute(mine, "core", [(0, 1), (1, 0)])
     all_heads = jnp.einsum(
@@ -84,10 +86,11 @@
         preferred_element_type=jnp.float32,
     ).astype(jnp.bfloat16)
     contract = (((1, 2), (1, 2)), ((), ()))
-    with_mine = lax.dot_general(all_heads, mine, contract, preferred_element_type=jnp.float32)
-    with_theirs = lax.dot_general(all_heads, theirs, contract, preferred_element_type=jnp.float32)
-    first = jnp.where(core == 0, with_mine, with_theirs)
-    second = jnp.where(core == 0, with_theirs, with_mine)
+    both = jnp.concatenate([mine, theirs], axis=0)
+    scores = lax.dot_general(all_heads, both, contract, preferred_element_type=jnp.float32)
+    half = scores.shape[1] // 2
+    first = jnp.where(core == 0, scores[:, :half], scores[:, half:])
+    second = jnp.where(core == 0, scores[:, half:], scores[:, :half])
     partial_scores = jnp.stack([first, second], axis=-1).reshape(HEADS, section_count)
     totals = from_everyone(partial_scores, TP).sum(axis=0)
     later = jnp.arange(section_count) > lax.axis_index(SECTION)

time: 331 us -> 324 us (0.979)
  blocking collectives: 22 us -> 35 us
  matrix products: 25.7 us -> 13.2 us
  waiting for transfers between devices: 175 us -> 181 us
  local copies, waits for them, and re-layouts: 33.9 us -> 28.1 us
  starting transfers between devices: 56.8 us -> 51.2 us
    all_to_all x1 -> x3, blocking collectives: 22 us -> 35 us  [from_everyone(): lax.all_to_all(jnp.broadcast_to(array[None], (count, *array.shape)), axis...]
    dot_general x2 -> x1, matrix products: 15.9 us -> 5.78 us  [on_device(): lax.dot_general(all_heads, both, contract, preferred_element_type=jnp.flo...]
    all_to_all x6 -> x3, waiting for transfers between devices: 55.9 us -> 63.4 us  [from_everyone(): lax.all_to_all(jnp.broadcast_to(array[None], (count, *array.shape)), axis...]
    all_to_all x0 -> x1, local copies, waits for them, and re-layouts: none -> 6.46 us  [on_device(): column_blocks = lax.all_to_all(blocks, TP, 0, 0, tiled=True)]
    all_to_all x6 -> x3, starting transfers between devices: 47.9 us -> 42.6 us  [from_everyone(): lax.all_to_all(jnp.broadcast_to(array[None], (count, *array.shape)), axis...]
    transpose x2 -> x1, local copies, waits for them, and re-layouts: 6.56 us -> 1.69 us  [gathered(): return jnp.transpose(row, (2, 1, 0, 3)).reshape(tokens, -1)]
    another operation x1 -> x0, local copies, waits for them, and re-layouts: 4.36 us -> none  [on_device(): blocks = weights.reshape(own_rows, tp_count, local_width).transpose(1, 0, 2)]
    unnamed x17, local copies, waits for them, and re-layouts: 4.97 us -> 9.23 us
  transfers between devices with their start and end apart: 9 -> 6, of which waited for: 5 -> 4; matrix products, arithmetic and copies ran while one was open for 13% -> 7% of each run, Pallas kernels for 0% -> 0%
where the time goes in v7:
time: 324 us; the launch traced here: 323 us
  waiting for transfers between devices  181 us (56%)
  starting transfers between devices  51.2 us (16%)
  blocking collectives  35 us (11%)
  local copies, waits for them, and re-layouts  28.1 us (9%)
  between operations  14.3 us (4%)
  matrix products  13.2 us (4%)
    all_gather x1, waiting for transfers between devices, on_device(): mine = lax.all_gather(target_row, PLANE, axis=0, tiled=False)  116 us
    all_to_all x3, waiting for transfers between devices, from_everyone(): lax.all_to_all(jnp.broadcast_to(array[None], (count, *array.shape)), axis...  63.4 us
    all_to_all x3, starting transfers between devices, from_everyone(): lax.all_to_all(jnp.broadcast_to(array[None], (count, *array.shape)), axis...  42.6 us
    all_to_all x3, blocking collectives, from_everyone(): lax.all_to_all(jnp.broadcast_to(array[None], (count, *array.shape)), axis...  35 us
    unnamed x17, local copies, waits for them, and re-layouts  9.23 us
  transfers between devices with their start and end apart: 6, of which 4 were waited for; matrix products, arithmetic and copies ran while one was open for 7% of the time, Pallas kernels for 0%

profile of v7, /device:TPU:1, one launch (start us, length us, event | category | flops | bytes accessed | tf_op | source)
XLA Modules:
  0.0 323.3 jit_solution(14472549571240503597)
XLA Ops:
  7.2 0.0 copy-start
  7.2 0.0 copy-start.5
  7.2 2.7 broadcast_in_dim.25
  9.9 9.0 %all-to-all-start = ((bf16[16,160,512]{2,1,0:T(8,128)(2,1)}), bf16[16,160,512]{2,1,0:T(8,128)(2,1)S(1)}, u32[]{:S(2)}, u32[]{:S(2)}) async-start(bf16[16,160,512]{2,1,0:T(8,128)(2,1)} %broadcast_in_dim.25), calls=%async_computation | async-start | bytes 5242880 | tf_op jit(solution)/shard_map/all_to_all | solution.py:20
  19.0 0.0 copy-done.5
  19.0 0.1 and_convert_fusion
  19.1 50.4 %all-to-all-done = bf16[16,160,512]{2,1,0:T(8,128)(2,1)S(1)} async-done(((bf16[16,160,512]{2,1,0:T(8,128)(2,1)}), bf16[16,160,512]{2,1,0:T(8,128)(2,1)S(1)}, u32[]{:S(2)}, u32[]{:S(2)}) %all-to-all-start) | async-done | bytes 2621472 | tf_op jit(solution)/shard_map/all_to_all | solution.py:20
  69.5 0.0 copy-start.1
  69.5 0.3 copy.62
  69.8 1.9 copy-done.1
  71.7 1.5 fusion.13
  73.3 0.0 copy-done.3
  73.3 0.2 fusion.12
  73.6 11.8 %all_to_all.35 = f32[4,160,128]{2,1,0:T(8,128)S(1)} all-to-all(f32[4,160,128]{2,1,0:T(8,128)S(1)} %broadcast_in_dim.26), channel_id=1, replica_groups=mesh['zh'=4,'y'=4,'core'=2,'zl'=4,'x'=4] {'x'}, dimensions={0} | all-to-all | bytes 655360 | tf_op jit(solution)/shard_map/all_to_all | solution.py:20
  85.4 13.9 %all_to_all.36 = bf16[4,160,128]{2,1,0:T(8,128)(2,1)S(1)} all-to-all(bf16[4,160,128]{2,1,0:T(8,128)(2,1)S(1)} %broadcast_in_dim.27), channel_id=1, replica_groups=mesh['zh'=4,'y'=4,'core'=2,'zl'=4,'x'=4] {'zl'}, dimensions={0} | all-to-all | bytes 327680 | tf_op jit(solution)/shard_map/all_to_all | solution.py:20
  99.4 0.0 copy-done
  99.4 0.0 copy-done.2
  99.4 1.0 fusion.38
  100.4 0.0 copy-done.4
  100.5 9.2 %all_to_all.37 = bf16[4,160,256]{2,1,0:T(8,128)(2,1)S(1)} all-to-all(bf16[4,160,256]{2,1,0:T(8,128)(2,1)S(1)} %broadcast_in_dim.30), channel_id=1, replica_groups=mesh['zh'=4,'y'=4,'core'=2,'zl'=4,'x'=4] {'zl'}, dimensions={0} | all-to-all | bytes 655360 | tf_op jit(solution)/shard_map/all_to_all | solution.py:20
  109.7 0.3 copy.50
  109.9 1.4 broadcast_in_dim.31
  111.4 3.5 %all-to-all-start.4 = ((bf16[4,4,160,256]{3,1,2,0:T(4,128)(2,1)}), bf16[4,4,160,256]{3,1,2,0:T(4,128)(2,1)S(1)}, u32[]{:S(2)}, u32[]{:S(2)}) async-start(bf16[4,4,160,256]{3,1,2,0:T(4,128)(2,1)} %broadcast_in_dim.31), calls=%async_computation.4 | async-start | bytes 2621440 | tf_op jit(solution)/shard_map/all_to_all | solution.py:20
  114.9 6.4 %copy.52 = bf16[1,256,8192]{1,2,0:T(8,128)(2,1)} copy(bf16[1,256,8192]{2,1,0:T(8,128)(2,1)} %param.8) | data formatting | bytes 8388608 | tf_op args[1]
  121.3 5.7 %all-to-all-done.4 = bf16[4,4,160,256]{3,1,2,0:T(4,128)(2,1)S(1)} async-done(((bf16[4,4,160,256]{3,1,2,0:T(4,128)(2,1)}), bf16[4,4,160,256]{3,1,2,0:T(4,128)(2,1)S(1)}, u32[]{:S(2)}, u32[]{:S(2)}) %all-to-all-start.4) | async-done | bytes 1310752 | tf_op jit(solution)/shard_map/all_to_all | solution.py:20
  127.0 4.5 %all-to-all-start.5 = ((bf16[16,256,512]{1,2,0:T(8,128)(2,1)}), bf16[16,256,512]{1,2,0:T(8,128)(2,1)}, u32[]{:S(2)}, u32[]{:S(2)}) async-start(bf16[16,256,512]{1,2,0:T(8,128)(2,1)} %bitcast.57), calls=%async_computation.5 | async-start | bytes 8388608 | tf_op jit(solution)/shard_map/all_to_all | solution.py:43
  131.6 0.0 all-gather.3.cloned.1.call-start
  131.6 0.7 all-gather.3.cloned.1.call-update
  132.3 116.5 %all-gather.3.cloned.1.call-done = bf16[2560,512]{1,0:T(8,128)(2,1)} async-done(((bf16[160,512]{1,0:T(8,128)(2,1)}), bf16[2560,512]{1,0:T(8,128)(2,1)}) %all-gather.3.cloned.1.call-update) | async-done | bytes 2621456 | tf_op jit(solution)/shard_map/all_gather | solution.py:77
  248.8 4.8 %copy.56 = bf16[16,160,512]{2,0,1:T(8,128)(2,1)} copy(bf16[16,160,512]{2,1,0:T(8,128)(2,1)} %bitcast.61) | data formatting | bytes 5242880 | tf_op jit(solution)/shard_map/all_gather | solution.py:77
  253.6 4.1 %collective-permute-start = (bf16[16,160,512]{2,0,1:T(8,128)(2,1)}, bf16[16,160,512]{2,0,1:T(8,128)(2,1)}, u32[]{:S(2)}, u32[]{:S(2)}) collective-permute-start(bf16[16,160,512]{2,0,1:T(8,128)(2,1)} %copy.56), channel_id=1, source_target_pairs={{0,16},{16,0},{1,17},{17,1},{2,18},{18,2},{3,19},{19,3},{4,20},{20... | collective-permute-start | bytes 7864328 | tf_op jit(solution)/shard_map/ppermute | solution.py:81
  257.7 1.7 copy.51
  259.4 0.5 reshape_reshape.3
  259.9 0.0 all-to-all-done.5
  259.9 6.5 %copy.53 = bf16[16,256,512]{2,1,0:T(8,128)(2,1)} copy(bf16[16,256,512]{1,2,0:T(8,128)(2,1)} %all-to-all-done.5) | data formatting | bytes 8388608 | tf_op jit(solution)/shard_map/all_to_all | solution.py:43
  266.4 3.7 %convolution_convert_fusion = bf16[32,160,512]{2,1,0:T(8,128)(2,1)S(1)} fusion(bf16[32,128,512]{2,1,0:T(8,128)(2,1)} %bitcast.58, bf16[160,32,128]{2,1,0:T(8,128)(2,1)S(1)} %reshape_reshape.3), kind=kOutput, calls=%fused_computation.7 | convolution fusion | flops 673710080 | bytes 10747904 | tf_op jit(solution)/shard_map/thc,hcd->htd/dot_general | solution.py:82
  270.1 0.0 copy-start.6
  270.1 0.0 collective-permute-done
  270.1 5.8 %fusion.16 = f32[32,32]{0,1:T(8,128)S(1)} fusion(bf16[16,160,512]{2,0,1:T(8,128)(2,1)} %collective-permute-done, bf16[16,160,512]{2,0,1:T(8,128)(2,1)} %copy.56, bf16[32,160,512]{2,1,0:T(8,128)(2,1)S(1)} %convolution_convert_fusion), kind=kOutput, calls=%fused_computation.15 | convolution fusion | flops 178257920 | bytes 10489856 | tf_op jit(solution)/shard_map/dot_general | solution.py:90
  276.0 0.1 copy.59
  276.1 0.8 reshape.133
  276.8 30.0 %all-to-all-start.6 = ((f32[16,1,1024]{2,1,0:T(1,128)}), f32[16,1,1024]{2,1,0:T(1,128)S(1)}, u32[]{:S(2)}, u32[]{:S(2)}) async-start(f32[16,1,1024]{2,1,0:T(1,128)} %reshape.133), calls=%async_computation.6 | async-start | bytes 131072 | tf_op jit(solution)/shard_map/all_to_all | solution.py:20
  306.9 7.2 %all-to-all-done.6 = f32[16,1,1024]{2,1,0:T(1,128)S(1)} async-done(((f32[16,1,1024]{2,1,0:T(1,128)}), f32[16,1,1024]{2,1,0:T(1,128)S(1)}, u32[]{:S(2)}, u32[]{:S(2)}) %all-to-all-start.6) | async-done | bytes 65568 | tf_op jit(solution)/shard_map/all_to_all | solution.py:20
  314.1 0.5 broadcast.112
  314.6 0.8 reduce.1
  315.4 0.1 reshape.134
  315.6 0.0 copy-done.6
  315.6 0.9 convolution_bitcast_fusion
  (15 shorter events, 0.2 us)
Async XLA Ops:
  7.2 92.2 %copy-start = (bf16[1,512,512]{2,1,0:T(8,128)(2,1)S(1)}, bf16[1,512,512]{2,1,0:T(8,128)(2,1)}, u32[]{:S(2)}) copy-start(bf16[1,512,512]{2,1,0:T(8,128)(2,1)} %param.9) | copy-start | bytes 1572868
  7.2 11.8 %copy-start.5 = (s32[160]{0:T(256)S(1)}, s32[160]{0:T(256)}, u32[]{:S(2)}) copy-start(s32[160]{0:T(256)} %param.12) | copy-start | bytes 1924
  9.9 59.6 %all-to-all-start = ((bf16[16,160,512]{2,1,0:T(8,128)(2,1)}), bf16[16,160,512]{2,1,0:T(8,128)(2,1)S(1)}, u32[]{:S(2)}, u32[]{:S(2)}) async-start(bf16[16,160,512]{2,1,0:T(8,128)(2,1)} %broadcast_in_dim.25), calls=%async_computation | async-start | bytes 5242880 | tf_op jit(solution)/shard_map/all_to_all | solution.py:20
  69.5 2.2 copy-start.1
  71.7 1.6 copy-start.3
  71.7 27.7 %copy-start.2 = (bf16[1,160,512]{2,1,0:T(8,128)(2,1)S(1)}, bf16[1,160,512]{2,1,0:T(8,128)(2,1)}, u32[]{:S(2)}) copy-start(bf16[1,160,512]{2,1,0:T(8,128)(2,1)} %param.7) | copy-start | bytes 491524
  71.7 28.7 %copy-start.4 = (bf16[1,160,256]{2,1,0:T(8,128)(2,1)S(1)}, bf16[1,160,256]{2,1,0:T(8,128)(2,1)}, u32[]{:S(2)}) copy-start(bf16[1,160,256]{2,1,0:T(8,128)(2,1)} %param.10) | copy-start | bytes 245764
  111.4 15.7 %all-to-all-start.4 = ((bf16[4,4,160,256]{3,1,2,0:T(4,128)(2,1)}), bf16[4,4,160,256]{3,1,2,0:T(4,128)(2,1)S(1)}, u32[]{:S(2)}, u32[]{:S(2)}) async-start(bf16[4,4,160,256]{3,1,2,0:T(4,128)(2,1)} %broadcast_in_dim.31), calls=%async_computation.4 | async-start | bytes 2621440 | tf_op jit(solution)/shard_map/all_to_all | solution.py:20
  127.0 132.9 %all-to-all-start.5 = ((bf16[16,256,512]{1,2,0:T(8,128)(2,1)}), bf16[16,256,512]{1,2,0:T(8,128)(2,1)}, u32[]{:S(2)}, u32[]{:S(2)}) async-start(bf16[16,256,512]{1,2,0:T(8,128)(2,1)} %bitcast.57), calls=%async_computation.5 | async-start | bytes 8388608 | tf_op jit(solution)/shard_map/all_to_all | solution.py:43
  131.6 117.2 %all-gather.3.cloned.1.call-start = ((), (), s32[]{:S(2)}) async-start(), calls=%async_computation.7 | async-start | bytes 2785280 | tf_op jit(solution)/shard_map/all_gather | solution.py:77
  253.6 16.5 %collective-permute-start = (bf16[16,160,512]{2,0,1:T(8,128)(2,1)}, bf16[16,160,512]{2,0,1:T(8,128)(2,1)}, u32[]{:S(2)}, u32[]{:S(2)}) collective-permute-start(bf16[16,160,512]{2,0,1:T(8,128)(2,1)} %copy.56), channel_id=1, source_target_pairs={{0,16},{16,0},{1,17},{17,1},{2,18},{18,2},{3,19},{19,3},{4,20},{20... | collective-permute-start | bytes 7864328 | tf_op jit(solution)/shard_map/ppermute | solution.py:81
  270.1 45.5 %copy-start.6 = (s32[1,32]{1,0:T(1,128)S(1)}, s32[1,32]{1,0:T(1,128)}, u32[]{:S(2)}) copy-start(s32[1,32]{1,0:T(1,128)} %param.13) | copy-start | bytes 388
  276.8 37.3 %all-to-all-start.6 = ((f32[16,1,1024]{2,1,0:T(1,128)}), f32[16,1,1024]{2,1,0:T(1,128)S(1)}, u32[]{:S(2)}, u32[]{:S(2)}) async-start(f32[16,1,1024]{2,1,0:T(1,128)} %reshape.133), calls=%async_computation.6 | async-start | bytes 131072 | tf_op jit(solution)/shard_map/all_to_all | solution.py:20
Sparse Core Ops, SparseCore 0:
  135.4 113.3 all-gather.2

commit v8 on v3

--- a/solution.py
+++ b/solution.py
@@ -12,7 +12,6 @@
 GROUP = 8
 TP = ("zl", "x")
 SECTION = ("zh", "y", "core")
-PLANE = ("zh", "y")
 
 
 def from_everyone(array, axis):
@@ -73,16 +72,12 @@
     )
     residual_grad = (grad_in[0].astype(jnp.float32) + increment).astype(jnp.bfloat16)
     target_row = increment.astype(jnp.bfloat16)
-    mine = lax.all_gather(target_row, PLANE, axis=0, tiled=False)
-    core = lax.axis_index("core")
-    theirs = lax.ppermute(mine, "core", [(0, 1), (1, 0)])
+    target_rows = lax.all_gather(target_row, SECTION, axis=0, tiled=False)
     all_heads = delta.reshape(HEADS, tokens, local_width)
     contract = (((1, 2), (1, 2)), ((), ()))
-    with_mine = lax.dot_general(all_heads, mine, contract, preferred_element_type=jnp.float32)
-    with_theirs = lax.dot_general(all_heads, theirs, contract, preferred_element_type=jnp.float32)
-    first = jnp.where(core == 0, with_mine, with_theirs)
-    second = jnp.where(core == 0, with_theirs, with_mine)
-    partial_scores = jnp.stack([first, second], axis=-1).reshape(HEADS, section_count)
+    partial_scores = lax.dot_general(
+        all_heads, target_rows, contract, preferred_element_type=jnp.float32
+    )
     totals = from_everyone(partial_scores, TP).sum(axis=0)
     later = jnp.arange(section_count) > lax.axis_index(SECTION)
     raw_scores = jnp.where(later[None, :], totals / tokens, jnp.zeros_like(totals))

time: 321 us -> 314 us (0.978)
  waiting for transfers between devices: 187 us -> 195 us
  starting transfers between devices: 64 us -> 57.7 us
  matrix products: 27.3 us -> 22.4 us
  local copies, waits for them, and re-layouts: 15.1 us -> 10.2 us
    all_to_all x1, waiting for transfers between devices: 0.01 us -> 130 us  [on_device(): delta = lax.all_to_all(pieces, TP, 0, 0, tiled=True)]
    all_gather x1, waiting for transfers between devices: 130 us -> 7.55 us  [on_device(): target_rows = lax.all_gather(target_row, SECTION, axis=0, tiled=False)]
    dot_general x2 -> x1, matrix products: 19.9 us -> 15 us  [on_device(): lax.dot_general(all_heads, target_rows, contract, preferred_element_type=...]
    all_gather x1 -> x0, local copies, waits for them, and re-layouts: 4.82 us -> none  [on_device(): mine = lax.all_gather(target_row, PLANE, axis=0, tiled=False)]
    all_to_all x3, starting transfers between devices: 55.5 us -> 52 us  [from_everyone(): lax.all_to_all(jnp.broadcast_to(array[None], (count, *array.shape)), axis...]
  transfers between devices with their start and end apart: 6 -> 5, of which waited for: 3 -> 4; matrix products, arithmetic and copies ran while one was open for 7% -> 3% of each run, Pallas kernels for 0% -> 0%
where the time goes in v8:
time: 314 us; the launch traced here: 312 us
  waiting for transfers between devices  195 us (62%)
  starting transfers between devices  57.7 us (18%)
  matrix products  22.4 us (7%)
  between operations  14.2 us (5%)
  blocking collectives  11.8 us (4%)
  local copies, waits for them, and re-layouts  10.2 us (3%)
    all_to_all x1, waiting for transfers between devices, on_device(): delta = lax.all_to_all(pieces, TP, 0, 0, tiled=True)  130 us
    all_to_all x3, waiting for transfers between devices, from_everyone(): lax.all_to_all(jnp.broadcast_to(array[None], (count, *array.shape)), axis...  57.8 us
    all_to_all x3, starting transfers between devices, from_everyone(): lax.all_to_all(jnp.broadcast_to(array[None], (count, *array.shape)), axis...  52 us
    dot_general x1, matrix products, on_device(): lax.dot_general(all_heads, target_rows, contract, preferred_element_type=...  15 us
    all_to_all x1, blocking collectives, from_everyone(): lax.all_to_all(jnp.broadcast_to(array[None], (count, *array.shape)), axis...  11.8 us
    all_gather x1, waiting for transfers between devices, on_device(): target_rows = lax.all_gather(target_row, SECTION, axis=0, tiled=False)  7.55 us
  transfers between devices with their start and end apart: 5, of which 4 were waited for; matrix products, arithmetic and copies ran while one was open for 3% of the time, Pallas kernels for 0%

profile of v8, /device:TPU:1, one launch (start us, length us, event | category | flops | bytes accessed | tf_op | source)
XLA Modules:
  0.0 312.2 jit_solution(6522015427781656960)
XLA Ops:
  7.2 0.0 copy-start
  7.2 0.0 copy-start.5
  7.2 2.8 broadcast_in_dim.19
  9.9 9.0 %all-to-all-start = ((bf16[16,160,512]{2,1,0:T(8,128)(2,1)}), bf16[16,160,512]{2,1,0:T(8,128)(2,1)S(1)}, u32[]{:S(2)}, u32[]{:S(2)}) async-start(bf16[16,160,512]{2,1,0:T(8,128)(2,1)} %broadcast_in_dim.19), calls=%async_computation | async-start | bytes 5242880 | tf_op jit(solution)/shard_map/all_to_all | solution.py:19
  19.0 0.0 copy-done.5
  19.0 0.1 and_convert_fusion
  19.1 50.4 %all-to-all-done = bf16[16,160,512]{2,1,0:T(8,128)(2,1)S(1)} async-done(((bf16[16,160,512]{2,1,0:T(8,128)(2,1)}), bf16[16,160,512]{2,1,0:T(8,128)(2,1)S(1)}, u32[]{:S(2)}, u32[]{:S(2)}) %all-to-all-start) | async-done | bytes 2621472 | tf_op jit(solution)/shard_map/all_to_all | solution.py:19
  69.5 0.0 copy-start.1
  69.6 0.3 copy.37
  69.8 0.0 copy-start.3
  69.8 1.9 copy-done.1
  71.7 0.0 copy-start.4
  71.7 1.5 fusion.10
  73.3 0.0 copy-done.3
  73.3 0.2 fusion.9
  73.6 11.8 %all_to_all.25 = f32[4,160,128]{2,1,0:T(8,128)S(1)} all-to-all(f32[4,160,128]{2,1,0:T(8,128)S(1)} %broadcast_in_dim.20), channel_id=1, replica_groups=mesh['zh'=4,'y'=4,'core'=2,'zl'=4,'x'=4] {'x'}, dimensions={0} | all-to-all | bytes 655360 | tf_op jit(solution)/shard_map/all_to_all | solution.py:19
  85.4 0.7 broadcast_in_dim.21
  86.1 8.6 %all-to-all-start.2 = ((bf16[4,160,128]{2,1,0:T(8,128)(2,1)}), bf16[4,160,128]{2,1,0:T(8,128)(2,1)S(1)}, u32[]{:S(2)}, u32[]{:S(2)}) async-start(bf16[4,160,128]{2,1,0:T(8,128)(2,1)} %broadcast_in_dim.21), calls=%async_computation.2 | async-start | bytes 327680 | tf_op jit(solution)/shard_map/all_to_all | solution.py:19
  94.7 0.0 copy-done.4
  94.7 3.7 %convolution_convert_fusion = bf16[2,160,8192]{2,1,0:T(8,128)(2,1)S(1)} fusion(bf16[2,128,8192]{2,1,0:T(8,128)(2,1)} %bitcast.58, bf16[160,2,128]{2,1,0:T(2,128)(2,1)S(1)} %reshape_squeeze.6), kind=kOutput, calls=%fused_computation | convolution fusion | flops 673710080 | bytes 9519104 | tf_op jit(solution)/shard_map/thc,hcd->htd/dot_general | solution.py:34
  98.4 3.1 copy.60
  101.5 0.0 all-to-all-done.2
  101.5 0.0 copy-start.2
  101.5 5.5 %all-to-all-start.3 = ((bf16[16,2,160,512]{3,2,1,0:T(8,128)(2,1)}), bf16[16,2,160,512]{3,2,1,0:T(8,128)(2,1)}, u32[]{:S(2)}, u32[]{:S(2)}) async-start(bf16[16,2,160,512]{3,2,1,0:T(8,128)(2,1)} %bitcast.55), calls=%async_computation.3 | async-start | bytes 10485760 | tf_op jit(solution)/shard_map/all_to_all | solution.py:41
  107.0 0.2 all-gather.3.cloned.1.call-start
  107.3 0.0 copy-done
  107.3 0.0 copy-done.2
  107.3 1.0 fusion.35
  108.3 0.0 all-gather.3.cloned.1.call-update
  108.4 129.6 %all-to-all-done.3 = bf16[16,2,160,512]{3,2,1,0:T(8,128)(2,1)} async-done(((bf16[16,2,160,512]{3,2,1,0:T(8,128)(2,1)}), bf16[16,2,160,512]{3,2,1,0:T(8,128)(2,1)}, u32[]{:S(2)}, u32[]{:S(2)}) %all-to-all-start.3) | async-done | bytes 5242912 | tf_op jit(solution)/shard_map/all_to_all | solution.py:41
  238.0 7.5 %all-gather.3.cloned.1.call-done = bf16[5120,512]{1,0:T(8,128)(2,1)} async-done(((bf16[160,512]{1,0:T(8,128)(2,1)}), bf16[5120,512]{1,0:T(8,128)(2,1)}) %all-gather.3.cloned.1.call-update) | async-done | bytes 5242896 | tf_op jit(solution)/shard_map/all_gather | solution.py:75
  245.5 0.0 copy-start.6
  245.5 15.0 %fusion.13 = f32[32,32]{1,0:T(8,128)S(1)} fusion(bf16[32,160,512]{2,1,0:T(8,128)(2,1)} %bitcast.62, bf16[32,160,512]{2,1,0:T(8,128)(2,1)} %bitcast.11), kind=kOutput, calls=%fused_computation.12 | convolution fusion | flops 167772160 | bytes 10489856 | tf_op jit(solution)/shard_map/dot_general | solution.py:78
  260.5 0.8 reshape.135
  261.3 34.4 %all-to-all-start.4 = ((f32[16,1,1024]{2,1,0:T(1,128)}), f32[16,1,1024]{2,1,0:T(1,128)S(1)}, u32[]{:S(2)}, u32[]{:S(2)}) async-start(f32[16,1,1024]{2,1,0:T(1,128)} %reshape.135), calls=%async_computation.4 | async-start | bytes 131072 | tf_op jit(solution)/shard_map/all_to_all | solution.py:19
  295.7 7.3 %all-to-all-done.4 = f32[16,1,1024]{2,1,0:T(1,128)S(1)} async-done(((f32[16,1,1024]{2,1,0:T(1,128)}), f32[16,1,1024]{2,1,0:T(1,128)S(1)}, u32[]{:S(2)}, u32[]{:S(2)}) %all-to-all-start.4) | async-done | bytes 65568 | tf_op jit(solution)/shard_map/all_to_all | solution.py:19
  303.0 0.5 broadcast.111
  303.5 0.8 reduce.1
  304.3 0.1 reshape.136
  304.5 0.0 copy-done.6
  304.5 0.9 convolution_bitcast_fusion
  (8 shorter events, 0.1 us)
Async XLA Ops:
  7.2 100.1 %copy-start = (bf16[1,512,512]{2,1,0:T(8,128)(2,1)S(1)}, bf16[1,512,512]{2,1,0:T(8,128)(2,1)}, u32[]{:S(2)}) copy-start(bf16[1,512,512]{2,1,0:T(8,128)(2,1)} %param.9) | copy-start | bytes 1572868
  7.2 11.8 %copy-start.5 = (s32[160]{0:T(256)S(1)}, s32[160]{0:T(256)}, u32[]{:S(2)}) copy-start(s32[160]{0:T(256)} %param.12) | copy-start | bytes 1924
  9.9 59.6 %all-to-all-start = ((bf16[16,160,512]{2,1,0:T(8,128)(2,1)}), bf16[16,160,512]{2,1,0:T(8,128)(2,1)S(1)}, u32[]{:S(2)}, u32[]{:S(2)}) async-start(bf16[16,160,512]{2,1,0:T(8,128)(2,1)} %broadcast_in_dim.19), calls=%async_computation | async-start | bytes 5242880 | tf_op jit(solution)/shard_map/all_to_all | solution.py:19
  69.5 2.2 copy-start.1
  69.8 3.5 %copy-start.3 = (bf16[1,2,160,160]{3,2,1,0:T(8,128)(2,1)S(1)}, bf16[1,2,160,160]{3,2,1,0:T(8,128)(2,1)}, u32[]{:S(2)}) copy-start(bf16[1,2,160,160]{3,2,1,0:T(8,128)(2,1)} %param.11) | copy-start | bytes 307204
  71.7 22.9 %copy-start.4 = (bf16[1,160,256]{2,1,0:T(8,128)(2,1)S(1)}, bf16[1,160,256]{2,1,0:T(8,128)(2,1)}, u32[]{:S(2)}) copy-start(bf16[1,160,256]{2,1,0:T(8,128)(2,1)} %param.10) | copy-start | bytes 245764
  86.1 15.4 %all-to-all-start.2 = ((bf16[4,160,128]{2,1,0:T(8,128)(2,1)}), bf16[4,160,128]{2,1,0:T(8,128)(2,1)S(1)}, u32[]{:S(2)}, u32[]{:S(2)}) async-start(bf16[4,160,128]{2,1,0:T(8,128)(2,1)} %broadcast_in_dim.21), calls=%async_computation.2 | async-start | bytes 327680 | tf_op jit(solution)/shard_map/all_to_all | solution.py:19
  101.5 5.8 %copy-start.2 = (bf16[1,160,512]{2,1,0:T(8,128)(2,1)S(1)}, bf16[1,160,512]{2,1,0:T(8,128)(2,1)}, u32[]{:S(2)}) copy-start(bf16[1,160,512]{2,1,0:T(8,128)(2,1)} %param.7) | copy-start | bytes 491524
  101.5 136.5 %all-to-all-start.3 = ((bf16[16,2,160,512]{3,2,1,0:T(8,128)(2,1)}), bf16[16,2,160,512]{3,2,1,0:T(8,128)(2,1)}, u32[]{:S(2)}, u32[]{:S(2)}) async-start(bf16[16,2,160,512]{3,2,1,0:T(8,128)(2,1)} %bitcast.55), calls=%async_computation.3 | async-start | bytes 10485760 | tf_op jit(solution)/shard_map/all_to_all | solution.py:41
  107.0 138.5 %all-gather.3.cloned.1.call-start = ((), (), s32[]{:S(2)}) async-start(), calls=%async_computation.5 | async-start | bytes 5406720 | tf_op jit(solution)/shard_map/all_gather | solution.py:75
  245.5 59.0 %copy-start.6 = (s32[1,32]{1,0:T(1,128)S(1)}, s32[1,32]{1,0:T(1,128)}, u32[]{:S(2)}) copy-start(s32[1,32]{1,0:T(1,128)} %param.13) | copy-start | bytes 388
  261.3 41.7 %all-to-all-start.4 = ((f32[16,1,1024]{2,1,0:T(1,128)}), f32[16,1,1024]{2,1,0:T(1,128)S(1)}, u32[]{:S(2)}, u32[]{:S(2)}) async-start(f32[16,1,1024]{2,1,0:T(1,128)} %reshape.135), calls=%async_computation.4 | async-start | bytes 131072 | tf_op jit(solution)/shard_map/all_to_all | solution.py:19
Sparse Core Ops, SparseCore 0:
  111.0 134.4 all-gather.2

commit v9 on v7

--- a/solution.py
+++ b/solution.py
@@ -75,7 +75,7 @@
     residual_grad = (grad_in[0].astype(jnp.float32) + increment).astype(jnp.bfloat16)
     target_row = increment.astype(jnp.bfloat16)
     mine = lax.all_gather(target_row, PLANE, axis=0, tiled=False)
-    delta_piece, target_row = lax.optimization_barrier((head_delta[0], target_row))
+    delta_piece, column_blocks = lax.optimization_barrier((head_delta[0], column_blocks))
     delta_cols = gathered(delta_piece)
     core = lax.axis_index("core")
     theirs = lax.ppermute(mine, "core", [(0, 1), (1, 0)])

time: 324 us -> 334 us (1.031)
  starting transfers between devices: 51.2 us -> 35.2 us
  waiting for transfers between devices: 181 us -> 193 us
  blocking collectives: 35 us -> 46 us
    all_to_all x3 -> x4, starting transfers between devices: 42.6 us -> 26.2 us  [from_everyone(): lax.all_to_all(jnp.broadcast_to(array[None], (count, *array.shape)), axis...]
    all_to_all x3 -> x2, blocking collectives: 35 us -> 46 us  [from_everyone(): lax.all_to_all(jnp.broadcast_to(array[None], (count, *array.shape)), axis...]
    all_gather x1, waiting for transfers between devices: 116 us -> 126 us  [on_device(): mine = lax.all_gather(target_row, PLANE, axis=0, tiled=False)]
    all_to_all x1 -> x0, local copies, waits for them, and re-layouts: 6.46 us -> none  [on_device(): column_blocks = lax.all_to_all(blocks, TP, 0, 0, tiled=True)]
    optimization_barrier x0 -> x1, local copies, waits for them, and re-layouts: none -> 6.44 us  [on_device(): lax.optimization_barrier((head_delta[0], column_blocks))]
    all_to_all x3 -> x4, waiting for transfers between devices: 63.4 us -> 67.4 us  [from_everyone(): lax.all_to_all(jnp.broadcast_to(array[None], (count, *array.shape)), axis...]
  transfers between devices with their start and end apart: 6 -> 7, of which waited for: 4 -> 4; matrix products, arithmetic and copies ran while one was open for 7% -> 8% of each run, Pallas kernels for 0% -> 0%
where the time goes in v9:
time: 334 us; the launch traced here: 331 us
  waiting for transfers between devices  193 us (58%)
  blocking collectives  46 us (14%)
  starting transfers between devices  35.2 us (11%)
  local copies, waits for them, and re-layouts  28.7 us (9%)
  between operations  14.3 us (4%)
  matrix products  13.2 us (4%)
    all_gather x1, waiting for transfers between devices, on_device(): mine = lax.all_gather(target_row, PLANE, axis=0, tiled=False)  126 us
    all_to_all x4, waiting for transfers between devices, from_everyone(): lax.all_to_all(jnp.broadcast_to(array[None], (count, *array.shape)), axis...  67.4 us
    all_to_all x2, blocking collectives, from_everyone(): lax.all_to_all(jnp.broadcast_to(array[None], (count, *array.shape)), axis...  46 us
    all_to_all x4, starting transfers between devices, from_everyone(): lax.all_to_all(jnp.broadcast_to(array[None], (count, *array.shape)), axis...  26.2 us
    unnamed x17, local copies, waits for them, and re-layouts  9.24 us
  transfers between devices with their start and end apart: 7, of which 4 were waited for; matrix products, arithmetic and copies ran while one was open for 8% of the time, Pallas kernels for 0%

profile of v9, /device:TPU:1, one launch (start us, length us, event | category | flops | bytes accessed | tf_op | source)
XLA Modules:
  0.0 331.4 jit_solution(13969855021204799494)
XLA Ops:
  7.2 0.0 copy-start
  7.2 0.0 copy-start.5
  7.2 2.7 broadcast_in_dim.25
  9.9 9.0 %all-to-all-start = ((bf16[16,160,512]{2,1,0:T(8,128)(2,1)}), bf16[16,160,512]{2,1,0:T(8,128)(2,1)S(1)}, u32[]{:S(2)}, u32[]{:S(2)}) async-start(bf16[16,160,512]{2,1,0:T(8,128)(2,1)} %broadcast_in_dim.25), calls=%async_computation | async-start | bytes 5242880 | tf_op jit(solution)/shard_map/all_to_all | solution.py:20
  19.0 0.0 copy-done.5
  19.0 0.1 and_convert_fusion
  19.1 50.4 %all-to-all-done = bf16[16,160,512]{2,1,0:T(8,128)(2,1)S(1)} async-done(((bf16[16,160,512]{2,1,0:T(8,128)(2,1)}), bf16[16,160,512]{2,1,0:T(8,128)(2,1)S(1)}, u32[]{:S(2)}, u32[]{:S(2)}) %all-to-all-start) | async-done | bytes 2621472 | tf_op jit(solution)/shard_map/all_to_all | solution.py:20
  69.5 0.3 copy.62
  69.9 1.9 copy-done.1
  71.7 1.5 fusion.13
  73.3 0.0 copy-done.3
  73.3 0.2 fusion.12
  73.6 11.8 %all_to_all.35 = f32[4,160,128]{2,1,0:T(8,128)S(1)} all-to-all(f32[4,160,128]{2,1,0:T(8,128)S(1)} %broadcast_in_dim.26), channel_id=1, replica_groups=mesh['zh'=4,'y'=4,'core'=2,'zl'=4,'x'=4] {'x'}, dimensions={0} | all-to-all | bytes 655360 | tf_op jit(solution)/shard_map/all_to_all | solution.py:20
  85.4 0.7 broadcast_in_dim.27
  86.1 8.6 %all-to-all-start.2 = ((bf16[4,160,128]{2,1,0:T(8,128)(2,1)}), bf16[4,160,128]{2,1,0:T(8,128)(2,1)S(1)}, u32[]{:S(2)}, u32[]{:S(2)}) async-start(bf16[4,160,128]{2,1,0:T(8,128)(2,1)} %broadcast_in_dim.27), calls=%async_computation.2 | async-start | bytes 327680 | tf_op jit(solution)/shard_map/all_to_all | solution.py:20
  94.7 6.4 %copy.50 = bf16[1,256,8192]{1,2,0:T(8,128)(2,1)} copy(bf16[1,256,8192]{2,1,0:T(8,128)(2,1)} %param.8) | data formatting | bytes 8388608 | tf_op args[1]
  101.1 0.0 all-to-all-done.2
  101.1 5.6 %all-to-all-start.3 = ((bf16[16,256,512]{1,2,0:T(8,128)(2,1)}), bf16[16,256,512]{1,2,0:T(8,128)(2,1)}, u32[]{:S(2)}, u32[]{:S(2)}) async-start(bf16[16,256,512]{1,2,0:T(8,128)(2,1)} %bitcast.57), calls=%async_computation.3 | async-start | bytes 8388608 | tf_op jit(solution)/shard_map/all_to_all | solution.py:43
  106.7 0.0 copy-start.4
  106.7 0.0 all-gather.3.cloned.1.call-start
  106.7 0.0 copy-done
  106.7 0.0 copy-done.2
  106.7 1.0 fusion.38
  107.8 0.0 all-gather.3.cloned.1.call-update
  107.8 125.6 %all-gather.3.cloned.1.call-done = bf16[2560,512]{1,0:T(8,128)(2,1)} async-done(((bf16[160,512]{1,0:T(8,128)(2,1)}), bf16[2560,512]{1,0:T(8,128)(2,1)}) %all-gather.3.cloned.1.call-update) | async-done | bytes 2621456 | tf_op jit(solution)/shard_map/all_gather | solution.py:77
  233.4 4.8 %copy.56 = bf16[16,160,512]{2,0,1:T(8,128)(2,1)} copy(bf16[16,160,512]{2,1,0:T(8,128)(2,1)} %bitcast.61) | data formatting | bytes 5242880 | tf_op jit(solution)/shard_map/all_gather | solution.py:77
  238.1 3.4 %collective-permute-start = (bf16[16,160,512]{2,0,1:T(8,128)(2,1)}, bf16[16,160,512]{2,0,1:T(8,128)(2,1)}, u32[]{:S(2)}, u32[]{:S(2)}) collective-permute-start(bf16[16,160,512]{2,0,1:T(8,128)(2,1)} %copy.56), channel_id=1, source_target_pairs={{0,16},{16,0},{1,17},{17,1},{2,18},{18,2},{3,19},{19,3},{4,20},{20... | collective-permute-start | bytes 7864328 | tf_op jit(solution)/shard_map/ppermute | solution.py:81
  241.5 0.0 all-to-all-done.3
  241.6 34.2 %all_to_all.36 = bf16[4,160,256]{2,1,0:T(8,128)(2,1)S(1)} all-to-all(bf16[4,160,256]{2,1,0:T(8,128)(2,1)S(1)} %broadcast_in_dim.30), channel_id=1, replica_groups=mesh['zh'=4,'y'=4,'core'=2,'zl'=4,'x'=4] {'zl'}, dimensions={0} | all-to-all | bytes 655360 | tf_op jit(solution)/shard_map/all_to_all | solution.py:20
  275.8 0.3 copy.51
  276.1 1.4 broadcast_in_dim.31
  277.5 4.0 %all-to-all-start.5 = ((bf16[4,4,160,256]{3,1,2,0:T(4,128)(2,1)}), bf16[4,4,160,256]{3,1,2,0:T(4,128)(2,1)S(1)}, u32[]{:S(2)}, u32[]{:S(2)}) async-start(bf16[4,4,160,256]{3,1,2,0:T(4,128)(2,1)} %broadcast_in_dim.31), calls=%async_computation.5 | async-start | bytes 2621440 | tf_op jit(solution)/shard_map/all_to_all | solution.py:20
  281.5 6.4 %copy.53 = bf16[16,256,512]{2,1,0:T(8,128)(2,1)} copy(bf16[16,256,512]{1,2,0:T(8,128)(2,1)} %all-to-all-done.3) | data formatting | bytes 8388608 | tf_op jit(solution)/shard_map/optimization_barrier | solution.py:78
  287.9 9.8 %all-to-all-done.5 = bf16[4,4,160,256]{3,1,2,0:T(4,128)(2,1)S(1)} async-done(((bf16[4,4,160,256]{3,1,2,0:T(4,128)(2,1)}), bf16[4,4,160,256]{3,1,2,0:T(4,128)(2,1)S(1)}, u32[]{:S(2)}, u32[]{:S(2)}) %all-to-all-start.5) | async-done | bytes 1310752 | tf_op jit(solution)/shard_map/all_to_all | solution.py:20
  297.7 1.7 copy.52
  299.4 0.5 reshape_reshape.3
  299.9 3.7 %convolution_convert_fusion = bf16[32,160,512]{2,1,0:T(8,128)(2,1)S(1)} fusion(bf16[32,128,512]{2,1,0:T(8,128)(2,1)} %bitcast.58, bf16[160,32,128]{2,1,0:T(8,128)(2,1)S(1)} %reshape_reshape.3), kind=kOutput, calls=%fused_computation.7 | convolution fusion | flops 673710080 | bytes 10747904 | tf_op jit(solution)/shard_map/thc,hcd->htd/dot_general | solution.py:82
  303.6 0.0 copy-start.6
  303.7 0.0 collective-permute-done
  303.7 5.8 %fusion.16 = f32[32,32]{0,1:T(8,128)S(1)} fusion(bf16[16,160,512]{2,0,1:T(8,128)(2,1)} %collective-permute-done, bf16[16,160,512]{2,0,1:T(8,128)(2,1)} %copy.56, bf16[32,160,512]{2,1,0:T(8,128)(2,1)S(1)} %convolution_convert_fusion), kind=kOutput, calls=%fused_computation.15 | convolution fusion | flops 178257920 | bytes 10489856 | tf_op jit(solution)/shard_map/dot_general | solution.py:90
  309.5 0.1 copy.59
  309.6 0.8 reshape.133
  310.4 4.6 %all-to-all-start.6 = ((f32[16,1,1024]{2,1,0:T(1,128)}), f32[16,1,1024]{2,1,0:T(1,128)S(1)}, u32[]{:S(2)}, u32[]{:S(2)}) async-start(f32[16,1,1024]{2,1,0:T(1,128)} %reshape.133), calls=%async_computation.6 | async-start | bytes 131072 | tf_op jit(solution)/shard_map/all_to_all | solution.py:20
  315.0 7.2 %all-to-all-done.6 = f32[16,1,1024]{2,1,0:T(1,128)S(1)} async-done(((f32[16,1,1024]{2,1,0:T(1,128)}), f32[16,1,1024]{2,1,0:T(1,128)S(1)}, u32[]{:S(2)}, u32[]{:S(2)}) %all-to-all-start.6) | async-done | bytes 65568 | tf_op jit(solution)/shard_map/all_to_all | solution.py:20
  322.2 0.5 broadcast.112
  322.7 0.8 reduce.1
  323.5 0.1 reshape.134
  323.7 0.9 convolution_bitcast_fusion
  (16 shorter events, 0.2 us)
Async XLA Ops:
  7.2 99.6 %copy-start = (bf16[1,512,512]{2,1,0:T(8,128)(2,1)S(1)}, bf16[1,512,512]{2,1,0:T(8,128)(2,1)}, u32[]{:S(2)}) copy-start(bf16[1,512,512]{2,1,0:T(8,128)(2,1)} %param.9) | copy-start | bytes 1572868
  7.2 11.8 %copy-start.5 = (s32[160]{0:T(256)S(1)}, s32[160]{0:T(256)}, u32[]{:S(2)}) copy-start(s32[160]{0:T(256)} %param.12) | copy-start | bytes 1924
  9.9 59.6 %all-to-all-start = ((bf16[16,160,512]{2,1,0:T(8,128)(2,1)}), bf16[16,160,512]{2,1,0:T(8,128)(2,1)S(1)}, u32[]{:S(2)}, u32[]{:S(2)}) async-start(bf16[16,160,512]{2,1,0:T(8,128)(2,1)} %broadcast_in_dim.25), calls=%async_computation | async-start | bytes 5242880 | tf_op jit(solution)/shard_map/all_to_all | solution.py:20
  69.5 2.2 copy-start.1
  71.7 1.6 copy-start.3
  86.1 15.0 %all-to-all-start.2 = ((bf16[4,160,128]{2,1,0:T(8,128)(2,1)}), bf16[4,160,128]{2,1,0:T(8,128)(2,1)S(1)}, u32[]{:S(2)}, u32[]{:S(2)}) async-start(bf16[4,160,128]{2,1,0:T(8,128)(2,1)} %broadcast_in_dim.27), calls=%async_computation.2 | async-start | bytes 327680 | tf_op jit(solution)/shard_map/all_to_all | solution.py:20
  101.1 5.6 %copy-start.2 = (bf16[1,160,512]{2,1,0:T(8,128)(2,1)S(1)}, bf16[1,160,512]{2,1,0:T(8,128)(2,1)}, u32[]{:S(2)}) copy-start(bf16[1,160,512]{2,1,0:T(8,128)(2,1)} %param.7) | copy-start | bytes 491524
  101.1 140.4 %all-to-all-start.3 = ((bf16[16,256,512]{1,2,0:T(8,128)(2,1)}), bf16[16,256,512]{1,2,0:T(8,128)(2,1)}, u32[]{:S(2)}, u32[]{:S(2)}) async-start(bf16[16,256,512]{1,2,0:T(8,128)(2,1)} %bitcast.57), calls=%async_computation.3 | async-start | bytes 8388608 | tf_op jit(solution)/shard_map/all_to_all | solution.py:43
  106.7 134.9 %copy-start.4 = (bf16[1,160,256]{2,1,0:T(8,128)(2,1)S(1)}, bf16[1,160,256]{2,1,0:T(8,128)(2,1)}, u32[]{:S(2)}) copy-start(bf16[1,160,256]{2,1,0:T(8,128)(2,1)} %param.10) | copy-start | bytes 245764
  106.7 126.7 %all-gather.3.cloned.1.call-start = ((), (), s32[]{:S(2)}) async-start(), calls=%async_computation.7 | async-start | bytes 2785280 | tf_op jit(solution)/shard_map/all_gather | solution.py:77
  238.1 65.5 %collective-permute-start = (bf16[16,160,512]{2,0,1:T(8,128)(2,1)}, bf16[16,160,512]{2,0,1:T(8,128)(2,1)}, u32[]{:S(2)}, u32[]{:S(2)}) collective-permute-start(bf16[16,160,512]{2,0,1:T(8,128)(2,1)} %copy.56), channel_id=1, source_target_pairs={{0,16},{16,0},{1,17},{17,1},{2,18},{18,2},{3,19},{19,3},{4,20},{20... | collective-permute-start | bytes 7864328 | tf_op jit(solution)/shard_map/ppermute | solution.py:81
  277.5 20.2 %all-to-all-start.5 = ((bf16[4,4,160,256]{3,1,2,0:T(4,128)(2,1)}), bf16[4,4,160,256]{3,1,2,0:T(4,128)(2,1)S(1)}, u32[]{:S(2)}, u32[]{:S(2)}) async-start(bf16[4,4,160,256]{3,1,2,0:T(4,128)(2,1)} %broadcast_in_dim.31), calls=%async_computation.5 | async-start | bytes 2621440 | tf_op jit(solution)/shard_map/all_to_all | solution.py:20
  303.6 20.0 %copy-start.6 = (s32[1,32]{1,0:T(1,128)S(1)}, s32[1,32]{1,0:T(1,128)}, u32[]{:S(2)}) copy-start(s32[1,32]{1,0:T(1,128)} %param.13) | copy-start | bytes 388
  310.4 11.8 %all-to-all-start.6 = ((f32[16,1,1024]{2,1,0:T(1,128)}), f32[16,1,1024]{2,1,0:T(1,128)S(1)}, u32[]{:S(2)}, u32[]{:S(2)}) async-start(f32[16,1,1024]{2,1,0:T(1,128)} %reshape.133), calls=%async_computation.6 | async-start | bytes 131072 | tf_op jit(solution)/shard_map/all_to_all | solution.py:20
Sparse Core Ops, SparseCore 0:
  110.5 122.8 all-gather.2

commit v10 on v6

--- a/solution.py
+++ b/solution.py
@@ -39,7 +39,6 @@
         preferred_element_type=jnp.float32,
     ).astype(jnp.bfloat16)
     pieces = own_delta.reshape(own_heads, tokens, tp_count, local_width).transpose(2, 0, 1, 3)
-    delta = lax.all_to_all(pieces, TP, 0, 0, tiled=True)
 
     token_ids = jnp.arange(tokens)
     block_ids = token_ids // PROMPT
@@ -50,6 +49,7 @@
     )
     visible = allowed.astype(jnp.bfloat16)
     everyone = from_everyone(grad_in[0], TP)
+    pieces, everyone = lax.optimization_barrier((pieces, everyone))
     grad_rows = jnp.moveaxis(everyone, 0, 1).reshape(tokens, width)
     head_grad = lax.dot_general(
         grad_rows,
@@ -74,6 +74,7 @@
     residual_grad = (grad_in[0].astype(jnp.float32) + increment).astype(jnp.bfloat16)
     target_row = increment.astype(jnp.bfloat16)
     mine = lax.all_gather(target_row, PLANE, axis=0, tiled=False)
+    delta = lax.all_to_all(pieces, TP, 0, 0, tiled=True)
     core = lax.axis_index("core")
     theirs = lax.ppermute(mine, "core", [(0, 1), (1, 0)])
     all_heads = delta.reshape(HEADS, tokens, local_width)

time: 314 us -> 309 us (0.984)
  blocking collectives: 11.8 us -> 25.8 us
  starting transfers between devices: 63.7 us -> 53.5 us
  waiting for transfers between devices: 192 us -> 185 us
    all_to_all x1 -> x2, blocking collectives: 11.8 us -> 25.8 us  [from_everyone(): lax.all_to_all(jnp.broadcast_to(array[None], (count, *array.shape)), axis...]
    all_to_all x3 -> x2, starting transfers between devices: 54.8 us -> 45.9 us  [from_everyone(): lax.all_to_all(jnp.broadcast_to(array[None], (count, *array.shape)), axis...]
    all_to_all x3 -> x2, waiting for transfers between devices: 57.7 us -> 50.9 us  [from_everyone(): lax.all_to_all(jnp.broadcast_to(array[None], (count, *array.shape)), axis...]
    all_gather x1, waiting for transfers between devices: 130 us -> 126 us  [on_device(): mine = lax.all_gather(target_row, PLANE, axis=0, tiled=False)]
    all_to_all x1, waiting for transfers between devices: 0.01 us -> 3.5 us  [on_device(): delta = lax.all_to_all(pieces, TP, 0, 0, tiled=True)]
  transfers between devices with their start and end apart: 6 -> 5, of which waited for: 4 -> 5; matrix products, arithmetic and copies ran while one was open for 4% -> 4% of each run, Pallas kernels for 0% -> 0%
where the time goes in v10:
time: 309 us
  waiting for transfers between devices  185 us (60%)
  starting transfers between devices  53.5 us (17%)
  blocking collectives  25.8 us (8%)
  matrix products  16.8 us (5%)
  between operations  14.3 us (5%)
  local copies, waits for them, and re-layouts  12.7 us (4%)
    all_gather x1, waiting for transfers between devices, on_device(): mine = lax.all_gather(target_row, PLANE, axis=0, tiled=False)  126 us
    all_to_all x2, waiting for transfers between devices, from_everyone(): lax.all_to_all(jnp.broadcast_to(array[None], (count, *array.shape)), axis...  50.9 us
    all_to_all x2, starting transfers between devices, from_everyone(): lax.all_to_all(jnp.broadcast_to(array[None], (count, *array.shape)), axis...  45.9 us
    all_to_all x2, blocking collectives, from_everyone(): lax.all_to_all(jnp.broadcast_to(array[None], (count, *array.shape)), axis...  25.8 us
    dot_general x1, matrix products, on_device(): lax.dot_general(all_heads, both, contract, preferred_element_type=jnp.flo...  9.4 us
  transfers between devices with their start and end apart: 5, of which 5 were waited for; matrix products, arithmetic and copies ran while one was open for 4% of the time, Pallas kernels for 0%

profile of v10, /device:TPU:1, one launch (start us, length us, event | category | flops | bytes accessed | tf_op | source)
XLA Modules:
  0.0 308.8 jit_solution(10530833592566752014)
XLA Ops:
  7.2 0.0 copy-start
  7.2 0.0 copy-start.4
  7.2 2.7 broadcast_in_dim.21
  9.9 9.0 %all-to-all-start = ((bf16[16,160,512]{2,1,0:T(8,128)(2,1)}), bf16[16,160,512]{2,1,0:T(8,128)(2,1)S(1)}, u32[]{:S(2)}, u32[]{:S(2)}) async-start(bf16[16,160,512]{2,1,0:T(8,128)(2,1)} %broadcast_in_dim.21), calls=%async_computation | async-start | bytes 5242880 | tf_op jit(solution)/shard_map/all_to_all | solution.py:20
  18.9 0.0 copy-done.4
  19.0 3.7 %convolution_convert_fusion = bf16[2,160,8192]{2,1,0:T(8,128)(2,1)S(1)} fusion(bf16[2,128,8192]{2,1,0:T(8,128)(2,1)} %bitcast.63, bf16[160,2,128]{2,1,0:T(2,128)(2,1)S(1)} %reshape_squeeze.6), kind=kOutput, calls=%fused_computation | convolution fusion | flops 673710080 | bytes 9519104 | tf_op jit(solution)/shard_map/thc,hcd->htd/dot_general | solution.py:35
  22.7 0.0 copy-start.5
  22.7 3.0 copy.70
  25.7 0.0 copy-done.5
  25.7 0.1 and_convert_fusion
  25.8 43.7 %all-to-all-done = bf16[16,160,512]{2,1,0:T(8,128)(2,1)S(1)} async-done(((bf16[16,160,512]{2,1,0:T(8,128)(2,1)}), bf16[16,160,512]{2,1,0:T(8,128)(2,1)S(1)}, u32[]{:S(2)}, u32[]{:S(2)}) %all-to-all-start) | async-done | bytes 2621472 | tf_op jit(solution)/shard_map/all_to_all | solution.py:20
  69.5 0.0 copy-start.1
  69.5 0.3 copy.51
  69.8 1.9 copy-done.1
  71.7 0.0 copy-start.3
  71.7 1.5 fusion.12
  73.3 0.0 copy-done.3
  73.3 0.2 fusion.11
  73.6 11.8 %all_to_all.25 = f32[4,160,128]{2,1,0:T(8,128)S(1)} all-to-all(f32[4,160,128]{2,1,0:T(8,128)S(1)} %broadcast_in_dim.22), channel_id=1, replica_groups=mesh['zh'=4,'y'=4,'core'=2,'zl'=4,'x'=4] {'x'}, dimensions={0} | all-to-all | bytes 655360 | tf_op jit(solution)/shard_map/all_to_all | solution.py:20
  85.4 13.9 %all_to_all.26 = bf16[4,160,128]{2,1,0:T(8,128)(2,1)S(1)} all-to-all(bf16[4,160,128]{2,1,0:T(8,128)(2,1)S(1)} %broadcast_in_dim.23), channel_id=1, replica_groups=mesh['zh'=4,'y'=4,'core'=2,'zl'=4,'x'=4] {'zl'}, dimensions={0} | all-to-all | bytes 327680 | tf_op jit(solution)/shard_map/all_to_all | solution.py:20
  99.4 0.0 copy-start.2
  99.4 4.7 %all-to-all-start.3 = ((bf16[16,2,160,512]{3,2,1,0:T(8,128)(2,1)}), bf16[16,2,160,512]{3,2,1,0:T(8,128)(2,1)}, u32[]{:S(2)}, u32[]{:S(2)}) async-start(bf16[16,2,160,512]{3,2,1,0:T(8,128)(2,1)} %bitcast.60), calls=%async_computation.3 | async-start | bytes 10485760 | tf_op jit(solution)/shard_map/all_to_all | solution.py:77
  104.1 0.0 all-gather.3.cloned.1.call-start
  104.2 0.0 copy-done
  104.2 0.0 copy-done.2
  104.2 1.0 fusion.38
  105.2 0.0 all-gather.3.cloned.1.call-update
  105.2 125.9 %all-gather.3.cloned.1.call-done = bf16[2560,512]{1,0:T(8,128)(2,1)} async-done(((bf16[160,512]{1,0:T(8,128)(2,1)}), bf16[2560,512]{1,0:T(8,128)(2,1)}) %all-gather.3.cloned.1.call-update) | async-done | bytes 2621456 | tf_op jit(solution)/shard_map/all_gather | solution.py:76
  231.1 3.2 %copy.44 = bf16[16,160,512]{2,0,1:T(8,128)(2,1)S(1)} copy(bf16[16,160,512]{2,1,0:T(8,128)(2,1)} %bitcast.64) | data formatting | bytes 5242880 | tf_op jit(solution)/shard_map/all_gather | solution.py:76
  234.3 2.8 collective-permute-start
  237.2 4.5 %collective-permute-done = bf16[16,160,512]{2,0,1:T(8,128)(2,1)} collective-permute-done((bf16[16,160,512]{2,0,1:T(8,128)(2,1)S(1)}, bf16[16,160,512]{2,0,1:T(8,128)(2,1)}, u32[]{:S(2)}, u32[]{:S(2)}) %collective-permute-start) | collective-permute-done | bytes 2621472 | tf_op jit(solution)/shard_map/ppermute | solution.py:79
  241.6 3.5 %all-to-all-done.3 = bf16[16,2,160,512]{3,2,1,0:T(8,128)(2,1)} async-done(((bf16[16,2,160,512]{3,2,1,0:T(8,128)(2,1)}), bf16[16,2,160,512]{3,2,1,0:T(8,128)(2,1)}, u32[]{:S(2)}, u32[]{:S(2)}) %all-to-all-start.3) | async-done | bytes 5242912 | tf_op jit(solution)/shard_map/all_to_all | solution.py:77
  245.1 0.0 copy-start.6
  245.1 9.4 %fusion.15 = f32[32,32]{0,1:T(8,128)S(1)} fusion(bf16[16,160,512]{2,0,1:T(8,128)(2,1)} %collective-permute-done, bf16[16,160,512]{2,0,1:T(8,128)(2,1)S(1)} %copy.44, bf16[32,160,512]{2,1,0:T(8,128)(2,1)} %bitcast.11), kind=kOutput, calls=%fused_computation.15 | convolution fusion | flops 178257920 | bytes 10489856 | tf_op jit(solution)/shard_map/dot_general | solution.py:83
  254.6 0.1 copy.46
  254.7 0.8 reshape.135
  255.4 36.9 %all-to-all-start.4 = ((f32[16,1,1024]{2,1,0:T(1,128)}), f32[16,1,1024]{2,1,0:T(1,128)S(1)}, u32[]{:S(2)}, u32[]{:S(2)}) async-start(f32[16,1,1024]{2,1,0:T(1,128)} %reshape.135), calls=%async_computation.4 | async-start | bytes 131072 | tf_op jit(solution)/shard_map/all_to_all | solution.py:20
  292.4 7.2 %all-to-all-done.4 = f32[16,1,1024]{2,1,0:T(1,128)S(1)} async-done(((f32[16,1,1024]{2,1,0:T(1,128)}), f32[16,1,1024]{2,1,0:T(1,128)S(1)}, u32[]{:S(2)}, u32[]{:S(2)}) %all-to-all-start.4) | async-done | bytes 65568 | tf_op jit(solution)/shard_map/all_to_all | solution.py:20
  299.6 0.5 broadcast.110
  300.1 0.8 reduce.1
  300.9 0.1 reshape.136
  301.1 0.0 copy-done.6
  301.1 0.9 convolution_bitcast_fusion
  (12 shorter events, 0.2 us)
Async XLA Ops:
  7.2 97.0 %copy-start = (bf16[1,512,512]{2,1,0:T(8,128)(2,1)S(1)}, bf16[1,512,512]{2,1,0:T(8,128)(2,1)}, u32[]{:S(2)}) copy-start(bf16[1,512,512]{2,1,0:T(8,128)(2,1)} %param.9) | copy-start | bytes 1572868
  7.2 11.8 %copy-start.4 = (bf16[1,160,256]{2,1,0:T(8,128)(2,1)S(1)}, bf16[1,160,256]{2,1,0:T(8,128)(2,1)}, u32[]{:S(2)}) copy-start(bf16[1,160,256]{2,1,0:T(8,128)(2,1)} %param.10) | copy-start | bytes 245764
  9.9 59.6 %all-to-all-start = ((bf16[16,160,512]{2,1,0:T(8,128)(2,1)}), bf16[16,160,512]{2,1,0:T(8,128)(2,1)S(1)}, u32[]{:S(2)}, u32[]{:S(2)}) async-start(bf16[16,160,512]{2,1,0:T(8,128)(2,1)} %broadcast_in_dim.21), calls=%async_computation | async-start | bytes 5242880 | tf_op jit(solution)/shard_map/all_to_all | solution.py:20
  22.7 3.0 copy-start.5
  69.5 2.2 copy-start.1
  71.7 1.6 copy-start.3
  99.4 4.8 %copy-start.2 = (bf16[1,160,512]{2,1,0:T(8,128)(2,1)S(1)}, bf16[1,160,512]{2,1,0:T(8,128)(2,1)}, u32[]{:S(2)}) copy-start(bf16[1,160,512]{2,1,0:T(8,128)(2,1)} %param.7) | copy-start | bytes 491524
  99.4 145.7 %all-to-all-start.3 = ((bf16[16,2,160,512]{3,2,1,0:T(8,128)(2,1)}), bf16[16,2,160,512]{3,2,1,0:T(8,128)(2,1)}, u32[]{:S(2)}, u32[]{:S(2)}) async-start(bf16[16,2,160,512]{3,2,1,0:T(8,128)(2,1)} %bitcast.60), calls=%async_computation.3 | async-start | bytes 10485760 | tf_op jit(solution)/shard_map/all_to_all | solution.py:77
  104.1 127.0 %all-gather.3.cloned.1.call-start = ((), (), s32[]{:S(2)}) async-start(), calls=%async_computation.5 | async-start | bytes 2785280 | tf_op jit(solution)/shard_map/all_gather | solution.py:76
  234.3 7.3 %collective-permute-start = (bf16[16,160,512]{2,0,1:T(8,128)(2,1)S(1)}, bf16[16,160,512]{2,0,1:T(8,128)(2,1)}, u32[]{:S(2)}, u32[]{:S(2)}) collective-permute-start(bf16[16,160,512]{2,0,1:T(8,128)(2,1)S(1)} %copy.44), channel_id=1, source_target_pairs={{0,16},{16,0},{1,17},{17,1},{2,18},{18,2},{3,19},{19,3},{4,20},{20... | collective-permute-start | bytes 7864328 | tf_op jit(solution)/shard_map/ppermute | solution.py:79
  245.1 56.0 %copy-start.6 = (s32[1,32]{1,0:T(1,128)S(1)}, s32[1,32]{1,0:T(1,128)}, u32[]{:S(2)}) copy-start(s32[1,32]{1,0:T(1,128)} %param.13) | copy-start | bytes 388
  255.4 44.2 %all-to-all-start.4 = ((f32[16,1,1024]{2,1,0:T(1,128)}), f32[16,1,1024]{2,1,0:T(1,128)S(1)}, u32[]{:S(2)}, u32[]{:S(2)}) async-start(f32[16,1,1024]{2,1,0:T(1,128)} %reshape.135), calls=%async_computation.4 | async-start | bytes 131072 | tf_op jit(solution)/shard_map/all_to_all | solution.py:20
Sparse Core Ops, SparseCore 0:
  108.0 123.1 all-gather.2

commit v11 on v10

--- a/solution.py
+++ b/solution.py
@@ -48,9 +48,10 @@
         & (positions[None, :] <= positions[:, None])
     )
     visible = allowed.astype(jnp.bfloat16)
-    everyone = from_everyone(grad_in[0], TP)
-    pieces, everyone = lax.optimization_barrier((pieces, everyone))
-    grad_rows = jnp.moveaxis(everyone, 0, 1).reshape(tokens, width)
+    column = from_everyone(grad_in[0], "zl")
+    pieces, column = lax.optimization_barrier((pieces, column))
+    row = from_everyone(column, "x")
+    grad_rows = jnp.transpose(row, (2, 1, 0, 3)).reshape(tokens, width)
     head_grad = lax.dot_general(
         grad_rows,
         weights,

time: 309 us -> 309 us (level)
  waiting for transfers between devices: 185 us -> 175 us
  local copies, waits for them, and re-layouts: 12.7 us -> 22.4 us
  blocking collectives: 25.8 us -> 16.2 us
  starting transfers between devices: 53.5 us -> 59.5 us
    all_to_all x2, blocking collectives: 25.8 us -> 16.2 us  [from_everyone(): lax.all_to_all(jnp.broadcast_to(array[None], (count, *array.shape)), axis...]
    all_to_all x2 -> x3, waiting for transfers between devices: 50.9 us -> 42.9 us  [from_everyone(): lax.all_to_all(jnp.broadcast_to(array[None], (count, *array.shape)), axis...]
    all_to_all x2 -> x3, starting transfers between devices: 45.9 us -> 52.1 us  [from_everyone(): lax.all_to_all(jnp.broadcast_to(array[None], (count, *array.shape)), axis...]
    transpose x0 -> x1, local copies, waits for them, and re-layouts: none -> 4.86 us  [on_device(): grad_rows = jnp.transpose(row, (2, 1, 0, 3)).reshape(tokens, width)]
    reshape x1, local copies, waits for them, and re-layouts: 0.3 us -> 4.26 us  [on_device(): grad_rows = jnp.transpose(row, (2, 1, 0, 3)).reshape(tokens, width)]
  transfers between devices with their start and end apart: 5 -> 6, of which waited for: 5 -> 6; matrix products, arithmetic and copies ran while one was open for 4% -> 4% of each run, Pallas kernels for 0% -> 0%
where the time goes in v11:
time: 309 us; the launch traced here: 308 us
  waiting for transfers between devices  175 us (57%)
  starting transfers between devices  59.5 us (19%)
  local copies, waits for them, and re-layouts  22.4 us (7%)
  matrix products  19 us (6%)
  blocking collectives  16.2 us (5%)
  between operations  14.2 us (5%)
    all_gather x1, waiting for transfers between devices, on_device(): mine = lax.all_gather(target_row, PLANE, axis=0, tiled=False)  128 us
    all_to_all x3, starting transfers between devices, from_everyone(): lax.all_to_all(jnp.broadcast_to(array[None], (count, *array.shape)), axis...  52.1 us
    all_to_all x3, waiting for transfers between devices, from_everyone(): lax.all_to_all(jnp.broadcast_to(array[None], (count, *array.shape)), axis...  42.9 us
    all_to_all x2, blocking collectives, from_everyone(): lax.all_to_all(jnp.broadcast_to(array[None], (count, *array.shape)), axis...  16.2 us
    dot_general x1, matrix products, on_device(): lax.dot_general(all_heads, both, contract, preferred_element_type=jnp.flo...  9.4 us
  transfers between devices with their start and end apart: 6, of which 6 were waited for; matrix products, arithmetic and copies ran while one was open for 4% of the time, Pallas kernels for 0%

profile of v11, /device:TPU:1, one launch (start us, length us, event | category | flops | bytes accessed | tf_op | source)
XLA Modules:
  0.0 307.9 jit_solution(14866060295771226259)
XLA Ops:
  7.2 0.0 copy-start
  7.2 1.9 broadcast_in_dim.23
  9.1 6.4 %all-to-all-start = ((bf16[4,160,512]{2,1,0:T(8,128)(2,1)}), bf16[4,160,512]{2,1,0:T(8,128)(2,1)S(1)}, u32[]{:S(2)}, u32[]{:S(2)}) async-start(bf16[4,160,512]{2,1,0:T(8,128)(2,1)} %broadcast_in_dim.23), calls=%async_computation | async-start | bytes 1310720 | tf_op jit(solution)/shard_map/all_to_all | solution.py:20
  15.5 0.9 reshape_squeeze.6
  16.4 3.7 %convolution_convert_fusion = bf16[2,160,8192]{2,1,0:T(8,128)(2,1)S(1)} fusion(bf16[2,128,8192]{2,1,0:T(8,128)(2,1)} %bitcast.61, bf16[160,2,128]{2,1,0:T(2,128)(2,1)S(1)} %reshape_squeeze.6), kind=kOutput, calls=%fused_computation | convolution fusion | flops 673710080 | bytes 9519104 | tf_op jit(solution)/shard_map/thc,hcd->htd/dot_general | solution.py:35
  20.1 3.0 copy.71
  23.1 5.5 %all-to-all-done = bf16[4,160,512]{2,1,0:T(8,128)(2,1)S(1)} async-done(((bf16[4,160,512]{2,1,0:T(8,128)(2,1)}), bf16[4,160,512]{2,1,0:T(8,128)(2,1)S(1)}, u32[]{:S(2)}, u32[]{:S(2)}) %all-to-all-start) | async-done | bytes 655392 | tf_op jit(solution)/shard_map/all_to_all | solution.py:20
  28.7 0.5 copy.39
  29.2 0.0 copy-start.3
  29.2 2.2 broadcast_in_dim.24
  31.4 7.7 %all-to-all-start.1 = ((bf16[4,4,160,512]{3,1,2,0:T(4,128)(2,1)}), bf16[4,4,160,512]{3,1,2,0:T(4,128)(2,1)S(1)}, u32[]{:S(2)}, u32[]{:S(2)}) async-start(bf16[4,4,160,512]{3,1,2,0:T(4,128)(2,1)} %broadcast_in_dim.24), calls=%async_computation.1 | async-start | bytes 5242880 | tf_op jit(solution)/shard_map/all_to_all | solution.py:20
  39.0 0.0 copy-done.3
  39.0 0.1 and_convert_fusion
  39.2 30.1 %all-to-all-done.1 = bf16[4,4,160,512]{3,1,2,0:T(4,128)(2,1)S(1)} async-done(((bf16[4,4,160,512]{3,1,2,0:T(4,128)(2,1)}), bf16[4,4,160,512]{3,1,2,0:T(4,128)(2,1)S(1)}, u32[]{:S(2)}, u32[]{:S(2)}) %all-to-all-start.1) | async-done | bytes 2621472 | tf_op jit(solution)/shard_map/all_to_all | solution.py:20
  69.3 4.9 %copy.40 = bf16[160,4,4,512]{3,2,1,0:T(4,128)(2,1)} copy(bf16[160,4,4,512]{3,1,0,2:T(4,128)(2,1)S(1)} %bitcast.60) | data formatting | bytes 5242880 | tf_op jit(solution)/shard_map/transpose | solution.py:54
  74.1 4.3 %reshape.130 = bf16[160,8192]{1,0:T(8,128)(2,1)S(1)} reshape(bf16[160,4,4,512]{3,2,1,0:T(4,128)(2,1)} %copy.40) | data formatting | bytes 5242880 | tf_op jit(solution)/shard_map/reshape | solution.py:54
  78.4 0.0 copy-start.2
  78.4 3.8 %fusion.12 = bf16[20,2,8,128]{3,2,1,0:T(8,128)(2,1)S(1)} fusion(bf16[160,8192]{1,0:T(8,128)(2,1)S(1)} %reshape.130, bf16[1,256,8192]{2,1,0:T(8,128)(2,1)} %param.8), kind=kOutput, calls=%fused_computation.13 | convolution fusion | flops 671129600 | bytes 6897664 | tf_op jit(solution)/shard_map/dot_general | solution.py:55
  82.2 0.0 copy-done.2
  82.2 0.2 fusion.11
  82.5 8.3 %all_to_all.30 = f32[4,160,128]{2,1,0:T(8,128)S(1)} all-to-all(f32[4,160,128]{2,1,0:T(8,128)S(1)} %broadcast_in_dim.25), channel_id=1, replica_groups=mesh['zh'=4,'y'=4,'core'=2,'zl'=4,'x'=4] {'x'}, dimensions={0} | all-to-all | bytes 655360 | tf_op jit(solution)/shard_map/all_to_all | solution.py:20
  90.8 7.9 %all_to_all.31 = bf16[4,160,128]{2,1,0:T(8,128)(2,1)S(1)} all-to-all(bf16[4,160,128]{2,1,0:T(8,128)(2,1)S(1)} %broadcast_in_dim.26), channel_id=1, replica_groups=mesh['zh'=4,'y'=4,'core'=2,'zl'=4,'x'=4] {'zl'}, dimensions={0} | all-to-all | bytes 327680 | tf_op jit(solution)/shard_map/all_to_all | solution.py:20
  98.7 0.0 copy-start.1
  98.7 4.7 %all-to-all-start.4 = ((bf16[16,2,160,512]{3,2,1,0:T(8,128)(2,1)}), bf16[16,2,160,512]{3,2,1,0:T(8,128)(2,1)}, u32[]{:S(2)}, u32[]{:S(2)}) async-start(bf16[16,2,160,512]{3,2,1,0:T(8,128)(2,1)} %bitcast.58), calls=%async_computation.4 | async-start | bytes 10485760 | tf_op jit(solution)/shard_map/all_to_all | solution.py:78
  103.4 0.0 all-gather.3.cloned.1.call-start
  103.5 0.0 copy-done
  103.5 0.0 copy-done.1
  103.5 1.0 fusion.38
  104.6 0.0 all-gather.3.cloned.1.call-update
  104.6 127.7 %all-gather.3.cloned.1.call-done = bf16[2560,512]{1,0:T(8,128)(2,1)} async-done(((bf16[160,512]{1,0:T(8,128)(2,1)}), bf16[2560,512]{1,0:T(8,128)(2,1)}) %all-gather.3.cloned.1.call-update) | async-done | bytes 2621456 | tf_op jit(solution)/shard_map/all_gather | solution.py:77
  232.3 3.2 %copy.46 = bf16[16,160,512]{2,0,1:T(8,128)(2,1)S(1)} copy(bf16[16,160,512]{2,1,0:T(8,128)(2,1)} %bitcast.62) | data formatting | bytes 5242880 | tf_op jit(solution)/shard_map/all_gather | solution.py:77
  235.5 2.7 collective-permute-start
  238.2 4.5 %collective-permute-done = bf16[16,160,512]{2,0,1:T(8,128)(2,1)} collective-permute-done((bf16[16,160,512]{2,0,1:T(8,128)(2,1)S(1)}, bf16[16,160,512]{2,0,1:T(8,128)(2,1)}, u32[]{:S(2)}, u32[]{:S(2)}) %collective-permute-start) | collective-permute-done | bytes 2621472 | tf_op jit(solution)/shard_map/ppermute | solution.py:80
  242.7 0.4 all-to-all-done.4
  243.1 0.0 copy-start.4
  243.1 9.4 %fusion.15 = f32[32,32]{0,1:T(8,128)S(1)} fusion(bf16[16,160,512]{2,0,1:T(8,128)(2,1)} %collective-permute-done, bf16[16,160,512]{2,0,1:T(8,128)(2,1)S(1)} %copy.46, bf16[32,160,512]{2,1,0:T(8,128)(2,1)} %bitcast.11), kind=kOutput, calls=%fused_computation.15 | convolution fusion | flops 178257920 | bytes 10489856 | tf_op jit(solution)/shard_map/dot_general | solution.py:84
  252.5 0.1 copy.48
  252.6 0.8 reshape.136
  253.4 38.0 %all-to-all-start.5 = ((f32[16,1,1024]{2,1,0:T(1,128)}), f32[16,1,1024]{2,1,0:T(1,128)S(1)}, u32[]{:S(2)}, u32[]{:S(2)}) async-start(f32[16,1,1024]{2,1,0:T(1,128)} %reshape.136), calls=%async_computation.5 | async-start | bytes 131072 | tf_op jit(solution)/shard_map/all_to_all | solution.py:20
  291.4 7.2 %all-to-all-done.5 = f32[16,1,1024]{2,1,0:T(1,128)S(1)} async-done(((f32[16,1,1024]{2,1,0:T(1,128)}), f32[16,1,1024]{2,1,0:T(1,128)S(1)}, u32[]{:S(2)}, u32[]{:S(2)}) %all-to-all-start.5) | async-done | bytes 65568 | tf_op jit(solution)/shard_map/all_to_all | solution.py:20
  298.7 0.5 broadcast.111
  299.2 0.8 reduce.1
  300.0 0.1 reshape.137
  300.1 0.0 copy-done.4
  300.1 0.9 convolution_bitcast_fusion
  (11 shorter events, 0.2 us)
Async XLA Ops:
  7.2 96.3 %copy-start = (bf16[1,512,512]{2,1,0:T(8,128)(2,1)S(1)}, bf16[1,512,512]{2,1,0:T(8,128)(2,1)}, u32[]{:S(2)}) copy-start(bf16[1,512,512]{2,1,0:T(8,128)(2,1)} %param.9) | copy-start | bytes 1572868
  9.1 19.6 %all-to-all-start = ((bf16[4,160,512]{2,1,0:T(8,128)(2,1)}), bf16[4,160,512]{2,1,0:T(8,128)(2,1)S(1)}, u32[]{:S(2)}, u32[]{:S(2)}) async-start(bf16[4,160,512]{2,1,0:T(8,128)(2,1)} %broadcast_in_dim.23), calls=%async_computation | async-start | bytes 1310720 | tf_op jit(solution)/shard_map/all_to_all | solution.py:20
  29.2 9.9 %copy-start.3 = (s32[160]{0:T(256)S(1)}, s32[160]{0:T(256)}, u32[]{:S(2)}) copy-start(s32[160]{0:T(256)} %param.12) | copy-start | bytes 1924
  31.4 37.9 %all-to-all-start.1 = ((bf16[4,4,160,512]{3,1,2,0:T(4,128)(2,1)}), bf16[4,4,160,512]{3,1,2,0:T(4,128)(2,1)S(1)}, u32[]{:S(2)}, u32[]{:S(2)}) async-start(bf16[4,4,160,512]{3,1,2,0:T(4,128)(2,1)} %broadcast_in_dim.24), calls=%async_computation.1 | async-start | bytes 5242880 | tf_op jit(solution)/shard_map/all_to_all | solution.py:20
  78.4 3.8 %copy-start.2 = (bf16[1,2,160,160]{3,2,1,0:T(8,128)(2,1)S(1)}, bf16[1,2,160,160]{3,2,1,0:T(8,128)(2,1)}, u32[]{:S(2)}) copy-start(bf16[1,2,160,160]{3,2,1,0:T(8,128)(2,1)} %param.11) | copy-start | bytes 307204
  98.7 4.8 %copy-start.1 = (bf16[1,160,512]{2,1,0:T(8,128)(2,1)S(1)}, bf16[1,160,512]{2,1,0:T(8,128)(2,1)}, u32[]{:S(2)}) copy-start(bf16[1,160,512]{2,1,0:T(8,128)(2,1)} %param.7) | copy-start | bytes 491524
  98.7 144.4 %all-to-all-start.4 = ((bf16[16,2,160,512]{3,2,1,0:T(8,128)(2,1)}), bf16[16,2,160,512]{3,2,1,0:T(8,128)(2,1)}, u32[]{:S(2)}, u32[]{:S(2)}) async-start(bf16[16,2,160,512]{3,2,1,0:T(8,128)(2,1)} %bitcast.58), calls=%async_computation.4 | async-start | bytes 10485760 | tf_op jit(solution)/shard_map/all_to_all | solution.py:78
  103.4 128.9 %all-gather.3.cloned.1.call-start = ((), (), s32[]{:S(2)}) async-start(), calls=%async_computation.6 | async-start | bytes 2785280 | tf_op jit(solution)/shard_map/all_gather | solution.py:77
  235.5 7.2 %collective-permute-start = (bf16[16,160,512]{2,0,1:T(8,128)(2,1)S(1)}, bf16[16,160,512]{2,0,1:T(8,128)(2,1)}, u32[]{:S(2)}, u32[]{:S(2)}) collective-permute-start(bf16[16,160,512]{2,0,1:T(8,128)(2,1)S(1)} %copy.46), channel_id=1, source_target_pairs={{0,16},{16,0},{1,17},{17,1},{2,18},{18,2},{3,19},{19,3},{4,20},{20... | collective-permute-start | bytes 7864328 | tf_op jit(solution)/shard_map/ppermute | solution.py:80
  243.1 57.1 %copy-start.4 = (s32[1,32]{1,0:T(1,128)S(1)}, s32[1,32]{1,0:T(1,128)}, u32[]{:S(2)}) copy-start(s32[1,32]{1,0:T(1,128)} %param.13) | copy-start | bytes 388
  253.4 45.2 %all-to-all-start.5 = ((f32[16,1,1024]{2,1,0:T(1,128)}), f32[16,1,1024]{2,1,0:T(1,128)S(1)}, u32[]{:S(2)}, u32[]{:S(2)}) async-start(f32[16,1,1024]{2,1,0:T(1,128)} %reshape.136), calls=%async_computation.5 | async-start | bytes 131072 | tf_op jit(solution)/shard_map/all_to_all | solution.py:20
Sparse Core Ops, SparseCore 0:
  107.3 124.9 all-gather.2

commit v12 on v9

--- a/solution.py
+++ b/solution.py
@@ -22,13 +22,6 @@
     )
 
 
-def gathered(piece):
-    column = from_everyone(piece, "zl")
-    row = from_everyone(column, "x")
-    tokens = piece.shape[0]
-    return jnp.transpose(row, (2, 1, 0, 3)).reshape(tokens, -1)
-
-
 def on_device(grad_in, out_proj, value_proj, head_delta, pattern, positions, node_map):
     tokens = grad_in.shape[1]
     local_width = grad_in.shape[2]
@@ -40,7 +33,6 @@
     weights = out_proj[0]
 
     blocks = weights.reshape(own_rows, tp_count, local_width).transpose(1, 0, 2)
-    column_blocks = lax.all_to_all(blocks, TP, 0, 0, tiled=True)
 
     token_ids = jnp.arange(tokens)
     block_ids = token_ids // PROMPT
@@ -50,8 +42,12 @@
         & (positions[None, :] <= positions[:, None])
     )
     visible = allowed.astype(jnp.bfloat16)
-    everyone = from_everyone(grad_in[0], TP)
-    grad_rows = jnp.moveaxis(everyone, 0, 1).reshape(tokens, width)
+    both_cols = jnp.concatenate([grad_in[0], head_delta[0]], axis=1)
+    column = from_everyone(both_cols, "zl")
+    blocks, column = lax.optimization_barrier((blocks, column))
+    row = jnp.transpose(from_everyone(column, "x"), (2, 1, 0, 3))
+    grad_rows = row[..., :local_width].reshape(tokens, width)
+    delta_cols = row[..., local_width:].reshape(tokens, HEADS * HEAD_DIM)
     head_grad = lax.dot_general(
         grad_rows,
         weights,
@@ -75,8 +71,7 @@
     residual_grad = (grad_in[0].astype(jnp.float32) + increment).astype(jnp.bfloat16)
     target_row = increment.astype(jnp.bfloat16)
     mine = lax.all_gather(target_row, PLANE, axis=0, tiled=False)
-    delta_piece, column_blocks = lax.optimization_barrier((head_delta[0], column_blocks))
-    delta_cols = gathered(delta_piece)
+    column_blocks = lax.all_to_all(blocks, TP, 0, 0, tiled=True)
     core = lax.axis_index("core")
     theirs = lax.ppermute(mine, "core", [(0, 1), (1, 0)])
     all_heads = jnp.einsum(

time: 334 us -> 325 us (0.973)
  blocking collectives: 46 us -> 16.2 us
  starting transfers between devices: 35.2 us -> 46.8 us
  local copies, waits for them, and re-layouts: 28.7 us -> 37.4 us
    all_to_all x2, blocking collectives: 46 us -> 16.2 us  [from_everyone(): lax.all_to_all(jnp.broadcast_to(array[None], (count, *array.shape)), axis...]
    all_to_all x4 -> x3, starting transfers between devices: 26.2 us -> 37.9 us  [from_everyone(): lax.all_to_all(jnp.broadcast_to(array[None], (count, *array.shape)), axis...]
    slice x0 -> x4, local copies, waits for them, and re-layouts: none -> 9.47 us  [the longest x2 6.01 us: on_device(): grad_rows = row[..., :local_width].reshape(tokens, width)]
    all_to_all x0 -> x1, local copies, waits for them, and re-layouts: none -> 6.4 us  [on_device(): column_blocks = lax.all_to_all(blocks, TP, 0, 0, tiled=True)]
    optimization_barrier x1, local copies, waits for them, and re-layouts: 6.44 us -> 0.76 us  [on_device(): blocks, column = lax.optimization_barrier((blocks, column))]
    unnamed x17 -> x13, local copies, waits for them, and re-layouts: 9.24 us -> 7.28 us
    all_to_all x4 -> x3, waiting for transfers between devices: 67.4 us -> 68.6 us  [from_everyone(): lax.all_to_all(jnp.broadcast_to(array[None], (count, *array.shape)), axis...]
  transfers between devices with their start and end apart: 7 -> 6, of which waited for: 4 -> 4; matrix products, arithmetic and copies ran while one was open for 8% -> 8% of each run, Pallas kernels for 0% -> 0%
where the time goes in v12:
time: 325 us; the launch traced here: 324 us
  waiting for transfers between devices  191 us (59%)
  starting transfers between devices  46.8 us (14%)
  local copies, waits for them, and re-layouts  37.4 us (12%)
  matrix products  16.2 us (5%)
  blocking collectives  16.2 us (5%)
  between operations  14.3 us (4%)
    all_gather x1, waiting for transfers between devices, on_device(): mine = lax.all_gather(target_row, PLANE, axis=0, tiled=False)  123 us
    all_to_all x3, waiting for transfers between devices, from_everyone(): lax.all_to_all(jnp.broadcast_to(array[None], (count, *array.shape)), axis...  68.6 us
    all_to_all x3, starting transfers between devices, from_everyone(): lax.all_to_all(jnp.broadcast_to(array[None], (count, *array.shape)), axis...  37.9 us
    all_to_all x2, blocking collectives, from_everyone(): lax.all_to_all(jnp.broadcast_to(array[None], (count, *array.shape)), axis...  16.2 us
    unnamed x13, local copies, waits for them, and re-layouts  7.28 us
  transfers between devices with their start and end apart: 6, of which 4 were waited for; matrix products, arithmetic and copies ran while one was open for 8% of the time, Pallas kernels for 0%

profile of v12, /device:TPU:1, one launch (start us, length us, event | category | flops | bytes accessed | tf_op | source)
XLA Modules:
  0.0 324.2 jit_solution(15112360596861654157)
XLA Ops:
  7.2 0.0 copy-start
  7.2 1.0 pad_maximum_fusion
  8.2 1.0 broadcast_in_dim.23
  9.2 6.4 %all-to-all-start = ((bf16[4,160,768]{2,1,0:T(8,128)(2,1)}), bf16[4,160,768]{2,1,0:T(8,128)(2,1)S(1)}, u32[]{:S(2)}, u32[]{:S(2)}) async-start(bf16[4,160,768]{2,1,0:T(8,128)(2,1)} %broadcast_in_dim.23), calls=%async_computation | async-start | bytes 1966080 | tf_op jit(solution)/shard_map/all_to_all | solution.py:20
  15.7 6.4 %copy.46 = bf16[1,256,8192]{1,2,0:T(8,128)(2,1)} copy(bf16[1,256,8192]{2,1,0:T(8,128)(2,1)} %param.8) | data formatting | bytes 8388608 | tf_op args[1]
  22.0 16.7 %all-to-all-done = bf16[4,160,768]{2,1,0:T(8,128)(2,1)S(1)} async-done(((bf16[4,160,768]{2,1,0:T(8,128)(2,1)}), bf16[4,160,768]{2,1,0:T(8,128)(2,1)S(1)}, u32[]{:S(2)}, u32[]{:S(2)}) %all-to-all-start) | async-done | bytes 983072 | tf_op jit(solution)/shard_map/all_to_all | solution.py:20
  38.7 0.8 copy.47
  39.5 2.9 broadcast_in_dim.24
  42.4 0.0 copy-start.3
  42.4 5.0 %all-to-all-start.1 = ((bf16[4,4,160,768]{3,1,2,0:T(4,128)(2,1)}), bf16[4,4,160,768]{3,1,2,0:T(4,128)(2,1)}, u32[]{:S(2)}, u32[]{:S(2)}) async-start(bf16[4,4,160,768]{3,1,2,0:T(4,128)(2,1)} %broadcast_in_dim.24), calls=%async_computation.1 | async-start | bytes 7864320 | tf_op jit(solution)/shard_map/all_to_all | solution.py:20
  47.4 0.0 copy-done.3
  47.4 0.1 and_convert_fusion
  47.6 44.6 %all-to-all-done.1 = bf16[4,4,160,768]{3,1,2,0:T(4,128)(2,1)} async-done(((bf16[4,4,160,768]{3,1,2,0:T(4,128)(2,1)}), bf16[4,4,160,768]{3,1,2,0:T(4,128)(2,1)}, u32[]{:S(2)}, u32[]{:S(2)}) %all-to-all-start.1) | async-done | bytes 3932192 | tf_op jit(solution)/shard_map/all_to_all | solution.py:20
  92.2 2.6 slice.18
  94.9 3.4 %copy.48 = bf16[160,4,4,512]{3,2,1,0:T(4,128)(2,1)S(1)} copy(bf16[160,4,4,512]{3,1,0,2:T(4,128)(2,1)S(1)} %slice.18) | data formatting | bytes 5242880 | tf_op jit(solution)/shard_map/slice | solution.py:49
  98.2 3.6 %reshape.127 = bf16[160,8192]{1,0:T(8,128)(2,1)} reshape(bf16[160,4,4,512]{3,2,1,0:T(4,128)(2,1)S(1)} %copy.48) | data formatting | bytes 5242880 | tf_op jit(solution)/shard_map/reshape | solution.py:49
  101.8 4.6 %fusion.13 = bf16[20,2,8,128]{3,2,1,0:T(8,128)(2,1)S(1)} fusion(bf16[160,8192]{1,0:T(8,128)(2,1)} %reshape.127, bf16[1,256,8192]{2,1,0:T(8,128)(2,1)} %param.8), kind=kOutput, calls=%fused_computation.13 | convolution fusion | flops 671129600 | bytes 6897664 | tf_op jit(solution)/shard_map/dot_general | solution.py:51
  106.4 0.0 copy-done.2
  106.4 0.2 fusion.12
  106.7 8.3 %all_to_all.30 = f32[4,160,128]{2,1,0:T(8,128)S(1)} all-to-all(f32[4,160,128]{2,1,0:T(8,128)S(1)} %broadcast_in_dim.25), channel_id=1, replica_groups=mesh['zh'=4,'y'=4,'core'=2,'zl'=4,'x'=4] {'x'}, dimensions={0} | all-to-all | bytes 655360 | tf_op jit(solution)/shard_map/all_to_all | solution.py:20
  115.0 7.9 %all_to_all.31 = bf16[4,160,128]{2,1,0:T(8,128)(2,1)S(1)} all-to-all(bf16[4,160,128]{2,1,0:T(8,128)(2,1)S(1)} %broadcast_in_dim.26), channel_id=1, replica_groups=mesh['zh'=4,'y'=4,'core'=2,'zl'=4,'x'=4] {'zl'}, dimensions={0} | all-to-all | bytes 327680 | tf_op jit(solution)/shard_map/all_to_all | solution.py:20
  122.9 4.7 %all-to-all-start.4 = ((bf16[16,256,512]{1,2,0:T(8,128)(2,1)}), bf16[16,256,512]{1,2,0:T(8,128)(2,1)}, u32[]{:S(2)}, u32[]{:S(2)}) async-start(bf16[16,256,512]{1,2,0:T(8,128)(2,1)} %bitcast.54), calls=%async_computation.4 | async-start | bytes 8388608 | tf_op jit(solution)/shard_map/all_to_all | solution.py:74
  127.6 0.0 all-gather.3.cloned.1.call-start
  127.7 0.0 copy-done
  127.7 0.0 copy-done.1
  127.7 1.0 fusion.38
  128.7 0.0 all-gather.3.cloned.1.call-update
  128.8 122.6 %all-gather.3.cloned.1.call-done = bf16[2560,512]{1,0:T(8,128)(2,1)} async-done(((bf16[160,512]{1,0:T(8,128)(2,1)}), bf16[2560,512]{1,0:T(8,128)(2,1)}) %all-gather.3.cloned.1.call-update) | async-done | bytes 2621456 | tf_op jit(solution)/shard_map/all_gather | solution.py:73
  251.4 4.7 %copy.56 = bf16[16,160,512]{2,0,1:T(8,128)(2,1)} copy(bf16[16,160,512]{2,1,0:T(8,128)(2,1)} %bitcast.56) | data formatting | bytes 5242880 | tf_op jit(solution)/shard_map/all_gather | solution.py:73
  256.1 4.2 %collective-permute-start = (bf16[16,160,512]{2,0,1:T(8,128)(2,1)}, bf16[16,160,512]{2,0,1:T(8,128)(2,1)}, u32[]{:S(2)}, u32[]{:S(2)}) collective-permute-start(bf16[16,160,512]{2,0,1:T(8,128)(2,1)} %copy.56), channel_id=1, source_target_pairs={{0,16},{16,0},{1,17},{17,1},{2,18},{18,2},{3,19},{19,3},{4,20},{20... | collective-permute-start | bytes 7864328 | tf_op jit(solution)/shard_map/ppermute | solution.py:76
  260.4 1.8 slice.19
  262.1 1.7 copy.52
  263.8 0.5 reshape_reshape.3
  264.4 0.0 all-to-all-done.4
  264.4 6.4 %copy.53 = bf16[16,256,512]{2,1,0:T(8,128)(2,1)} copy(bf16[16,256,512]{1,2,0:T(8,128)(2,1)} %all-to-all-done.4) | data formatting | bytes 8388608 | tf_op jit(solution)/shard_map/all_to_all | solution.py:74
  270.8 3.7 %convolution_convert_fusion = bf16[32,160,512]{2,1,0:T(8,128)(2,1)S(1)} fusion(bf16[32,128,512]{2,1,0:T(8,128)(2,1)} %bitcast.55, bf16[160,32,128]{2,1,0:T(8,128)(2,1)S(1)} %reshape_reshape.3), kind=kOutput, calls=%fused_computation.7 | convolution fusion | flops 673710080 | bytes 10747904 | tf_op jit(solution)/shard_map/thc,hcd->htd/dot_general | solution.py:77
  274.5 0.0 copy-start.4
  274.5 0.0 collective-permute-done
  274.5 5.8 %fusion.16 = f32[32,32]{0,1:T(8,128)S(1)} fusion(bf16[16,160,512]{2,0,1:T(8,128)(2,1)} %collective-permute-done, bf16[16,160,512]{2,0,1:T(8,128)(2,1)} %copy.56, bf16[32,160,512]{2,1,0:T(8,128)(2,1)S(1)} %convolution_convert_fusion), kind=kOutput, calls=%fused_computation.15 | convolution fusion | flops 178257920 | bytes 10489856 | tf_op jit(solution)/shard_map/dot_general | solution.py:85
  280.3 0.1 copy.59
  280.4 0.8 reshape.133
  281.2 26.5 %all-to-all-start.5 = ((f32[16,1,1024]{2,1,0:T(1,128)}), f32[16,1,1024]{2,1,0:T(1,128)S(1)}, u32[]{:S(2)}, u32[]{:S(2)}) async-start(f32[16,1,1024]{2,1,0:T(1,128)} %reshape.133), calls=%async_computation.5 | async-start | bytes 131072 | tf_op jit(solution)/shard_map/all_to_all | solution.py:20
  307.7 7.2 %all-to-all-done.5 = f32[16,1,1024]{2,1,0:T(1,128)S(1)} async-done(((f32[16,1,1024]{2,1,0:T(1,128)}), f32[16,1,1024]{2,1,0:T(1,128)S(1)}, u32[]{:S(2)}, u32[]{:S(2)}) %all-to-all-start.5) | async-done | bytes 65568 | tf_op jit(solution)/shard_map/all_to_all | solution.py:20
  315.0 0.5 broadcast.112
  315.5 0.8 reduce.1
  316.3 0.1 reshape.134
  316.4 0.0 copy-done.4
  316.4 0.9 convolution_bitcast_fusion
  (13 shorter events, 0.2 us)
Async XLA Ops:
  7.2 120.5 %copy-start = (bf16[1,512,512]{2,1,0:T(8,128)(2,1)S(1)}, bf16[1,512,512]{2,1,0:T(8,128)(2,1)}, u32[]{:S(2)}) copy-start(bf16[1,512,512]{2,1,0:T(8,128)(2,1)} %param.9) | copy-start | bytes 1572868
  9.2 29.5 %all-to-all-start = ((bf16[4,160,768]{2,1,0:T(8,128)(2,1)}), bf16[4,160,768]{2,1,0:T(8,128)(2,1)S(1)}, u32[]{:S(2)}, u32[]{:S(2)}) async-start(bf16[4,160,768]{2,1,0:T(8,128)(2,1)} %broadcast_in_dim.23), calls=%async_computation | async-start | bytes 1966080 | tf_op jit(solution)/shard_map/all_to_all | solution.py:20
  42.4 5.0 %copy-start.3 = (s32[160]{0:T(256)S(1)}, s32[160]{0:T(256)}, u32[]{:S(2)}) copy-start(s32[160]{0:T(256)} %param.12) | copy-start | bytes 1924
  42.4 49.8 %all-to-all-start.1 = ((bf16[4,4,160,768]{3,1,2,0:T(4,128)(2,1)}), bf16[4,4,160,768]{3,1,2,0:T(4,128)(2,1)}, u32[]{:S(2)}, u32[]{:S(2)}) async-start(bf16[4,4,160,768]{3,1,2,0:T(4,128)(2,1)} %broadcast_in_dim.24), calls=%async_computation.1 | async-start | bytes 7864320 | tf_op jit(solution)/shard_map/all_to_all | solution.py:20
  101.8 4.6 %copy-start.2 = (bf16[1,2,160,160]{3,2,1,0:T(8,128)(2,1)S(1)}, bf16[1,2,160,160]{3,2,1,0:T(8,128)(2,1)}, u32[]{:S(2)}) copy-start(bf16[1,2,160,160]{3,2,1,0:T(8,128)(2,1)} %param.11) | copy-start | bytes 307204
  122.9 4.7 %copy-start.1 = (bf16[1,160,512]{2,1,0:T(8,128)(2,1)S(1)}, bf16[1,160,512]{2,1,0:T(8,128)(2,1)}, u32[]{:S(2)}) copy-start(bf16[1,160,512]{2,1,0:T(8,128)(2,1)} %param.7) | copy-start | bytes 491524
  122.9 141.4 %all-to-all-start.4 = ((bf16[16,256,512]{1,2,0:T(8,128)(2,1)}), bf16[16,256,512]{1,2,0:T(8,128)(2,1)}, u32[]{:S(2)}, u32[]{:S(2)}) async-start(bf16[16,256,512]{1,2,0:T(8,128)(2,1)} %bitcast.54), calls=%async_computation.4 | async-start | bytes 8388608 | tf_op jit(solution)/shard_map/all_to_all | solution.py:74
  127.6 123.8 %all-gather.3.cloned.1.call-start = ((), (), s32[]{:S(2)}) async-start(), calls=%async_computation.6 | async-start | bytes 2785280 | tf_op jit(solution)/shard_map/all_gather | solution.py:73
  256.1 18.4 %collective-permute-start = (bf16[16,160,512]{2,0,1:T(8,128)(2,1)}, bf16[16,160,512]{2,0,1:T(8,128)(2,1)}, u32[]{:S(2)}, u32[]{:S(2)}) collective-permute-start(bf16[16,160,512]{2,0,1:T(8,128)(2,1)} %copy.56), channel_id=1, source_target_pairs={{0,16},{16,0},{1,17},{17,1},{2,18},{18,2},{3,19},{19,3},{4,20},{20... | collective-permute-start | bytes 7864328 | tf_op jit(solution)/shard_map/ppermute | solution.py:76
  274.5 42.0 %copy-start.4 = (s32[1,32]{1,0:T(1,128)S(1)}, s32[1,32]{1,0:T(1,128)}, u32[]{:S(2)}) copy-start(s32[1,32]{1,0:T(1,128)} %param.13) | copy-start | bytes 388
  281.2 33.7 %all-to-all-start.5 = ((f32[16,1,1024]{2,1,0:T(1,128)}), f32[16,1,1024]{2,1,0:T(1,128)S(1)}, u32[]{:S(2)}, u32[]{:S(2)}) async-start(f32[16,1,1024]{2,1,0:T(1,128)} %reshape.133), calls=%async_computation.5 | async-start | bytes 131072 | tf_op jit(solution)/shard_map/all_to_all | solution.py:20
Sparse Core Ops, SparseCore 0:
  131.5 119.8 all-gather.2

commit v13 on v8

--- a/solution.py
+++ b/solution.py
@@ -38,7 +38,6 @@
         preferred_element_type=jnp.float32,
     ).astype(jnp.bfloat16)
     pieces = own_delta.reshape(own_heads, tokens, tp_count, local_width).transpose(2, 0, 1, 3)
-    delta = lax.all_to_all(pieces, TP, 0, 0, tiled=True)
 
     token_ids = jnp.arange(tokens)
     block_ids = token_ids // PROMPT
@@ -48,8 +47,10 @@
         & (positions[None, :] <= positions[:, None])
     )
     visible = allowed.astype(jnp.bfloat16)
-    everyone = from_everyone(grad_in[0], TP)
-    grad_rows = jnp.moveaxis(everyone, 0, 1).reshape(tokens, width)
+    column = from_everyone(grad_in[0], "zl")
+    pieces, column = lax.optimization_barrier((pieces, column))
+    row = from_everyone(column, "x")
+    grad_rows = jnp.transpose(row, (2, 1, 0, 3)).reshape(tokens, width)
     head_grad = lax.dot_general(
         grad_rows,
         weights,
@@ -73,11 +74,12 @@
     residual_grad = (grad_in[0].astype(jnp.float32) + increment).astype(jnp.bfloat16)
     target_row = increment.astype(jnp.bfloat16)
     target_rows = lax.all_gather(target_row, SECTION, axis=0, tiled=False)
+    delta = lax.all_to_all(pieces, TP, 0, 0, tiled=True)
     all_heads = delta.reshape(HEADS, tokens, local_width)
     contract = (((1, 2), (1, 2)), ((), ()))
     partial_scores = lax.dot_general(
-        all_heads, target_rows, contract, preferred_element_type=jnp.float32
-    )
+        target_rows, all_heads, contract, preferred_element_type=jnp.float32
+    ).T
     totals = from_everyone(partial_scores, TP).sum(axis=0)
     later = jnp.arange(section_count) > lax.axis_index(SECTION)
     raw_scores = jnp.where(later[None, :], totals / tokens, jnp.zeros_like(totals))

time: 314 us -> 310 us (0.987)
  waiting for transfers between devices: 195 us -> 179 us
  local copies, waits for them, and re-layouts: 10.2 us -> 19.1 us
  blocking collectives: 11.8 us -> 16.2 us
  starting transfers between devices: 57.7 us -> 54.1 us
    all_to_all x1, waiting for transfers between devices: 130 us -> 7.94 us  [on_device(): delta = lax.all_to_all(pieces, TP, 0, 0, tiled=True)]
    all_gather x1, waiting for transfers between devices: 7.55 us -> 128 us  [on_device(): target_rows = lax.all_gather(target_row, SECTION, axis=0, tiled=False)]
    all_to_all x3, waiting for transfers between devices: 57.8 us -> 42.9 us  [from_everyone(): lax.all_to_all(jnp.broadcast_to(array[None], (count, *array.shape)), axis...]
    transpose x0 -> x1, local copies, waits for them, and re-layouts: none -> 4.87 us  [on_device(): grad_rows = jnp.transpose(row, (2, 1, 0, 3)).reshape(tokens, width)]
    all_to_all x1 -> x2, blocking collectives: 11.8 us -> 16.2 us  [from_everyone(): lax.all_to_all(jnp.broadcast_to(array[None], (count, *array.shape)), axis...]
    reshape x1, local copies, waits for them, and re-layouts: 0.26 us -> 4.26 us  [on_device(): grad_rows = jnp.transpose(row, (2, 1, 0, 3)).reshape(tokens, width)]
  transfers between devices with their start and end apart: 5 -> 5, of which waited for: 4 -> 5; matrix products, arithmetic and copies ran while one was open for 3% -> 3% of each run, Pallas kernels for 0% -> 0%
where the time goes in v13:
time: 310 us; the launch traced here: 308 us
  waiting for transfers between devices  179 us (58%)
  starting transfers between devices  54.1 us (17%)
  matrix products  24.6 us (8%)
  local copies, waits for them, and re-layouts  19.1 us (6%)
  blocking collectives  16.2 us (5%)
  between operations  14.2 us (5%)
    all_gather x1, waiting for transfers between devices, on_device(): target_rows = lax.all_gather(target_row, SECTION, axis=0, tiled=False)  128 us
    all_to_all x3, starting transfers between devices, from_everyone(): lax.all_to_all(jnp.broadcast_to(array[None], (count, *array.shape)), axis...  49.2 us
    all_to_all x3, waiting for transfers between devices, from_everyone(): lax.all_to_all(jnp.broadcast_to(array[None], (count, *array.shape)), axis...  42.9 us
    all_to_all x2, blocking collectives, from_everyone(): lax.all_to_all(jnp.broadcast_to(array[None], (count, *array.shape)), axis...  16.2 us
    dot_general x1, matrix products, on_device(): lax.dot_general(target_rows, all_heads, contract, preferred_element_type=...  15 us
    all_to_all x1, waiting for transfers between devices, on_device(): delta = lax.all_to_all(pieces, TP, 0, 0, tiled=True)  7.94 us
  transfers between devices with their start and end apart: 5, of which 5 were waited for; matrix products, arithmetic and copies ran while one was open for 3% of the time, Pallas kernels for 0%

profile of v13, /device:TPU:1, one launch (start us, length us, event | category | flops | bytes accessed | tf_op | source)
XLA Modules:
  0.0 308.3 jit_solution(167829260709998432)
XLA Ops:
  7.2 0.0 copy-start
  7.2 1.9 broadcast_in_dim.21
  9.1 6.4 %all-to-all-start = ((bf16[4,160,512]{2,1,0:T(8,128)(2,1)}), bf16[4,160,512]{2,1,0:T(8,128)(2,1)S(1)}, u32[]{:S(2)}, u32[]{:S(2)}) async-start(bf16[4,160,512]{2,1,0:T(8,128)(2,1)} %broadcast_in_dim.21), calls=%async_computation | async-start | bytes 1310720 | tf_op jit(solution)/shard_map/all_to_all | solution.py:19
  15.5 0.9 reshape_squeeze.6
  16.4 3.7 %convolution_convert_fusion = bf16[2,160,8192]{2,1,0:T(8,128)(2,1)S(1)} fusion(bf16[2,128,8192]{2,1,0:T(8,128)(2,1)} %bitcast.56, bf16[160,2,128]{2,1,0:T(2,128)(2,1)S(1)} %reshape_squeeze.6), kind=kOutput, calls=%fused_computation | convolution fusion | flops 673710080 | bytes 9519104 | tf_op jit(solution)/shard_map/thc,hcd->htd/dot_general | solution.py:34
  20.1 3.0 copy.61
  23.1 0.0 copy-start.3
  23.1 5.5 %all-to-all-done = bf16[4,160,512]{2,1,0:T(8,128)(2,1)S(1)} async-done(((bf16[4,160,512]{2,1,0:T(8,128)(2,1)}), bf16[4,160,512]{2,1,0:T(8,128)(2,1)S(1)}, u32[]{:S(2)}, u32[]{:S(2)}) %all-to-all-start) | async-done | bytes 655392 | tf_op jit(solution)/shard_map/all_to_all | solution.py:19
  28.7 0.5 copy.29
  29.2 2.2 broadcast_in_dim.22
  31.4 7.7 %all-to-all-start.1 = ((bf16[4,4,160,512]{3,1,2,0:T(4,128)(2,1)}), bf16[4,4,160,512]{3,1,2,0:T(4,128)(2,1)S(1)}, u32[]{:S(2)}, u32[]{:S(2)}) async-start(bf16[4,4,160,512]{3,1,2,0:T(4,128)(2,1)} %broadcast_in_dim.22), calls=%async_computation.1 | async-start | bytes 5242880 | tf_op jit(solution)/shard_map/all_to_all | solution.py:19
  39.0 0.0 copy-done.3
  39.0 0.1 and_convert_fusion
  39.2 30.1 %all-to-all-done.1 = bf16[4,4,160,512]{3,1,2,0:T(4,128)(2,1)S(1)} async-done(((bf16[4,4,160,512]{3,1,2,0:T(4,128)(2,1)}), bf16[4,4,160,512]{3,1,2,0:T(4,128)(2,1)S(1)}, u32[]{:S(2)}, u32[]{:S(2)}) %all-to-all-start.1) | async-done | bytes 2621472 | tf_op jit(solution)/shard_map/all_to_all | solution.py:19
  69.3 4.9 %copy.30 = bf16[160,4,4,512]{3,2,1,0:T(4,128)(2,1)} copy(bf16[160,4,4,512]{3,1,0,2:T(4,128)(2,1)S(1)} %bitcast.55) | data formatting | bytes 5242880 | tf_op jit(solution)/shard_map/transpose | solution.py:53
  74.1 4.3 %reshape.130 = bf16[160,8192]{1,0:T(8,128)(2,1)S(1)} reshape(bf16[160,4,4,512]{3,2,1,0:T(4,128)(2,1)} %copy.30) | data formatting | bytes 5242880 | tf_op jit(solution)/shard_map/reshape | solution.py:53
  78.4 0.0 copy-start.2
  78.4 3.8 %fusion.10 = bf16[20,2,8,128]{3,2,1,0:T(8,128)(2,1)S(1)} fusion(bf16[160,8192]{1,0:T(8,128)(2,1)S(1)} %reshape.130, bf16[1,256,8192]{2,1,0:T(8,128)(2,1)} %param.8), kind=kOutput, calls=%fused_computation.11 | convolution fusion | flops 671129600 | bytes 6897664 | tf_op jit(solution)/shard_map/dot_general | solution.py:54
  82.2 0.0 copy-done.2
  82.2 0.2 fusion.9
  82.5 8.3 %all_to_all.30 = f32[4,160,128]{2,1,0:T(8,128)S(1)} all-to-all(f32[4,160,128]{2,1,0:T(8,128)S(1)} %broadcast_in_dim.23), channel_id=1, replica_groups=mesh['zh'=4,'y'=4,'core'=2,'zl'=4,'x'=4] {'x'}, dimensions={0} | all-to-all | bytes 655360 | tf_op jit(solution)/shard_map/all_to_all | solution.py:19
  90.8 7.9 %all_to_all.31 = bf16[4,160,128]{2,1,0:T(8,128)(2,1)S(1)} all-to-all(bf16[4,160,128]{2,1,0:T(8,128)(2,1)S(1)} %broadcast_in_dim.24), channel_id=1, replica_groups=mesh['zh'=4,'y'=4,'core'=2,'zl'=4,'x'=4] {'zl'}, dimensions={0} | all-to-all | bytes 327680 | tf_op jit(solution)/shard_map/all_to_all | solution.py:19
  98.7 0.0 copy-start.1
  98.7 4.7 %all-to-all-start.4 = ((bf16[16,2,160,512]{3,2,1,0:T(8,128)(2,1)}), bf16[16,2,160,512]{3,2,1,0:T(8,128)(2,1)}, u32[]{:S(2)}, u32[]{:S(2)}) async-start(bf16[16,2,160,512]{3,2,1,0:T(8,128)(2,1)} %bitcast.53), calls=%async_computation.4 | async-start | bytes 10485760 | tf_op jit(solution)/shard_map/all_to_all | solution.py:77
  103.5 0.2 all-gather.3.cloned.1.call-start
  103.7 0.0 copy-done
  103.7 0.0 copy-done.1
  103.7 1.0 fusion.35
  104.8 0.0 all-gather.3.cloned.1.call-update
  104.8 128.3 %all-gather.3.cloned.1.call-done = bf16[5120,512]{1,0:T(8,128)(2,1)} async-done(((bf16[160,512]{1,0:T(8,128)(2,1)}), bf16[5120,512]{1,0:T(8,128)(2,1)}) %all-gather.3.cloned.1.call-update) | async-done | bytes 5242896 | tf_op jit(solution)/shard_map/all_gather | solution.py:76
  233.0 7.9 %all-to-all-done.4 = bf16[16,2,160,512]{3,2,1,0:T(8,128)(2,1)} async-done(((bf16[16,2,160,512]{3,2,1,0:T(8,128)(2,1)}), bf16[16,2,160,512]{3,2,1,0:T(8,128)(2,1)}, u32[]{:S(2)}, u32[]{:S(2)}) %all-to-all-start.4) | async-done | bytes 5242912 | tf_op jit(solution)/shard_map/all_to_all | solution.py:77
  241.0 0.0 copy-start.4
  241.0 15.0 %fusion.13 = f32[32,32]{1,0:T(8,128)S(1)} fusion(bf16[32,160,512]{2,1,0:T(8,128)(2,1)} %bitcast.59, bf16[32,160,512]{2,1,0:T(8,128)(2,1)} %bitcast.11), kind=kOutput, calls=%fused_computation.12 | convolution fusion | flops 167772160 | bytes 10489856 | tf_op jit(solution)/shard_map/dot_general | solution.py:80
  256.0 0.8 reshape.136
  256.8 35.1 %all-to-all-start.5 = ((f32[16,1,1024]{2,1,0:T(1,128)}), f32[16,1,1024]{2,1,0:T(1,128)S(1)}, u32[]{:S(2)}, u32[]{:S(2)}) async-start(f32[16,1,1024]{2,1,0:T(1,128)} %reshape.136), calls=%async_computation.5 | async-start | bytes 131072 | tf_op jit(solution)/shard_map/all_to_all | solution.py:19
  291.9 7.2 %all-to-all-done.5 = f32[16,1,1024]{2,1,0:T(1,128)S(1)} async-done(((f32[16,1,1024]{2,1,0:T(1,128)}), f32[16,1,1024]{2,1,0:T(1,128)S(1)}, u32[]{:S(2)}, u32[]{:S(2)}) %all-to-all-start.5) | async-done | bytes 65568 | tf_op jit(solution)/shard_map/all_to_all | solution.py:19
  299.1 0.5 broadcast.112
  299.6 0.8 reduce.1
  300.4 0.1 reshape.137
  300.6 0.0 copy-done.4
  300.6 0.9 convolution_bitcast_fusion
  (8 shorter events, 0.1 us)
Async XLA Ops:
  7.2 96.5 %copy-start = (bf16[1,512,512]{2,1,0:T(8,128)(2,1)S(1)}, bf16[1,512,512]{2,1,0:T(8,128)(2,1)}, u32[]{:S(2)}) copy-start(bf16[1,512,512]{2,1,0:T(8,128)(2,1)} %param.9) | copy-start | bytes 1572868
  9.1 19.6 %all-to-all-start = ((bf16[4,160,512]{2,1,0:T(8,128)(2,1)}), bf16[4,160,512]{2,1,0:T(8,128)(2,1)S(1)}, u32[]{:S(2)}, u32[]{:S(2)}) async-start(bf16[4,160,512]{2,1,0:T(8,128)(2,1)} %broadcast_in_dim.21), calls=%async_computation | async-start | bytes 1310720 | tf_op jit(solution)/shard_map/all_to_all | solution.py:19
  23.1 15.9 %copy-start.3 = (s32[160]{0:T(256)S(1)}, s32[160]{0:T(256)}, u32[]{:S(2)}) copy-start(s32[160]{0:T(256)} %param.12) | copy-start | bytes 1924
  31.4 37.9 %all-to-all-start.1 = ((bf16[4,4,160,512]{3,1,2,0:T(4,128)(2,1)}), bf16[4,4,160,512]{3,1,2,0:T(4,128)(2,1)S(1)}, u32[]{:S(2)}, u32[]{:S(2)}) async-start(bf16[4,4,160,512]{3,1,2,0:T(4,128)(2,1)} %broadcast_in_dim.22), calls=%async_computation.1 | async-start | bytes 5242880 | tf_op jit(solution)/shard_map/all_to_all | solution.py:19
  78.4 3.8 %copy-start.2 = (bf16[1,2,160,160]{3,2,1,0:T(8,128)(2,1)S(1)}, bf16[1,2,160,160]{3,2,1,0:T(8,128)(2,1)}, u32[]{:S(2)}) copy-start(bf16[1,2,160,160]{3,2,1,0:T(8,128)(2,1)} %param.11) | copy-start | bytes 307204
  98.7 5.0 %copy-start.1 = (bf16[1,160,512]{2,1,0:T(8,128)(2,1)S(1)}, bf16[1,160,512]{2,1,0:T(8,128)(2,1)}, u32[]{:S(2)}) copy-start(bf16[1,160,512]{2,1,0:T(8,128)(2,1)} %param.7) | copy-start | bytes 491524
  98.7 142.3 %all-to-all-start.4 = ((bf16[16,2,160,512]{3,2,1,0:T(8,128)(2,1)}), bf16[16,2,160,512]{3,2,1,0:T(8,128)(2,1)}, u32[]{:S(2)}, u32[]{:S(2)}) async-start(bf16[16,2,160,512]{3,2,1,0:T(8,128)(2,1)} %bitcast.53), calls=%async_computation.4 | async-start | bytes 10485760 | tf_op jit(solution)/shard_map/all_to_all | solution.py:77
  103.5 129.6 %all-gather.3.cloned.1.call-start = ((), (), s32[]{:S(2)}) async-start(), calls=%async_computation.6 | async-start | bytes 5406720 | tf_op jit(solution)/shard_map/all_gather | solution.py:76
  241.0 59.6 %copy-start.4 = (s32[1,32]{1,0:T(1,128)S(1)}, s32[1,32]{1,0:T(1,128)}, u32[]{:S(2)}) copy-start(s32[1,32]{1,0:T(1,128)} %param.13) | copy-start | bytes 388
  256.8 42.3 %all-to-all-start.5 = ((f32[16,1,1024]{2,1,0:T(1,128)}), f32[16,1,1024]{2,1,0:T(1,128)S(1)}, u32[]{:S(2)}, u32[]{:S(2)}) async-start(f32[16,1,1024]{2,1,0:T(1,128)} %reshape.136), calls=%async_computation.5 | async-start | bytes 131072 | tf_op jit(solution)/shard_map/all_to_all | solution.py:19
Sparse Core Ops, SparseCore 0:
  107.4 125.5 all-gather.2

commit v14 on v11

--- a/solution.py
+++ b/solution.py
@@ -74,10 +74,11 @@
     )
     residual_grad = (grad_in[0].astype(jnp.float32) + increment).astype(jnp.bfloat16)
     target_row = increment.astype(jnp.bfloat16)
-    mine = lax.all_gather(target_row, PLANE, axis=0, tiled=False)
+    mine_flat = lax.all_gather(target_row, PLANE, axis=0, tiled=True)
+    mine = mine_flat.reshape(-1, tokens, local_width)
     delta = lax.all_to_all(pieces, TP, 0, 0, tiled=True)
     core = lax.axis_index("core")
-    theirs = lax.ppermute(mine, "core", [(0, 1), (1, 0)])
+    theirs = lax.ppermute(mine_flat, "core", [(0, 1), (1, 0)]).reshape(mine.shape)
     all_heads = delta.reshape(HEADS, tokens, local_width)
     contract = (((1, 2), (1, 2)), ((), ()))
     both = jnp.concatenate([mine, theirs], axis=0)

time: 309 us -> 309 us (level)
  local copies, waits for them, and re-layouts: 22.4 us -> 26.8 us
  waiting for transfers between devices: 175 us -> 171 us
    reshape x0 -> x2, local copies, waits for them, and re-layouts: none -> 7.64 us  [the longest x1 4.72 us: on_device(): mine = mine_flat.reshape(-1, tokens, local_width)]
    ppermute x1, waiting for transfers between devices: 4.46 us -> 0.01 us  [on_device(): lax.ppermute(mine_flat, 'core', [(0, 1), (1, 0)]).reshape(mine.shape)]
    all_gather x1 -> x0, local copies, waits for them, and re-layouts: 3.19 us -> none  [on_device(): mine = lax.all_gather(target_row, PLANE, axis=0, tiled=False)]
  transfers between devices with their start and end apart: 6 -> 6, of which waited for: 6 -> 5; matrix products, arithmetic and copies ran while one was open for 4% -> 5% of each run, Pallas kernels for 0% -> 0%
where the time goes in v14:
time: 309 us
  waiting for transfers between devices  171 us (55%)
  starting transfers between devices  59.5 us (19%)
  local copies, waits for them, and re-layouts  26.8 us (9%)
  matrix products  19.8 us (6%)
  blocking collectives  16.2 us (5%)
  between operations  14.2 us (5%)
    all_gather x1, waiting for transfers between devices, on_device(): mine_flat = lax.all_gather(target_row, PLANE, axis=0, tiled=True)  128 us
    all_to_all x3, starting transfers between devices, from_everyone(): lax.all_to_all(jnp.broadcast_to(array[None], (count, *array.shape)), axis...  52.1 us
    all_to_all x3, waiting for transfers between devices, from_everyone(): lax.all_to_all(jnp.broadcast_to(array[None], (count, *array.shape)), axis...  42.9 us
    all_to_all x2, blocking collectives, from_everyone(): lax.all_to_all(jnp.broadcast_to(array[None], (count, *array.shape)), axis...  16.2 us
    dot_general x1, matrix products, on_device(): lax.dot_general(all_heads, both, contract, preferred_element_type=jnp.flo...  10.1 us
  transfers between devices with their start and end apart: 6, of which 5 were waited for; matrix products, arithmetic and copies ran while one was open for 5% of the time, Pallas kernels for 0%

profile of v14, /device:TPU:1, one launch (start us, length us, event | category | flops | bytes accessed | tf_op | source)
XLA Modules:
  0.0 308.6 jit_solution(7410919047480028644)
XLA Ops:
  7.2 0.0 copy-start
  7.2 1.9 broadcast_in_dim.23
  9.1 6.4 %all-to-all-start = ((bf16[4,160,512]{2,1,0:T(8,128)(2,1)}), bf16[4,160,512]{2,1,0:T(8,128)(2,1)S(1)}, u32[]{:S(2)}, u32[]{:S(2)}) async-start(bf16[4,160,512]{2,1,0:T(8,128)(2,1)} %broadcast_in_dim.23), calls=%async_computation | async-start | bytes 1310720 | tf_op jit(solution)/shard_map/all_to_all | solution.py:20
  15.5 0.9 reshape_squeeze.6
  16.4 3.7 %convolution_convert_fusion = bf16[2,160,8192]{2,1,0:T(8,128)(2,1)S(1)} fusion(bf16[2,128,8192]{2,1,0:T(8,128)(2,1)} %bitcast.62, bf16[160,2,128]{2,1,0:T(2,128)(2,1)S(1)} %reshape_squeeze.6), kind=kOutput, calls=%fused_computation | convolution fusion | flops 673710080 | bytes 9519104 | tf_op jit(solution)/shard_map/thc,hcd->htd/dot_general | solution.py:35
  20.1 3.0 copy.71
  23.1 5.5 %all-to-all-done = bf16[4,160,512]{2,1,0:T(8,128)(2,1)S(1)} async-done(((bf16[4,160,512]{2,1,0:T(8,128)(2,1)}), bf16[4,160,512]{2,1,0:T(8,128)(2,1)S(1)}, u32[]{:S(2)}, u32[]{:S(2)}) %all-to-all-start) | async-done | bytes 655392 | tf_op jit(solution)/shard_map/all_to_all | solution.py:20
  28.7 0.5 copy.39
  29.2 0.0 copy-start.3
  29.2 2.2 broadcast_in_dim.24
  31.4 7.7 %all-to-all-start.1 = ((bf16[4,4,160,512]{3,1,2,0:T(4,128)(2,1)}), bf16[4,4,160,512]{3,1,2,0:T(4,128)(2,1)S(1)}, u32[]{:S(2)}, u32[]{:S(2)}) async-start(bf16[4,4,160,512]{3,1,2,0:T(4,128)(2,1)} %broadcast_in_dim.24), calls=%async_computation.1 | async-start | bytes 5242880 | tf_op jit(solution)/shard_map/all_to_all | solution.py:20
  39.0 0.0 copy-done.3
  39.0 0.1 and_convert_fusion
  39.2 30.1 %all-to-all-done.1 = bf16[4,4,160,512]{3,1,2,0:T(4,128)(2,1)S(1)} async-done(((bf16[4,4,160,512]{3,1,2,0:T(4,128)(2,1)}), bf16[4,4,160,512]{3,1,2,0:T(4,128)(2,1)S(1)}, u32[]{:S(2)}, u32[]{:S(2)}) %all-to-all-start.1) | async-done | bytes 2621472 | tf_op jit(solution)/shard_map/all_to_all | solution.py:20
  69.3 4.9 %copy.40 = bf16[160,4,4,512]{3,2,1,0:T(4,128)(2,1)} copy(bf16[160,4,4,512]{3,1,0,2:T(4,128)(2,1)S(1)} %bitcast.61) | data formatting | bytes 5242880 | tf_op jit(solution)/shard_map/transpose | solution.py:54
  74.1 4.3 %reshape.136 = bf16[160,8192]{1,0:T(8,128)(2,1)S(1)} reshape(bf16[160,4,4,512]{3,2,1,0:T(4,128)(2,1)} %copy.40) | data formatting | bytes 5242880 | tf_op jit(solution)/shard_map/reshape | solution.py:54
  78.4 0.0 copy-start.2
  78.4 3.8 %fusion.12 = bf16[20,2,8,128]{3,2,1,0:T(8,128)(2,1)S(1)} fusion(bf16[160,8192]{1,0:T(8,128)(2,1)S(1)} %reshape.136, bf16[1,256,8192]{2,1,0:T(8,128)(2,1)} %param.8), kind=kOutput, calls=%fused_computation.13 | convolution fusion | flops 671129600 | bytes 6897664 | tf_op jit(solution)/shard_map/dot_general | solution.py:55
  82.2 0.0 copy-done.2
  82.2 0.2 fusion.11
  82.5 8.3 %all_to_all.30 = f32[4,160,128]{2,1,0:T(8,128)S(1)} all-to-all(f32[4,160,128]{2,1,0:T(8,128)S(1)} %broadcast_in_dim.25), channel_id=1, replica_groups=mesh['zh'=4,'y'=4,'core'=2,'zl'=4,'x'=4] {'x'}, dimensions={0} | all-to-all | bytes 655360 | tf_op jit(solution)/shard_map/all_to_all | solution.py:20
  90.8 7.9 %all_to_all.31 = bf16[4,160,128]{2,1,0:T(8,128)(2,1)S(1)} all-to-all(bf16[4,160,128]{2,1,0:T(8,128)(2,1)S(1)} %broadcast_in_dim.26), channel_id=1, replica_groups=mesh['zh'=4,'y'=4,'core'=2,'zl'=4,'x'=4] {'zl'}, dimensions={0} | all-to-all | bytes 327680 | tf_op jit(solution)/shard_map/all_to_all | solution.py:20
  98.7 0.0 copy-start.1
  98.7 4.7 %all-to-all-start.4 = ((bf16[16,2,160,512]{3,2,1,0:T(8,128)(2,1)}), bf16[16,2,160,512]{3,2,1,0:T(8,128)(2,1)}, u32[]{:S(2)}, u32[]{:S(2)}) async-start(bf16[16,2,160,512]{3,2,1,0:T(8,128)(2,1)} %bitcast.59), calls=%async_computation.4 | async-start | bytes 10485760 | tf_op jit(solution)/shard_map/all_to_all | solution.py:79
  103.4 0.0 all-gather.2.cloned.1.call-start
  103.5 0.0 copy-done
  103.5 0.0 copy-done.1
  103.5 1.0 fusion.38
  104.6 0.0 all-gather.2.cloned.1.call-update
  104.6 127.7 %all-gather.2.cloned.1.call-done = bf16[2560,512]{1,0:T(8,128)(2,1)} async-done(((bf16[160,512]{1,0:T(8,128)(2,1)}), bf16[2560,512]{1,0:T(8,128)(2,1)}) %all-gather.2.cloned.1.call-update) | async-done | bytes 2621456 | tf_op jit(solution)/shard_map/all_gather | solution.py:77
  232.3 2.7 collective-permute-start
  235.0 4.7 %copy.45 = bf16[16,160,512]{2,0,1:T(8,128)(2,1)} copy(bf16[16,160,512]{2,1,0:T(8,128)(2,1)} %bitcast.63) | data formatting | bytes 5242880 | tf_op jit(solution)/shard_map/reshape | solution.py:78
  239.7 0.0 collective-permute-done
  239.7 2.9 copy.46
  242.6 0.4 all-to-all-done.4
  243.1 0.0 copy-start.4
  243.1 10.1 %fusion.15 = f32[32,32]{0,1:T(8,128)S(1)} fusion(bf16[16,160,512]{2,0,1:T(8,128)(2,1)} %copy.46, bf16[16,160,512]{2,0,1:T(8,128)(2,1)} %copy.45, bf16[32,160,512]{2,1,0:T(8,128)(2,1)} %bitcast.11), kind=kOutput, calls=%fused_computation.15 | convolution fusion | flops 178257920 | bytes 10489856 | tf_op jit(solution)/shard_map/dot_general | solution.py:85
  253.3 0.1 copy.48
  253.4 0.8 reshape.143
  254.2 37.9 %all-to-all-start.5 = ((f32[16,1,1024]{2,1,0:T(1,128)}), f32[16,1,1024]{2,1,0:T(1,128)S(1)}, u32[]{:S(2)}, u32[]{:S(2)}) async-start(f32[16,1,1024]{2,1,0:T(1,128)} %reshape.143), calls=%async_computation.5 | async-start | bytes 131072 | tf_op jit(solution)/shard_map/all_to_all | solution.py:20
  292.2 7.2 %all-to-all-done.5 = f32[16,1,1024]{2,1,0:T(1,128)S(1)} async-done(((f32[16,1,1024]{2,1,0:T(1,128)}), f32[16,1,1024]{2,1,0:T(1,128)S(1)}, u32[]{:S(2)}, u32[]{:S(2)}) %all-to-all-start.5) | async-done | bytes 65568 | tf_op jit(solution)/shard_map/all_to_all | solution.py:20
  299.4 0.5 broadcast.111
  299.9 0.8 reduce.1
  300.7 0.1 reshape.144
  300.8 0.0 copy-done.4
  300.9 0.9 convolution_bitcast_fusion
  (11 shorter events, 0.2 us)
Async XLA Ops:
  7.2 96.3 %copy-start = (bf16[1,512,512]{2,1,0:T(8,128)(2,1)S(1)}, bf16[1,512,512]{2,1,0:T(8,128)(2,1)}, u32[]{:S(2)}) copy-start(bf16[1,512,512]{2,1,0:T(8,128)(2,1)} %param.9) | copy-start | bytes 1572868
  9.1 19.6 %all-to-all-start = ((bf16[4,160,512]{2,1,0:T(8,128)(2,1)}), bf16[4,160,512]{2,1,0:T(8,128)(2,1)S(1)}, u32[]{:S(2)}, u32[]{:S(2)}) async-start(bf16[4,160,512]{2,1,0:T(8,128)(2,1)} %broadcast_in_dim.23), calls=%async_computation | async-start | bytes 1310720 | tf_op jit(solution)/shard_map/all_to_all | solution.py:20
  29.2 9.9 %copy-start.3 = (s32[160]{0:T(256)S(1)}, s32[160]{0:T(256)}, u32[]{:S(2)}) copy-start(s32[160]{0:T(256)} %param.12) | copy-start | bytes 1924
  31.4 37.9 %all-to-all-start.1 = ((bf16[4,4,160,512]{3,1,2,0:T(4,128)(2,1)}), bf16[4,4,160,512]{3,1,2,0:T(4,128)(2,1)S(1)}, u32[]{:S(2)}, u32[]{:S(2)}) async-start(bf16[4,4,160,512]{3,1,2,0:T(4,128)(2,1)} %broadcast_in_dim.24), calls=%async_computation.1 | async-start | bytes 5242880 | tf_op jit(solution)/shard_map/all_to_all | solution.py:20
  78.4 3.8 %copy-start.2 = (bf16[1,2,160,160]{3,2,1,0:T(8,128)(2,1)S(1)}, bf16[1,2,160,160]{3,2,1,0:T(8,128)(2,1)}, u32[]{:S(2)}) copy-start(bf16[1,2,160,160]{3,2,1,0:T(8,128)(2,1)} %param.11) | copy-start | bytes 307204
  98.7 4.8 %copy-start.1 = (bf16[1,160,512]{2,1,0:T(8,128)(2,1)S(1)}, bf16[1,160,512]{2,1,0:T(8,128)(2,1)}, u32[]{:S(2)}) copy-start(bf16[1,160,512]{2,1,0:T(8,128)(2,1)} %param.7) | copy-start | bytes 491524
  98.7 144.4 %all-to-all-start.4 = ((bf16[16,2,160,512]{3,2,1,0:T(8,128)(2,1)}), bf16[16,2,160,512]{3,2,1,0:T(8,128)(2,1)}, u32[]{:S(2)}, u32[]{:S(2)}) async-start(bf16[16,2,160,512]{3,2,1,0:T(8,128)(2,1)} %bitcast.59), calls=%async_computation.4 | async-start | bytes 10485760 | tf_op jit(solution)/shard_map/all_to_all | solution.py:79
  103.4 128.9 %all-gather.2.cloned.1.call-start = ((), (), s32[]{:S(2)}) async-start(), calls=%async_computation.6 | async-start | bytes 2785280 | tf_op jit(solution)/shard_map/all_gather | solution.py:77
  232.3 7.4 %collective-permute-start = (bf16[2560,512]{1,0:T(8,128)(2,1)}, bf16[2560,512]{1,0:T(8,128)(2,1)S(1)}, u32[]{:S(2)}, u32[]{:S(2)}) collective-permute-start(bf16[2560,512]{1,0:T(8,128)(2,1)} %all-gather.2.cloned.1.call-done), channel_id=1, source_target_pairs={{0,16},{16,0},{1,17},{17,1},{2,18},{18,2},{3,19},{19,3},{4,20},{20... | collective-permute-start | bytes 7864328 | tf_op jit(solution)/shard_map/ppermute | solution.py:81
  243.1 57.8 %copy-start.4 = (s32[1,32]{1,0:T(1,128)S(1)}, s32[1,32]{1,0:T(1,128)}, u32[]{:S(2)}) copy-start(s32[1,32]{1,0:T(1,128)} %param.13) | copy-start | bytes 388
  254.2 45.2 %all-to-all-start.5 = ((f32[16,1,1024]{2,1,0:T(1,128)}), f32[16,1,1024]{2,1,0:T(1,128)S(1)}, u32[]{:S(2)}, u32[]{:S(2)}) async-start(f32[16,1,1024]{2,1,0:T(1,128)} %reshape.143), calls=%async_computation.5 | async-start | bytes 131072 | tf_op jit(solution)/shard_map/all_to_all | solution.py:20
Sparse Core Ops, SparseCore 0:
  107.3 124.9 all-gather.1

commit v15 on v11

--- a/solution.py
+++ b/solution.py
@@ -51,12 +51,10 @@
     column = from_everyone(grad_in[0], "zl")
     pieces, column = lax.optimization_barrier((pieces, column))
     row = from_everyone(column, "x")
-    grad_rows = jnp.transpose(row, (2, 1, 0, 3)).reshape(tokens, width)
-    head_grad = lax.dot_general(
-        grad_rows,
-        weights,
-        (((1,), (1,)), ((), ())),
-        preferred_element_type=jnp.float32,
+    zl_count = column.shape[0]
+    by_block = weights.reshape(own_rows, zl_count, tp_count // zl_count, local_width)
+    head_grad = jnp.einsum(
+        "xztc,jzxc->tj", row, by_block, preferred_element_type=jnp.float32
     ).astype(jnp.bfloat16)
     masked = pattern[0] * visible[None]
     value_grad = jnp.einsum(

time: 309 us -> 302 us (0.977)
  waiting for transfers between devices: 175 us -> 168 us
  matrix products: 19 us -> 22.1 us
    all_to_all x3, waiting for transfers between devices: 42.9 us -> 35 us  [from_everyone(): lax.all_to_all(jnp.broadcast_to(array[None], (count, *array.shape)), axis...]
    another operation x0 -> x1, local copies, waits for them, and re-layouts: none -> 7.88 us  [on_device(): weights.reshape(own_rows, zl_count, tp_count // zl_count, local_width)]
    transpose x1 -> x0, local copies, waits for them, and re-layouts: 4.86 us -> none  [on_device(): grad_rows = jnp.transpose(row, (2, 1, 0, 3)).reshape(tokens, width)]
    reshape x1 -> x0, local copies, waits for them, and re-layouts: 4.26 us -> none  [on_device(): grad_rows = jnp.transpose(row, (2, 1, 0, 3)).reshape(tokens, width)]
  transfers between devices with their start and end apart: 6 -> 6, of which waited for: 6 -> 6; matrix products, arithmetic and copies ran while one was open for 4% -> 7% of each run, Pallas kernels for 0% -> 0%
where the time goes in v15:
time: 302 us; the launch traced here: 301 us
  waiting for transfers between devices  168 us (56%)
  starting transfers between devices  59.6 us (20%)
  matrix products  22.1 us (7%)
  local copies, waits for them, and re-layouts  20.2 us (7%)
  blocking collectives  16.2 us (5%)
  between operations  14.2 us (5%)
    all_gather x1, waiting for transfers between devices, on_device(): mine = lax.all_gather(target_row, PLANE, axis=0, tiled=False)  127 us
    all_to_all x3, starting transfers between devices, from_everyone(): lax.all_to_all(jnp.broadcast_to(array[None], (count, *array.shape)), axis...  52.1 us
    all_to_all x3, waiting for transfers between devices, from_everyone(): lax.all_to_all(jnp.broadcast_to(array[None], (count, *array.shape)), axis...  35 us
    all_to_all x2, blocking collectives, from_everyone(): lax.all_to_all(jnp.broadcast_to(array[None], (count, *array.shape)), axis...  16.2 us
    dot_general x1, matrix products, on_device(): lax.dot_general(all_heads, both, contract, preferred_element_type=jnp.flo...  9.4 us
    another operation x1, local copies, waits for them, and re-layouts, on_device(): weights.reshape(own_rows, zl_count, tp_count // zl_count, local_width)  7.88 us
    dot_general x1, matrix products, on_device(): jnp.einsum('xztc,jzxc->tj', row, by_block, preferred_element_type=jnp.flo...  6.84 us
  transfers between devices with their start and end apart: 6, of which 6 were waited for; matrix products, arithmetic and copies ran while one was open for 7% of the time, Pallas kernels for 0%

profile of v15, /device:TPU:1, one launch (start us, length us, event | category | flops | bytes accessed | tf_op | source)
XLA Modules:
  0.0 300.9 jit_solution(3778548399071223707)
XLA Ops:
  7.2 0.0 copy-start
  7.2 1.9 broadcast_in_dim.23
  9.1 6.4 %all-to-all-start = ((bf16[4,160,512]{2,1,0:T(8,128)(2,1)}), bf16[4,160,512]{2,1,0:T(8,128)(2,1)S(1)}, u32[]{:S(2)}, u32[]{:S(2)}) async-start(bf16[4,160,512]{2,1,0:T(8,128)(2,1)} %broadcast_in_dim.23), calls=%async_computation | async-start | bytes 1310720 | tf_op jit(solution)/shard_map/all_to_all | solution.py:20
  15.5 0.9 reshape_squeeze.9
  16.4 3.7 %convolution_convert_fusion = bf16[2,160,8192]{2,1,0:T(8,128)(2,1)S(1)} fusion(bf16[2,128,8192]{2,1,0:T(8,128)(2,1)} %bitcast.60, bf16[160,2,128]{2,1,0:T(2,128)(2,1)S(1)} %reshape_squeeze.9), kind=kOutput, calls=%fused_computation | convolution fusion | flops 673710080 | bytes 9519104 | tf_op jit(solution)/shard_map/thc,hcd->htd/dot_general | solution.py:35
  20.1 3.0 copy.80
  23.1 5.5 %all-to-all-done = bf16[4,160,512]{2,1,0:T(8,128)(2,1)S(1)} async-done(((bf16[4,160,512]{2,1,0:T(8,128)(2,1)}), bf16[4,160,512]{2,1,0:T(8,128)(2,1)S(1)}, u32[]{:S(2)}, u32[]{:S(2)}) %all-to-all-start) | async-done | bytes 655392 | tf_op jit(solution)/shard_map/all_to_all | solution.py:20
  28.7 1.7 broadcast_in_dim.24
  30.4 7.7 %all-to-all-start.1 = ((bf16[4,4,160,512]{3,2,1,0:T(8,128)(2,1)}), bf16[4,4,160,512]{3,2,1,0:T(8,128)(2,1)S(1)}, u32[]{:S(2)}, u32[]{:S(2)}) async-start(bf16[4,4,160,512]{3,2,1,0:T(8,128)(2,1)} %broadcast_in_dim.24), calls=%async_computation.1 | async-start | bytes 5242880 | tf_op jit(solution)/shard_map/all_to_all | solution.py:20
  38.1 0.0 copy-start.3
  38.1 7.9 %reshape_squeeze.11 = bf16[256,4,4,512]{3,2,1,0:T(4,128)(2,1)} reshape(bf16[1,256,8192]{2,1,0:T(8,128)(2,1)} %param.8) | data formatting | bytes 8388608 | tf_op jit(solution)/shard_map/reshape;squeeze | solution.py:55
  45.9 0.0 copy-start.2
  46.0 0.0 copy-done.3
  46.0 0.1 and_convert_fusion
  46.1 22.2 %all-to-all-done.1 = bf16[4,4,160,512]{3,2,1,0:T(8,128)(2,1)S(1)} async-done(((bf16[4,4,160,512]{3,2,1,0:T(8,128)(2,1)}), bf16[4,4,160,512]{3,2,1,0:T(8,128)(2,1)S(1)}, u32[]{:S(2)}, u32[]{:S(2)}) %all-to-all-start.1) | async-done | bytes 2621472 | tf_op jit(solution)/shard_map/all_to_all | solution.py:20
  68.3 6.8 %fusion.15 = bf16[20,2,8,128]{3,2,1,0:T(8,128)(2,1)S(1)} fusion(bf16[4,4,160,512]{3,2,1,0:T(8,128)(2,1)S(1)} %all-to-all-done.1, bf16[256,4,4,512]{3,2,1,0:T(4,128)(2,1)} %reshape_squeeze.11), kind=kOutput, calls=%fused_computation.14 | convolution fusion | flops 671129600 | bytes 6897664 | tf_op jit(solution)/shard_map/xztc,jzxc->tj/dot_general | solution.py:56
  75.2 0.0 copy-done.2
  75.2 0.2 fusion.14
  75.4 8.3 %all_to_all.30 = f32[4,160,128]{2,1,0:T(8,128)S(1)} all-to-all(f32[4,160,128]{2,1,0:T(8,128)S(1)} %broadcast_in_dim.25), channel_id=1, replica_groups=mesh['zh'=4,'y'=4,'core'=2,'zl'=4,'x'=4] {'x'}, dimensions={0} | all-to-all | bytes 655360 | tf_op jit(solution)/shard_map/all_to_all | solution.py:20
  83.7 7.9 %all_to_all.31 = bf16[4,160,128]{2,1,0:T(8,128)(2,1)S(1)} all-to-all(bf16[4,160,128]{2,1,0:T(8,128)(2,1)S(1)} %broadcast_in_dim.26), channel_id=1, replica_groups=mesh['zh'=4,'y'=4,'core'=2,'zl'=4,'x'=4] {'zl'}, dimensions={0} | all-to-all | bytes 327680 | tf_op jit(solution)/shard_map/all_to_all | solution.py:20
  91.7 0.0 copy-start.1
  91.7 4.7 %all-to-all-start.4 = ((bf16[16,2,160,512]{3,2,1,0:T(8,128)(2,1)}), bf16[16,2,160,512]{3,2,1,0:T(8,128)(2,1)}, u32[]{:S(2)}, u32[]{:S(2)}) async-start(bf16[16,2,160,512]{3,2,1,0:T(8,128)(2,1)} %bitcast.58), calls=%async_computation.4 | async-start | bytes 10485760 | tf_op jit(solution)/shard_map/all_to_all | solution.py:76
  96.4 0.0 all-gather.3.cloned.1.call-start
  96.5 0.0 copy-done
  96.5 0.0 copy-done.1
  96.5 1.0 fusion.41
  97.5 0.0 all-gather.3.cloned.1.call-update
  97.5 127.3 %all-gather.3.cloned.1.call-done = bf16[2560,512]{1,0:T(8,128)(2,1)} async-done(((bf16[160,512]{1,0:T(8,128)(2,1)}), bf16[2560,512]{1,0:T(8,128)(2,1)}) %all-gather.3.cloned.1.call-update) | async-done | bytes 2621456 | tf_op jit(solution)/shard_map/all_gather | solution.py:75
  224.9 3.2 %copy.46 = bf16[16,160,512]{2,0,1:T(8,128)(2,1)S(1)} copy(bf16[16,160,512]{2,1,0:T(8,128)(2,1)} %bitcast.61) | data formatting | bytes 5242880 | tf_op jit(solution)/shard_map/all_gather | solution.py:75
  228.1 2.6 collective-permute-start
  230.7 4.5 %collective-permute-done = bf16[16,160,512]{2,0,1:T(8,128)(2,1)} collective-permute-done((bf16[16,160,512]{2,0,1:T(8,128)(2,1)S(1)}, bf16[16,160,512]{2,0,1:T(8,128)(2,1)}, u32[]{:S(2)}, u32[]{:S(2)}) %collective-permute-start) | collective-permute-done | bytes 2621472 | tf_op jit(solution)/shard_map/ppermute | solution.py:78
  235.2 0.8 all-to-all-done.4
  236.0 0.0 copy-start.4
  236.0 9.4 %fusion.18 = f32[32,32]{0,1:T(8,128)S(1)} fusion(bf16[16,160,512]{2,0,1:T(8,128)(2,1)} %collective-permute-done, bf16[16,160,512]{2,0,1:T(8,128)(2,1)S(1)} %copy.46, bf16[32,160,512]{2,1,0:T(8,128)(2,1)} %bitcast.11), kind=kOutput, calls=%fused_computation.16 | convolution fusion | flops 178257920 | bytes 10489856 | tf_op jit(solution)/shard_map/dot_general | solution.py:82
  245.5 0.1 copy.48
  245.6 0.8 reshape.133
  246.4 38.0 %all-to-all-start.5 = ((f32[16,1,1024]{2,1,0:T(1,128)}), f32[16,1,1024]{2,1,0:T(1,128)S(1)}, u32[]{:S(2)}, u32[]{:S(2)}) async-start(f32[16,1,1024]{2,1,0:T(1,128)} %reshape.133), calls=%async_computation.5 | async-start | bytes 131072 | tf_op jit(solution)/shard_map/all_to_all | solution.py:20
  284.4 7.2 %all-to-all-done.5 = f32[16,1,1024]{2,1,0:T(1,128)S(1)} async-done(((f32[16,1,1024]{2,1,0:T(1,128)}), f32[16,1,1024]{2,1,0:T(1,128)S(1)}, u32[]{:S(2)}, u32[]{:S(2)}) %all-to-all-start.5) | async-done | bytes 65568 | tf_op jit(solution)/shard_map/all_to_all | solution.py:20
  291.7 0.5 broadcast.111
  292.2 0.8 reduce.1
  293.0 0.1 reshape.134
  293.2 0.0 copy-done.4
  293.2 0.9 convolution_bitcast_fusion
  (11 shorter events, 0.2 us)
Async XLA Ops:
  7.2 89.3 %copy-start = (bf16[1,512,512]{2,1,0:T(8,128)(2,1)S(1)}, bf16[1,512,512]{2,1,0:T(8,128)(2,1)}, u32[]{:S(2)}) copy-start(bf16[1,512,512]{2,1,0:T(8,128)(2,1)} %param.9) | copy-start | bytes 1572868
  9.1 19.6 %all-to-all-start = ((bf16[4,160,512]{2,1,0:T(8,128)(2,1)}), bf16[4,160,512]{2,1,0:T(8,128)(2,1)S(1)}, u32[]{:S(2)}, u32[]{:S(2)}) async-start(bf16[4,160,512]{2,1,0:T(8,128)(2,1)} %broadcast_in_dim.23), calls=%async_computation | async-start | bytes 1310720 | tf_op jit(solution)/shard_map/all_to_all | solution.py:20
  30.4 37.9 %all-to-all-start.1 = ((bf16[4,4,160,512]{3,2,1,0:T(8,128)(2,1)}), bf16[4,4,160,512]{3,2,1,0:T(8,128)(2,1)S(1)}, u32[]{:S(2)}, u32[]{:S(2)}) async-start(bf16[4,4,160,512]{3,2,1,0:T(8,128)(2,1)} %broadcast_in_dim.24), calls=%async_computation.1 | async-start | bytes 5242880 | tf_op jit(solution)/shard_map/all_to_all | solution.py:20
  38.1 7.9 %copy-start.3 = (s32[160]{0:T(256)S(1)}, s32[160]{0:T(256)}, u32[]{:S(2)}) copy-start(s32[160]{0:T(256)} %param.12) | copy-start | bytes 1924
  45.9 29.2 %copy-start.2 = (bf16[1,2,160,160]{3,2,1,0:T(8,128)(2,1)S(1)}, bf16[1,2,160,160]{3,2,1,0:T(8,128)(2,1)}, u32[]{:S(2)}) copy-start(bf16[1,2,160,160]{3,2,1,0:T(8,128)(2,1)} %param.11) | copy-start | bytes 307204
  91.7 4.8 %copy-start.1 = (bf16[1,160,512]{2,1,0:T(8,128)(2,1)S(1)}, bf16[1,160,512]{2,1,0:T(8,128)(2,1)}, u32[]{:S(2)}) copy-start(bf16[1,160,512]{2,1,0:T(8,128)(2,1)} %param.7) | copy-start | bytes 491524
  91.7 144.4 %all-to-all-start.4 = ((bf16[16,2,160,512]{3,2,1,0:T(8,128)(2,1)}), bf16[16,2,160,512]{3,2,1,0:T(8,128)(2,1)}, u32[]{:S(2)}, u32[]{:S(2)}) async-start(bf16[16,2,160,512]{3,2,1,0:T(8,128)(2,1)} %bitcast.58), calls=%async_computation.4 | async-start | bytes 10485760 | tf_op jit(solution)/shard_map/all_to_all | solution.py:76
  96.4 128.5 %all-gather.3.cloned.1.call-start = ((), (), s32[]{:S(2)}) async-start(), calls=%async_computation.6 | async-start | bytes 2785280 | tf_op jit(solution)/shard_map/all_gather | solution.py:75
  228.1 7.1 %collective-permute-start = (bf16[16,160,512]{2,0,1:T(8,128)(2,1)S(1)}, bf16[16,160,512]{2,0,1:T(8,128)(2,1)}, u32[]{:S(2)}, u32[]{:S(2)}) collective-permute-start(bf16[16,160,512]{2,0,1:T(8,128)(2,1)S(1)} %copy.46), channel_id=1, source_target_pairs={{0,16},{16,0},{1,17},{17,1},{2,18},{18,2},{3,19},{19,3},{4,20},{20... | collective-permute-start | bytes 7864328 | tf_op jit(solution)/shard_map/ppermute | solution.py:78
  236.0 57.1 %copy-start.4 = (s32[1,32]{1,0:T(1,128)S(1)}, s32[1,32]{1,0:T(1,128)}, u32[]{:S(2)}) copy-start(s32[1,32]{1,0:T(1,128)} %param.13) | copy-start | bytes 388
  246.4 45.3 %all-to-all-start.5 = ((f32[16,1,1024]{2,1,0:T(1,128)}), f32[16,1,1024]{2,1,0:T(1,128)S(1)}, u32[]{:S(2)}, u32[]{:S(2)}) async-start(f32[16,1,1024]{2,1,0:T(1,128)} %reshape.133), calls=%async_computation.5 | async-start | bytes 131072 | tf_op jit(solution)/shard_map/all_to_all | solution.py:20
Sparse Core Ops, SparseCore 0:
  100.3 124.5 all-gather.2
